TPU v7x, 32 devices: a whole 2x2x4 slice. The times are simulated.
32 devices in a mesh: area: 4 (over x, core), sub: 8 (over z, y).
Axes of the slice: x: 2, y: 2, z: 4, core: 2. Of those that a mesh axis runs over, the one named last changes fastest.
Arguments:
- blocks: float32 [4, 512, 64, 256], P('area', 'sub'), as said below
- pattern: int32 [4, 512, 4], P('area', 'sub'), may hold values from 0 to 511, as said below
- line_ends: int32 [4, 2, 64], P('area'), may hold values from 0 to 32767, as said below
- sources: float32 [4, 4, 32768], P(None, 'area', 'sub'), may hold values from -6 to 6
- capacity: float32 [4, 32768], P('area', 'sub'), may hold values from 0.2 to 2
- start_volt: float32 [4, 32768], P('area', 'sub'), may hold values from -6 to 6
- start_hist: float32 [4, 2, 64], P('area'), may hold values from -6 to 6
- surge: float32 [4, 64], P('area'), may hold values from 0.2 to 1
Outputs:
- volt: float32 [4, 32768], P('area', 'sub')
- hist: float32 [4, 2, 64], P('area')
Inputs may be any that keep to these rules, and one draw needn't show every extreme that they name: pattern[a, r, 0] = r. Split the 512 block rows of an area into aligned groups of 64: the other entries of a row never point into the row's own group, no two of them in one group are equal, and the entries of one group point into between 27 and 28 distinct block rows of each other group, exactly 28 for some group. `line_ends`: within an area the line-end buses are distinct and rise from the first left end to the last right end. `blocks`: the diagonal of each first stored block lies in 2 to 4.
All inputs are finite; a program needn't handle non-finite values.
Results may differ from a plain program's by a relative error of at most 0.00011.
Values sent between devices are 32-bit elements; how exact they have to be, the bound alone decides.
No kernel may reach another device: no remote copies, remote signals or barrier semaphores. Data moves between devices by JAX's collectives and lax.ppermute only.
A program may use at most 64 MiB of HBM per device.

v0:
```python
import jax
import jax.numpy as jnp
from jax import lax
from jax.sharding import PartitionSpec as P

STEPS = 4
SWEEPS = 8


def shifted(value, axis, steps):
    count = lax.axis_size(axis)
    pairs = [(source, (source + steps) % count) for source in range(count)]
    return lax.ppermute(value, axis, pairs)


def collect(value):
    count = lax.axis_size("sub")
    half = count // 2
    partner = lax.ppermute(value, "sub", [(i, i ^ 1) for i in range(count)])
    pair = jnp.stack([value, partner])
    parts = [pair]
    for k in range(1, half):
        moves = [(i, ((i // 2 + k) % half) * 2 + i % 2) for i in range(count)]
        parts.append(lax.ppermute(pair, "sub", moves))
    return jnp.stack(parts).reshape((count,) + value.shape)


def slot_of(index, me, count, chunk):
    owner = index // chunk
    slot = ((me // 2 - owner // 2) % (count // 2)) * 2 + ((owner % 2) ^ (me % 2))
    return slot * chunk + index % chunk


def apply_blocks(blocks, own_part, others):
    picked = jnp.concatenate([own_part, others], axis=1)
    result = jnp.sum(blocks[0] * picked[:, None, :], axis=2)
    return result.reshape(1, -1)


def next_hist(end_volt, hist, surge):
    message = -2.0 * surge * end_volt[:, 1] - hist[:, 1]
    new_left = shifted(message, "area", 1)
    outgoing_ends = jnp.stack([end_volt[:, 0], hist[:, 0]], axis=1)
    from_right = shifted(outgoing_ends, "area", -1)
    new_right = -2.0 * surge * from_right[:, 0] - from_right[:, 1]
    return jnp.stack([new_left, new_right], axis=1)


def on_device(blocks, pattern, line_ends, sources, capacity, start_volt, start_hist, surge):
    width = blocks.shape[2]
    rows_here = blocks.shape[1]
    local_count = rows_here * width
    offset = lax.axis_index("sub") * local_count
    diag = jnp.diagonal(blocks[..., :width], axis1=2, axis2=3).reshape(1, local_count)
    system_diag = diag + capacity
    count = lax.axis_size("sub")
    me = lax.axis_index("sub")
    remote_cols = slot_of(pattern[0][:, 1:].reshape(-1), me, count, rows_here)
    end_index = slot_of(line_ends[0], me, count, local_count)
    local_ends = line_ends - offset
    inside = (local_ends >= 0) & (local_ends < local_count)
    safe_ends = jnp.clip(local_ends, 0, local_count - 1)
    volt = start_volt
    hist = start_hist
    for step in range(STEPS):
        field = volt
        rhs = None
        for sweep in range(SWEEPS):
            whole = collect(field)
            if rhs is None:
                if step > 0:
                    end_volt = whole.reshape(-1)[end_index][None]
                    hist = next_hist(end_volt, hist, surge)
                rhs = sources[step] + capacity * volt
                inject = jnp.where(inside, -hist, 0.0)
                rhs = rhs.at[0, safe_ends.reshape(-1)].add(inject.reshape(-1))
            own_part = field.reshape(rows_here, width)
            others = whole.reshape(-1, width)[remote_cols]
            others = others.reshape(rows_here, -1)
            result = apply_blocks(blocks, own_part, others)
            field = field + (rhs - result - capacity * field) / system_diag
        volt = field
    partial_volt = jnp.where(inside, volt[0][safe_ends[0]][None], 0.0)
    end_volt = jnp.sum(collect(partial_volt), axis=0)
    hist = next_hist(end_volt, hist, surge)
    return (volt, hist)


def solution(mesh):
    in_specs = (
        P("area", "sub", None, None),
        P("area", "sub", None),
        P("area", None, None),
        P(None, "area", "sub"),
        P("area", "sub"),
        P("area", "sub"),
        P("area", None, None),
        P("area", None),
    )
    out_specs = (P("area", "sub"), P("area", None, None))
    return jax.shard_map(
        on_device, mesh=mesh, in_specs=in_specs, out_specs=out_specs, check_vma=False
    )
```

profile of v0, /device:TPU:0, one launch (start us, length us, event | category | flops | bytes accessed | tf_op | source)
XLA Modules:
  0.0 550.2 jit_solution(9960173269646349710)
XLA Ops:
  0.6 3.1 collective-permute-start
  21.2 2.8 fusion
  25.5 3.2 collective-permute-done.4
  29.8 2.8 collective-permute-start.7
  36.2 2.8 fusion.1
  40.5 3.2 collective-permute-done.8
  52.6 2.8 fusion.2
  56.8 3.2 collective-permute-done.12
  68.2 2.8 fusion.3
  72.4 3.2 collective-permute-done.16
  84.6 2.8 fusion.4
  88.9 3.2 collective-permute-done.20
  100.1 2.8 fusion.5
  104.3 3.2 collective-permute-done.24
  116.2 2.8 fusion.6
  120.4 3.2 collective-permute-done.28
  131.9 2.8 fusion.7
  136.3 3.1 collective-permute-done.32
  152.0 2.8 fusion.8
  157.8 3.2 collective-permute-done.38
  169.3 2.8 fusion.9
  173.6 3.2 collective-permute-done.42
  185.2 2.8 fusion.10
  189.5 3.1 collective-permute-done.46
  201.0 2.8 fusion.11
  205.4 3.1 collective-permute-done.50
  217.4 2.8 fusion.12
  221.6 3.2 collective-permute-done.54
  234.1 2.8 fusion.13
  238.3 3.2 collective-permute-done.58
  249.6 2.8 fusion.14
  253.8 3.2 collective-permute-done.62
  265.7 2.8 fusion.15
  270.0 3.2 collective-permute-done.66
  290.3 3.2 collective-permute-done.72
  302.2 2.8 fusion.17
  306.5 3.2 collective-permute-done.76
  317.9 2.8 fusion.18
  322.2 3.2 collective-permute-done.80
  333.9 2.8 fusion.19
  338.2 3.2 collective-permute-done.84
  349.6 2.8 fusion.20
  353.9 3.2 collective-permute-done.88
  366.5 2.8 fusion.21
  370.7 3.2 collective-permute-done.92
  382.0 2.8 fusion.22
  386.3 3.2 collective-permute-done.96
  398.1 2.8 fusion.23
  402.3 3.2 collective-permute-done.100
  423.9 3.2 collective-permute-done.106
  435.6 2.8 fusion.25
  439.8 3.2 collective-permute-done.110
  451.0 2.8 fusion.26
  455.3 3.2 collective-permute-done.114
  466.9 2.8 fusion.27
  471.2 3.2 collective-permute-done.118
  482.5 2.8 fusion.28
  486.7 3.2 collective-permute-done.122
  499.1 2.8 fusion.29
  503.4 3.2 collective-permute-done.126
  514.5 2.8 fusion.30
  518.9 3.1 collective-permute-done.130
  530.5 2.8 fusion.31
  535.3 3.0 collective-permute-done.134
  (623 shorter events, 356.7 us)
Async XLA Ops:
  0.6 7.5 %collective-permute-start = (f32[1,4096]{1,0:T(1,128)}, f32[1,4096]{1,0:T(1,128)S(1)}, u32[]{:S(2)}, u32[]{:S(2)}) collective-permute-start(f32[1,4096]{1,0:T(1,128)} %param.13), channel_id=1, source_target_pairs={{0,1},{1,0},{2,3},{3,2},{4,5},{5,4},{6,7},{7,6},{8,9},{9,8},{10,11... | collective-permute-start | bytes 49160 | tf_op jit(solution)/shard_map/ppermute | solution.py:19
  9.0 11.1 %collective-permute-start.1 = (f32[2,1,4096]{2,0,1:T(2,128)S(1)}, f32[2,1,4096]{2,0,1:T(2,128)S(1)}, u32[]{:S(2)}, u32[]{:S(2)}) collective-permute-start(f32[2,1,4096]{2,0,1:T(2,128)S(1)} %get-tuple-element.140), channel_id=1, source_target_pairs={{0,2},{1,3},{2,4},{3,5},{4,6},{5,7},{6,0},{7,1},{8,10},{9,11},{10,... | collective-permute-start | bytes 98312 | tf_op jit(solution)/shard_map/ppermute | solution.py:24
  10.6 9.5 %collective-permute-start.2 = (f32[2,1,4096]{2,0,1:T(2,128)S(1)}, f32[2,1,4096]{2,0,1:T(2,128)S(1)}, u32[]{:S(2)}, u32[]{:S(2)}) collective-permute-start(f32[2,1,4096]{2,0,1:T(2,128)S(1)} %get-tuple-element.140), channel_id=1, source_target_pairs={{0,4},{1,5},{2,6},{3,7},{4,0},{5,1},{6,2},{7,3},{8,12},{9,13},{10,... | collective-permute-start | bytes 98312 | tf_op jit(solution)/shard_map/ppermute | solution.py:24
  13.2 6.9 %collective-permute-start.3 = (f32[2,1,4096]{2,0,1:T(2,128)S(1)}, f32[2,1,4096]{2,0,1:T(2,128)S(1)}, u32[]{:S(2)}, u32[]{:S(2)}) collective-permute-start(f32[2,1,4096]{2,0,1:T(2,128)S(1)} %get-tuple-element.140), channel_id=1, source_target_pairs={{0,6},{1,7},{2,0},{3,1},{4,2},{5,3},{6,4},{7,5},{8,14},{9,15},{10,... | collective-permute-start | bytes 98312 | tf_op jit(solution)/shard_map/ppermute | solution.py:24
  28.7 5.9 %collective-permute-start.5 = (f32[2,1,4096]{2,0,1:T(2,128)S(1)}, f32[2,1,4096]{2,0,1:T(2,128)S(1)}, u32[]{:S(2)}, u32[]{:S(2)}) collective-permute-start(f32[2,1,4096]{2,0,1:T(2,128)S(1)} %get-tuple-element.138), channel_id=1, source_target_pairs={{0,2},{1,3},{2,4},{3,5},{4,6},{5,7},{6,0},{7,1},{8,10},{9,11},{10,... | collective-permute-start | bytes 98312 | tf_op jit(solution)/shard_map/ppermute | solution.py:24
  29.5 5.6 %collective-permute-start.6 = (f32[2,1,4096]{2,0,1:T(2,128)S(1)}, f32[2,1,4096]{2,0,1:T(2,128)S(1)}, u32[]{:S(2)}, u32[]{:S(2)}) collective-permute-start(f32[2,1,4096]{2,0,1:T(2,128)S(1)} %get-tuple-element.138), channel_id=1, source_target_pairs={{0,4},{1,5},{2,6},{3,7},{4,0},{5,1},{6,2},{7,3},{8,12},{9,13},{10,... | collective-permute-start | bytes 98312 | tf_op jit(solution)/shard_map/ppermute | solution.py:24
  29.8 5.3 collective-permute-start.7
  43.7 5.8 %collective-permute-start.9 = (f32[2,1,4096]{2,0,1:T(2,128)S(1)}, f32[2,1,4096]{2,0,1:T(2,128)S(1)}, u32[]{:S(2)}, u32[]{:S(2)}) collective-permute-start(f32[2,1,4096]{2,0,1:T(2,128)S(1)} %get-tuple-element.136), channel_id=1, source_target_pairs={{0,2},{1,3},{2,4},{3,5},{4,6},{5,7},{6,0},{7,1},{8,10},{9,11},{10,... | collective-permute-start | bytes 98312 | tf_op jit(solution)/shard_map/ppermute | solution.py:24
  60.1 5.8 %collective-permute-start.13 = (f32[2,1,4096]{2,0,1:T(2,128)S(1)}, f32[2,1,4096]{2,0,1:T(2,128)S(1)}, u32[]{:S(2)}, u32[]{:S(2)}) collective-permute-start(f32[2,1,4096]{2,0,1:T(2,128)S(1)} %get-tuple-element.134), channel_id=1, source_target_pairs={{0,2},{1,3},{2,4},{3,5},{4,6},{5,7},{6,0},{7,1},{8,10},{9,11},{10,... | collective-permute-start | bytes 98312 | tf_op jit(solution)/shard_map/ppermute | solution.py:24
  60.7 5.2 collective-permute-start.14
  75.6 5.8 %collective-permute-start.17 = (f32[2,1,4096]{2,0,1:T(2,128)S(1)}, f32[2,1,4096]{2,0,1:T(2,128)S(1)}, u32[]{:S(2)}, u32[]{:S(2)}) collective-permute-start(f32[2,1,4096]{2,0,1:T(2,128)S(1)} %get-tuple-element.132), channel_id=1, source_target_pairs={{0,2},{1,3},{2,4},{3,5},{4,6},{5,7},{6,0},{7,1},{8,10},{9,11},{10,... | collective-permute-start | bytes 98312 | tf_op jit(solution)/shard_map/ppermute | solution.py:24
  77.1 5.0 collective-permute-start.18
  92.1 5.8 %collective-permute-start.21 = (f32[2,1,4096]{2,0,1:T(2,128)S(1)}, f32[2,1,4096]{2,0,1:T(2,128)S(1)}, u32[]{:S(2)}, u32[]{:S(2)}) collective-permute-start(f32[2,1,4096]{2,0,1:T(2,128)S(1)} %get-tuple-element.130), channel_id=1, source_target_pairs={{0,2},{1,3},{2,4},{3,5},{4,6},{5,7},{6,0},{7,1},{8,10},{9,11},{10,... | collective-permute-start | bytes 98312 | tf_op jit(solution)/shard_map/ppermute | solution.py:24
  93.3 5.6 %collective-permute-start.22 = (f32[2,1,4096]{2,0,1:T(2,128)S(1)}, f32[2,1,4096]{2,0,1:T(2,128)S(1)}, u32[]{:S(2)}, u32[]{:S(2)}) collective-permute-start(f32[2,1,4096]{2,0,1:T(2,128)S(1)} %get-tuple-element.130), channel_id=1, source_target_pairs={{0,4},{1,5},{2,6},{3,7},{4,0},{5,1},{6,2},{7,3},{8,12},{9,13},{10,... | collective-permute-start | bytes 98312 | tf_op jit(solution)/shard_map/ppermute | solution.py:24
  107.5 6.0 %collective-permute-start.25 = (f32[2,1,4096]{2,0,1:T(2,128)S(1)}, f32[2,1,4096]{2,0,1:T(2,128)S(1)}, u32[]{:S(2)}, u32[]{:S(2)}) collective-permute-start(f32[2,1,4096]{2,0,1:T(2,128)S(1)} %get-tuple-element.128), channel_id=1, source_target_pairs={{0,2},{1,3},{2,4},{3,5},{4,6},{5,7},{6,0},{7,1},{8,10},{9,11},{10,... | collective-permute-start | bytes 98312 | tf_op jit(solution)/shard_map/ppermute | solution.py:24
  109.3 4.9 collective-permute-start.26
  123.7 5.8 %collective-permute-start.29 = (f32[2,1,4096]{2,0,1:T(2,128)S(1)}, f32[2,1,4096]{2,0,1:T(2,128)S(1)}, u32[]{:S(2)}, u32[]{:S(2)}) collective-permute-start(f32[2,1,4096]{2,0,1:T(2,128)S(1)} %get-tuple-element.126), channel_id=1, source_target_pairs={{0,2},{1,3},{2,4},{3,5},{4,6},{5,7},{6,0},{7,1},{8,10},{9,11},{10,... | collective-permute-start | bytes 98312 | tf_op jit(solution)/shard_map/ppermute | solution.py:24
  124.8 5.4 collective-permute-start.30
  139.4 5.8 %collective-permute-start.33 = (f32[2,1,4096]{2,0,1:T(2,128)S(1)}, f32[2,1,4096]{2,0,1:T(2,128)S(1)}, u32[]{:S(2)}, u32[]{:S(2)}) collective-permute-start(f32[2,1,4096]{2,0,1:T(2,128)S(1)} %get-tuple-element.124), channel_id=1, source_target_pairs={{0,2},{1,3},{2,4},{3,5},{4,6},{5,7},{6,0},{7,1},{8,10},{9,11},{10,... | collective-permute-start | bytes 98312 | tf_op jit(solution)/shard_map/ppermute | solution.py:24
  140.7 5.2 collective-permute-start.34
  161.0 5.8 %collective-permute-start.39 = (f32[2,1,4096]{2,0,1:T(2,128)S(1)}, f32[2,1,4096]{2,0,1:T(2,128)S(1)}, u32[]{:S(2)}, u32[]{:S(2)}) collective-permute-start(f32[2,1,4096]{2,0,1:T(2,128)S(1)} %get-tuple-element.122), channel_id=1, source_target_pairs={{0,2},{1,3},{2,4},{3,5},{4,6},{5,7},{6,0},{7,1},{8,10},{9,11},{10,... | collective-permute-start | bytes 98312 | tf_op jit(solution)/shard_map/ppermute | solution.py:24
  162.2 5.3 collective-permute-start.40
  176.8 5.8 %collective-permute-start.43 = (f32[2,1,4096]{2,0,1:T(2,128)S(1)}, f32[2,1,4096]{2,0,1:T(2,128)S(1)}, u32[]{:S(2)}, u32[]{:S(2)}) collective-permute-start(f32[2,1,4096]{2,0,1:T(2,128)S(1)} %get-tuple-element.120), channel_id=1, source_target_pairs={{0,2},{1,3},{2,4},{3,5},{4,6},{5,7},{6,0},{7,1},{8,10},{9,11},{10,... | collective-permute-start | bytes 98312 | tf_op jit(solution)/shard_map/ppermute | solution.py:24
  178.2 5.1 collective-permute-start.44
  192.7 5.8 %collective-permute-start.47 = (f32[2,1,4096]{2,0,1:T(2,128)S(1)}, f32[2,1,4096]{2,0,1:T(2,128)S(1)}, u32[]{:S(2)}, u32[]{:S(2)}) collective-permute-start(f32[2,1,4096]{2,0,1:T(2,128)S(1)} %get-tuple-element.118), channel_id=1, source_target_pairs={{0,2},{1,3},{2,4},{3,5},{4,6},{5,7},{6,0},{7,1},{8,10},{9,11},{10,... | collective-permute-start | bytes 98312 | tf_op jit(solution)/shard_map/ppermute | solution.py:24
  193.9 5.2 collective-permute-start.48
  208.5 5.8 %collective-permute-start.51 = (f32[2,1,4096]{2,0,1:T(2,128)S(1)}, f32[2,1,4096]{2,0,1:T(2,128)S(1)}, u32[]{:S(2)}, u32[]{:S(2)}) collective-permute-start(f32[2,1,4096]{2,0,1:T(2,128)S(1)} %get-tuple-element.116), channel_id=1, source_target_pairs={{0,2},{1,3},{2,4},{3,5},{4,6},{5,7},{6,0},{7,1},{8,10},{9,11},{10,... | collective-permute-start | bytes 98312 | tf_op jit(solution)/shard_map/ppermute | solution.py:24
  209.8 5.2 collective-permute-start.52
  224.8 5.8 %collective-permute-start.55 = (f32[2,1,4096]{2,0,1:T(2,128)S(1)}, f32[2,1,4096]{2,0,1:T(2,128)S(1)}, u32[]{:S(2)}, u32[]{:S(2)}) collective-permute-start(f32[2,1,4096]{2,0,1:T(2,128)S(1)} %get-tuple-element.114), channel_id=1, source_target_pairs={{0,2},{1,3},{2,4},{3,5},{4,6},{5,7},{6,0},{7,1},{8,10},{9,11},{10,... | collective-permute-start | bytes 98312 | tf_op jit(solution)/shard_map/ppermute | solution.py:24
  226.0 6.4 %collective-permute-start.56 = (f32[2,1,4096]{2,0,1:T(2,128)S(1)}, f32[2,1,4096]{2,0,1:T(2,128)S(1)}, u32[]{:S(2)}, u32[]{:S(2)}) collective-permute-start(f32[2,1,4096]{2,0,1:T(2,128)S(1)} %get-tuple-element.114), channel_id=1, source_target_pairs={{0,4},{1,5},{2,6},{3,7},{4,0},{5,1},{6,2},{7,3},{8,12},{9,13},{10,... | collective-permute-start | bytes 98312 | tf_op jit(solution)/shard_map/ppermute | solution.py:24
  241.6 5.9 %collective-permute-start.59 = (f32[2,1,4096]{2,0,1:T(2,128)S(1)}, f32[2,1,4096]{2,0,1:T(2,128)S(1)}, u32[]{:S(2)}, u32[]{:S(2)}) collective-permute-start(f32[2,1,4096]{2,0,1:T(2,128)S(1)} %get-tuple-element.112), channel_id=1, source_target_pairs={{0,2},{1,3},{2,4},{3,5},{4,6},{5,7},{6,0},{7,1},{8,10},{9,11},{10,... | collective-permute-start | bytes 98312 | tf_op jit(solution)/shard_map/ppermute | solution.py:24
  242.4 5.5 %collective-permute-start.60 = (f32[2,1,4096]{2,0,1:T(2,128)S(1)}, f32[2,1,4096]{2,0,1:T(2,128)S(1)}, u32[]{:S(2)}, u32[]{:S(2)}) collective-permute-start(f32[2,1,4096]{2,0,1:T(2,128)S(1)} %get-tuple-element.112), channel_id=1, source_target_pairs={{0,4},{1,5},{2,6},{3,7},{4,0},{5,1},{6,2},{7,3},{8,12},{9,13},{10,... | collective-permute-start | bytes 98312 | tf_op jit(solution)/shard_map/ppermute | solution.py:24
  257.1 5.8 %collective-permute-start.63 = (f32[2,1,4096]{2,0,1:T(2,128)S(1)}, f32[2,1,4096]{2,0,1:T(2,128)S(1)}, u32[]{:S(2)}, u32[]{:S(2)}) collective-permute-start(f32[2,1,4096]{2,0,1:T(2,128)S(1)} %get-tuple-element.110), channel_id=1, source_target_pairs={{0,2},{1,3},{2,4},{3,5},{4,6},{5,7},{6,0},{7,1},{8,10},{9,11},{10,... | collective-permute-start | bytes 98312 | tf_op jit(solution)/shard_map/ppermute | solution.py:24
  273.2 5.8 %collective-permute-start.67 = (f32[2,1,4096]{2,0,1:T(2,128)S(1)}, f32[2,1,4096]{2,0,1:T(2,128)S(1)}, u32[]{:S(2)}, u32[]{:S(2)}) collective-permute-start(f32[2,1,4096]{2,0,1:T(2,128)S(1)} %get-tuple-element.108), channel_id=1, source_target_pairs={{0,2},{1,3},{2,4},{3,5},{4,6},{5,7},{6,0},{7,1},{8,10},{9,11},{10,... | collective-permute-start | bytes 98312 | tf_op jit(solution)/shard_map/ppermute | solution.py:24
  274.2 5.4 collective-permute-start.68
  293.5 5.8 %collective-permute-start.73 = (f32[2,1,4096]{2,0,1:T(2,128)S(1)}, f32[2,1,4096]{2,0,1:T(2,128)S(1)}, u32[]{:S(2)}, u32[]{:S(2)}) collective-permute-start(f32[2,1,4096]{2,0,1:T(2,128)S(1)} %get-tuple-element.106), channel_id=1, source_target_pairs={{0,2},{1,3},{2,4},{3,5},{4,6},{5,7},{6,0},{7,1},{8,10},{9,11},{10,... | collective-permute-start | bytes 98312 | tf_op jit(solution)/shard_map/ppermute | solution.py:24
  295.0 5.0 collective-permute-start.74
  309.7 5.8 %collective-permute-start.77 = (f32[2,1,4096]{2,0,1:T(2,128)S(1)}, f32[2,1,4096]{2,0,1:T(2,128)S(1)}, u32[]{:S(2)}, u32[]{:S(2)}) collective-permute-start(f32[2,1,4096]{2,0,1:T(2,128)S(1)} %get-tuple-element.104), channel_id=1, source_target_pairs={{0,2},{1,3},{2,4},{3,5},{4,6},{5,7},{6,0},{7,1},{8,10},{9,11},{10,... | collective-permute-start | bytes 98312 | tf_op jit(solution)/shard_map/ppermute | solution.py:24
  310.7 5.4 collective-permute-start.78
  325.4 5.8 %collective-permute-start.81 = (f32[2,1,4096]{2,0,1:T(2,128)S(1)}, f32[2,1,4096]{2,0,1:T(2,128)S(1)}, u32[]{:S(2)}, u32[]{:S(2)}) collective-permute-start(f32[2,1,4096]{2,0,1:T(2,128)S(1)} %get-tuple-element.102), channel_id=1, source_target_pairs={{0,2},{1,3},{2,4},{3,5},{4,6},{5,7},{6,0},{7,1},{8,10},{9,11},{10,... | collective-permute-start | bytes 98312 | tf_op jit(solution)/shard_map/ppermute | solution.py:24
  327.0 4.9 collective-permute-start.82
  341.4 5.8 %collective-permute-start.85 = (f32[2,1,4096]{2,0,1:T(2,128)S(1)}, f32[2,1,4096]{2,0,1:T(2,128)S(1)}, u32[]{:S(2)}, u32[]{:S(2)}) collective-permute-start(f32[2,1,4096]{2,0,1:T(2,128)S(1)} %get-tuple-element.100), channel_id=1, source_target_pairs={{0,2},{1,3},{2,4},{3,5},{4,6},{5,7},{6,0},{7,1},{8,10},{9,11},{10,... | collective-permute-start | bytes 98312 | tf_op jit(solution)/shard_map/ppermute | solution.py:24
  342.5 5.3 collective-permute-start.86
  357.1 5.8 %collective-permute-start.89 = (f32[2,1,4096]{2,0,1:T(2,128)S(1)}, f32[2,1,4096]{2,0,1:T(2,128)S(1)}, u32[]{:S(2)}, u32[]{:S(2)}) collective-permute-start(f32[2,1,4096]{2,0,1:T(2,128)S(1)} %get-tuple-element.98), channel_id=1, source_target_pairs={{0,2},{1,3},{2,4},{3,5},{4,6},{5,7},{6,0},{7,1},{8,10},{9,11},{10,... | collective-permute-start | bytes 98312 | tf_op jit(solution)/shard_map/ppermute | solution.py:24
  358.6 6.2 %collective-permute-start.90 = (f32[2,1,4096]{2,0,1:T(2,128)S(1)}, f32[2,1,4096]{2,0,1:T(2,128)S(1)}, u32[]{:S(2)}, u32[]{:S(2)}) collective-permute-start(f32[2,1,4096]{2,0,1:T(2,128)S(1)} %get-tuple-element.98), channel_id=1, source_target_pairs={{0,4},{1,5},{2,6},{3,7},{4,0},{5,1},{6,2},{7,3},{8,12},{9,13},{10,... | collective-permute-start | bytes 98312 | tf_op jit(solution)/shard_map/ppermute | solution.py:24
  373.9 5.9 %collective-permute-start.93 = (f32[2,1,4096]{2,0,1:T(2,128)S(1)}, f32[2,1,4096]{2,0,1:T(2,128)S(1)}, u32[]{:S(2)}, u32[]{:S(2)}) collective-permute-start(f32[2,1,4096]{2,0,1:T(2,128)S(1)} %get-tuple-element.96), channel_id=1, source_target_pairs={{0,2},{1,3},{2,4},{3,5},{4,6},{5,7},{6,0},{7,1},{8,10},{9,11},{10,... | collective-permute-start | bytes 98312 | tf_op jit(solution)/shard_map/ppermute | solution.py:24
  374.7 5.5 %collective-permute-start.94 = (f32[2,1,4096]{2,0,1:T(2,128)S(1)}, f32[2,1,4096]{2,0,1:T(2,128)S(1)}, u32[]{:S(2)}, u32[]{:S(2)}) collective-permute-start(f32[2,1,4096]{2,0,1:T(2,128)S(1)} %get-tuple-element.96), channel_id=1, source_target_pairs={{0,4},{1,5},{2,6},{3,7},{4,0},{5,1},{6,2},{7,3},{8,12},{9,13},{10,... | collective-permute-start | bytes 98312 | tf_op jit(solution)/shard_map/ppermute | solution.py:24
  389.4 5.8 %collective-permute-start.97 = (f32[2,1,4096]{2,0,1:T(2,128)S(1)}, f32[2,1,4096]{2,0,1:T(2,128)S(1)}, u32[]{:S(2)}, u32[]{:S(2)}) collective-permute-start(f32[2,1,4096]{2,0,1:T(2,128)S(1)} %get-tuple-element.94), channel_id=1, source_target_pairs={{0,2},{1,3},{2,4},{3,5},{4,6},{5,7},{6,0},{7,1},{8,10},{9,11},{10,... | collective-permute-start | bytes 98312 | tf_op jit(solution)/shard_map/ppermute | solution.py:24
  405.5 5.8 %collective-permute-start.101 = (f32[2,1,4096]{2,0,1:T(2,128)S(1)}, f32[2,1,4096]{2,0,1:T(2,128)S(1)}, u32[]{:S(2)}, u32[]{:S(2)}) collective-permute-start(f32[2,1,4096]{2,0,1:T(2,128)S(1)} %get-tuple-element.92), channel_id=1, source_target_pairs={{0,2},{1,3},{2,4},{3,5},{4,6},{5,7},{6,0},{7,1},{8,10},{9,11},{10,... | collective-permute-start | bytes 98312 | tf_op jit(solution)/shard_map/ppermute | solution.py:24
  406.6 5.4 collective-permute-start.102
  427.1 5.8 %collective-permute-start.107 = (f32[2,1,4096]{2,0,1:T(2,128)S(1)}, f32[2,1,4096]{2,0,1:T(2,128)S(1)}, u32[]{:S(2)}, u32[]{:S(2)}) collective-permute-start(f32[2,1,4096]{2,0,1:T(2,128)S(1)} %get-tuple-element.90), channel_id=1, source_target_pairs={{0,2},{1,3},{2,4},{3,5},{4,6},{5,7},{6,0},{7,1},{8,10},{9,11},{10,... | collective-permute-start | bytes 98312 | tf_op jit(solution)/shard_map/ppermute | solution.py:24
  428.5 5.0 collective-permute-start.108
  443.0 5.8 %collective-permute-start.111 = (f32[2,1,4096]{2,0,1:T(2,128)S(1)}, f32[2,1,4096]{2,0,1:T(2,128)S(1)}, u32[]{:S(2)}, u32[]{:S(2)}) collective-permute-start(f32[2,1,4096]{2,0,1:T(2,128)S(1)} %get-tuple-element.88), channel_id=1, source_target_pairs={{0,2},{1,3},{2,4},{3,5},{4,6},{5,7},{6,0},{7,1},{8,10},{9,11},{10,... | collective-permute-start | bytes 98312 | tf_op jit(solution)/shard_map/ppermute | solution.py:24
  444.1 5.4 collective-permute-start.112
  458.5 5.8 %collective-permute-start.115 = (f32[2,1,4096]{2,0,1:T(2,128)S(1)}, f32[2,1,4096]{2,0,1:T(2,128)S(1)}, u32[]{:S(2)}, u32[]{:S(2)}) collective-permute-start(f32[2,1,4096]{2,0,1:T(2,128)S(1)} %get-tuple-element.86), channel_id=1, source_target_pairs={{0,2},{1,3},{2,4},{3,5},{4,6},{5,7},{6,0},{7,1},{8,10},{9,11},{10,... | collective-permute-start | bytes 98312 | tf_op jit(solution)/shard_map/ppermute | solution.py:24
  460.1 4.9 collective-permute-start.116
  474.4 5.8 %collective-permute-start.119 = (f32[2,1,4096]{2,0,1:T(2,128)S(1)}, f32[2,1,4096]{2,0,1:T(2,128)S(1)}, u32[]{:S(2)}, u32[]{:S(2)}) collective-permute-start(f32[2,1,4096]{2,0,1:T(2,128)S(1)} %get-tuple-element.84), channel_id=1, source_target_pairs={{0,2},{1,3},{2,4},{3,5},{4,6},{5,7},{6,0},{7,1},{8,10},{9,11},{10,... | collective-permute-start | bytes 98312 | tf_op jit(solution)/shard_map/ppermute | solution.py:24
  475.5 5.3 collective-permute-start.120
  489.9 5.8 %collective-permute-start.123 = (f32[2,1,4096]{2,0,1:T(2,128)S(1)}, f32[2,1,4096]{2,0,1:T(2,128)S(1)}, u32[]{:S(2)}, u32[]{:S(2)}) collective-permute-start(f32[2,1,4096]{2,0,1:T(2,128)S(1)} %get-tuple-element.82), channel_id=1, source_target_pairs={{0,2},{1,3},{2,4},{3,5},{4,6},{5,7},{6,0},{7,1},{8,10},{9,11},{10,... | collective-permute-start | bytes 98312 | tf_op jit(solution)/shard_map/ppermute | solution.py:24
  491.4 6.2 %collective-permute-start.124 = (f32[2,1,4096]{2,0,1:T(2,128)S(1)}, f32[2,1,4096]{2,0,1:T(2,128)S(1)}, u32[]{:S(2)}, u32[]{:S(2)}) collective-permute-start(f32[2,1,4096]{2,0,1:T(2,128)S(1)} %get-tuple-element.82), channel_id=1, source_target_pairs={{0,4},{1,5},{2,6},{3,7},{4,0},{5,1},{6,2},{7,3},{8,12},{9,13},{10,... | collective-permute-start | bytes 98312 | tf_op jit(solution)/shard_map/ppermute | solution.py:24
  506.6 5.9 %collective-permute-start.127 = (f32[2,1,4096]{2,0,1:T(2,128)S(1)}, f32[2,1,4096]{2,0,1:T(2,128)S(1)}, u32[]{:S(2)}, u32[]{:S(2)}) collective-permute-start(f32[2,1,4096]{2,0,1:T(2,128)S(1)} %get-tuple-element.80), channel_id=1, source_target_pairs={{0,2},{1,3},{2,4},{3,5},{4,6},{5,7},{6,0},{7,1},{8,10},{9,11},{10,... | collective-permute-start | bytes 98312 | tf_op jit(solution)/shard_map/ppermute | solution.py:24
  507.4 5.5 %collective-permute-start.128 = (f32[2,1,4096]{2,0,1:T(2,128)S(1)}, f32[2,1,4096]{2,0,1:T(2,128)S(1)}, u32[]{:S(2)}, u32[]{:S(2)}) collective-permute-start(f32[2,1,4096]{2,0,1:T(2,128)S(1)} %get-tuple-element.80), channel_id=1, source_target_pairs={{0,4},{1,5},{2,6},{3,7},{4,0},{5,1},{6,2},{7,3},{8,12},{9,13},{10,... | collective-permute-start | bytes 98312 | tf_op jit(solution)/shard_map/ppermute | solution.py:24
  522.0 5.8 %collective-permute-start.131 = (f32[2,1,4096]{2,0,1:T(2,128)S(1)}, f32[2,1,4096]{2,0,1:T(2,128)S(1)}, u32[]{:S(2)}, u32[]{:S(2)}) collective-permute-start(f32[2,1,4096]{2,0,1:T(2,128)S(1)} %get-tuple-element.78), channel_id=1, source_target_pairs={{0,2},{1,3},{2,4},{3,5},{4,6},{5,7},{6,0},{7,1},{8,10},{9,11},{10,... | collective-permute-start | bytes 98312 | tf_op jit(solution)/shard_map/ppermute | solution.py:24
  538.3 5.4 collective-permute-start.135
  (86 other events, 581.1 us)
where the time goes:
time: 561 us; the launch traced here: 550 us
  waiting for transfers between devices  207 us (37%)
  starting transfers between devices  163 us (29%)
  other arithmetic  128 us (23%)
  local copies, waits for them, and re-layouts  49.1 us (9%)
    ppermute x99, starting transfers between devices, collect(): parts.append(lax.ppermute(pair, 'sub', moves))  135 us
    ppermute x33, waiting for transfers between devices, collect(): partner = lax.ppermute(value, 'sub', [(i, i ^ 1) for i in range(count)])  101 us
    ppermute x99, waiting for transfers between devices, collect(): parts.append(lax.ppermute(pair, 'sub', moves))  98.9 us
    reduce_sum x32, other arithmetic, apply_blocks(): result = jnp.sum(blocks[0] * picked[:, None, :], axis=2)  89.8 us
    gather x32, local copies, waits for them, and re-layouts, on_device(): others = whole.reshape(-1, width)[remote_cols]  24.2 us
    ppermute x33, starting transfers between devices, collect(): partner = lax.ppermute(value, 'sub', [(i, i ^ 1) for i in range(count)])  23.5 us
    add x32, other arithmetic, on_device(): field = field + (rhs - result - capacity * field) / system_diag  22.3 us
  transfers between devices with their start and end apart: 140, of which 130 were waited for; matrix products, arithmetic and copies ran while one was open for 4% of the time, Pallas kernels for 0%

commit v1 on v0

--- a/solution.py
+++ b/solution.py
@@ -16,18 +16,19 @@
 def collect(value):
     count = lax.axis_size("sub")
     half = count // 2
-    partner = lax.ppermute(value, "sub", [(i, i ^ 1) for i in range(count)])
-    pair = jnp.stack([value, partner])
-    parts = [pair]
+    parts = [value]
     for k in range(1, half):
         moves = [(i, ((i // 2 + k) % half) * 2 + i % 2) for i in range(count)]
-        parts.append(lax.ppermute(pair, "sub", moves))
-    return jnp.stack(parts).reshape((count,) + value.shape)
+        parts.append(lax.ppermute(value, "sub", moves))
+    group = jnp.stack(parts)
+    partner = lax.ppermute(group, "sub", [(i, i ^ 1) for i in range(count)])
+    return jnp.stack([group, partner]).reshape((count,) + value.shape)
 
 
 def slot_of(index, me, count, chunk):
     owner = index // chunk
-    slot = ((me // 2 - owner // 2) % (count // 2)) * 2 + ((owner % 2) ^ (me % 2))
+    half = count // 2
+    slot = ((owner % 2) ^ (me % 2)) * half + (me // 2 - owner // 2) % half
     return slot * chunk + index % chunk
 
 

time: 561 us -> 573 us (1.021)
  starting transfers between devices: 163 us -> 197 us
  waiting for transfers between devices: 207 us -> 189 us
    ppermute x132, starting transfers between devices: 158 us -> 192 us  [the longest x99 140 us: collect(): parts.append(lax.ppermute(value, 'sub', moves))]
    ppermute x132, waiting for transfers between devices: 200 us -> 182 us  [the longest x99 93.7 us: collect(): parts.append(lax.ppermute(value, 'sub', moves))]
  transfers between devices with their start and end apart: 140 -> 140, of which waited for: 130 -> 125; matrix products, arithmetic and copies ran while one was open for 4% -> 4% of each run, Pallas kernels for 0% -> 0%
where the time goes in v1:
time: 573 us; the launch traced here: 563 us
  starting transfers between devices  197 us (34%)
  waiting for transfers between devices  189 us (33%)
  other arithmetic  128 us (22%)
  local copies, waits for them, and re-layouts  47.5 us (8%)
    ppermute x99, starting transfers between devices, collect(): parts.append(lax.ppermute(value, 'sub', moves))  140 us
    ppermute x99, waiting for transfers between devices, collect(): parts.append(lax.ppermute(value, 'sub', moves))  93.7 us
    reduce_sum x32, other arithmetic, apply_blocks(): result = jnp.sum(blocks[0] * picked[:, None, :], axis=2)  89.8 us
    ppermute x33, waiting for transfers between devices, collect(): partner = lax.ppermute(group, 'sub', [(i, i ^ 1) for i in range(count)])  88.1 us
    ppermute x33, starting transfers between devices, collect(): partner = lax.ppermute(group, 'sub', [(i, i ^ 1) for i in range(count)])  52.3 us
    gather x32, local copies, waits for them, and re-layouts, on_device(): others = whole.reshape(-1, width)[remote_cols]  23.2 us
    add x32, other arithmetic, on_device(): field = field + (rhs - result - capacity * field) / system_diag  22.3 us
  transfers between devices with their start and end apart: 140, of which 125 were waited for; matrix products, arithmetic and copies ran while one was open for 4% of the time, Pallas kernels for 0%

profile of v1, /device:TPU:0, one launch (start us, length us, event | category | flops | bytes accessed | tf_op | source)
XLA Modules:
  0.0 563.3 jit_solution(8061952392461251834)
XLA Ops:
  0.6 3.1 collective-permute-start
  19.4 2.7 collective-permute-done.3
  23.2 2.8 fusion
  27.9 2.8 collective-permute-start.6
  34.7 2.7 collective-permute-done.7
  38.5 2.8 fusion.1
  51.5 2.7 collective-permute-done.11
  55.2 2.8 fusion.2
  67.4 2.7 collective-permute-done.15
  71.1 2.8 fusion.3
  83.7 2.7 collective-permute-done.19
  87.5 2.8 fusion.4
  99.5 2.7 collective-permute-done.23
  103.2 2.8 fusion.5
  115.9 2.7 collective-permute-done.27
  119.7 2.8 fusion.6
  135.6 2.8 fusion.7
  156.1 2.8 fusion.8
  169.7 2.7 collective-permute-done.41
  173.5 2.8 fusion.9
  185.9 2.7 collective-permute-done.45
  189.7 2.8 fusion.10
  197.2 4.1 collective-permute-done.46
  203.0 2.7 collective-permute-done.49
  206.8 2.8 fusion.11
  211.2 2.7 collective-permute-start.51
  219.8 2.7 collective-permute-done.53
  223.6 2.8 fusion.12
  235.4 2.7 collective-permute-done.57
  239.2 2.8 fusion.13
  242.8 2.7 collective-permute-start.58
  252.1 2.7 collective-permute-done.61
  255.8 2.8 fusion.14
  260.2 3.1 collective-permute-start.63
  268.7 2.7 collective-permute-done.65
  272.5 2.8 fusion.15
  276.8 2.7 collective-permute-start.67
  292.0 2.8 fusion.16
  309.4 2.8 fusion.17
  326.0 2.8 fusion.18
  338.1 2.7 collective-permute-done.83
  342.0 2.8 fusion.19
  358.5 2.8 fusion.20
  370.5 3.0 collective-permute-done.91
  374.7 2.8 fusion.21
  387.1 2.7 collective-permute-done.95
  391.0 2.8 fusion.22
  395.8 2.8 collective-permute-start.97
  408.0 2.8 fusion.23
  412.2 2.9 collective-permute-start.101
  428.5 2.8 fusion.24
  442.2 2.7 collective-permute-done.109
  445.9 2.8 fusion.25
  458.5 2.7 collective-permute-done.113
  462.2 2.8 fusion.26
  474.4 2.7 collective-permute-done.117
  478.1 2.8 fusion.27
  490.7 2.7 collective-permute-done.121
  494.4 2.8 fusion.28
  506.5 3.0 collective-permute-done.125
  510.5 2.8 fusion.29
  526.8 2.8 fusion.30
  539.4 2.7 collective-permute-done.133
  543.1 2.8 fusion.31
  (618 shorter events, 381.7 us)
Async XLA Ops:
  0.6 17.0 %collective-permute-start = (f32[1,4096]{1,0:T(1,128)}, f32[1,4096]{1,0:T(1,128)S(1)}, u32[]{:S(2)}, u32[]{:S(2)}) collective-permute-start(f32[1,4096]{1,0:T(1,128)} %param.13), channel_id=1, source_target_pairs={{0,2},{1,3},{2,4},{3,5},{4,6},{5,7},{6,0},{7,1},{8,10},{9,11},{10,... | collective-permute-start | bytes 49160 | tf_op jit(solution)/shard_map/ppermute | solution.py:22
  3.7 13.9 %collective-permute-start.1 = (f32[1,4096]{1,0:T(1,128)}, f32[1,4096]{1,0:T(1,128)S(1)}, u32[]{:S(2)}, u32[]{:S(2)}) collective-permute-start(f32[1,4096]{1,0:T(1,128)} %param.13), channel_id=1, source_target_pairs={{0,4},{1,5},{2,6},{3,7},{4,0},{5,1},{6,2},{7,3},{8,12},{9,13},{10,... | collective-permute-start | bytes 49160 | tf_op jit(solution)/shard_map/ppermute | solution.py:22
  6.3 11.4 %collective-permute-start.2 = (f32[1,4096]{1,0:T(1,128)}, f32[1,4096]{1,0:T(1,128)S(1)}, u32[]{:S(2)}, u32[]{:S(2)}) collective-permute-start(f32[1,4096]{1,0:T(1,128)} %param.13), channel_id=1, source_target_pairs={{0,6},{1,7},{2,0},{3,1},{4,2},{5,3},{6,4},{7,5},{8,14},{9,15},{10,... | collective-permute-start | bytes 49160 | tf_op jit(solution)/shard_map/ppermute | solution.py:22
  26.8 5.6 collective-permute-start.4
  27.6 4.9 collective-permute-start.5
  27.9 5.1 collective-permute-start.6
  42.1 5.6 collective-permute-start.8
  44.2 4.6 collective-permute-start.9
  58.8 5.6 collective-permute-start.12
  59.5 5.0 collective-permute-start.13
  74.7 5.6 collective-permute-start.16
  76.2 4.6 collective-permute-start.17
  91.1 5.6 collective-permute-start.20
  92.1 5.0 collective-permute-start.21
  106.9 5.6 collective-permute-start.24
  108.5 4.6 collective-permute-start.25
  123.3 5.6 collective-permute-start.28
  124.4 4.8 collective-permute-start.29
  139.2 5.6 collective-permute-start.32
  140.7 4.6 collective-permute-start.33
  161.3 5.7 %collective-permute-start.38 = (f32[1,4096]{1,0:T(1,128)S(1)}, f32[1,4096]{1,0:T(1,128)S(1)}, u32[]{:S(2)}, u32[]{:S(2)}) collective-permute-start(f32[1,4096]{1,0:T(1,128)S(1)} %get-tuple-element.53), channel_id=1, source_target_pairs={{0,2},{1,3},{2,4},{3,5},{4,6},{5,7},{6,0},{7,1},{8,10},{9,11},{10,... | collective-permute-start | bytes 49160 | tf_op jit(solution)/shard_map/ppermute | solution.py:22
  162.3 4.8 collective-permute-start.39
  177.1 5.6 collective-permute-start.42
  178.6 4.6 collective-permute-start.43
  195.8 5.5 collective-permute-start.46
  195.8 5.5 collective-permute-start.47
  210.4 5.6 collective-permute-start.50
  211.2 4.8 collective-permute-start.51
  227.2 5.6 collective-permute-start.54
  228.2 5.0 collective-permute-start.55
  242.8 5.6 collective-permute-start.58
  245.5 4.6 collective-permute-start.59
  259.5 5.7 %collective-permute-start.62 = (f32[1,4096]{1,0:T(1,128)S(1)}, f32[1,4096]{1,0:T(1,128)S(1)}, u32[]{:S(2)}, u32[]{:S(2)}) collective-permute-start(f32[1,4096]{1,0:T(1,128)S(1)} %get-tuple-element.41), channel_id=1, source_target_pairs={{0,2},{1,3},{2,4},{3,5},{4,6},{5,7},{6,0},{7,1},{8,10},{9,11},{10,... | collective-permute-start | bytes 49160 | tf_op jit(solution)/shard_map/ppermute | solution.py:22
  260.2 5.0 collective-permute-start.63
  276.1 5.6 collective-permute-start.66
  276.8 4.9 collective-permute-start.67
  297.2 5.7 %collective-permute-start.72 = (f32[1,4096]{1,0:T(1,128)S(1)}, f32[1,4096]{1,0:T(1,128)S(1)}, u32[]{:S(2)}, u32[]{:S(2)}) collective-permute-start(f32[1,4096]{1,0:T(1,128)S(1)} %get-tuple-element.35), channel_id=1, source_target_pairs={{0,2},{1,3},{2,4},{3,5},{4,6},{5,7},{6,0},{7,1},{8,10},{9,11},{10,... | collective-permute-start | bytes 49160 | tf_op jit(solution)/shard_map/ppermute | solution.py:22
  298.2 4.8 collective-permute-start.73
  313.0 5.6 collective-permute-start.76
  314.6 4.6 collective-permute-start.77
  329.6 5.6 collective-permute-start.80
  330.6 4.9 collective-permute-start.81
  345.6 5.6 collective-permute-start.84
  362.1 5.6 collective-permute-start.88
  363.1 4.9 collective-permute-start.89
  378.3 5.6 collective-permute-start.92
  380.8 4.6 collective-permute-start.93
  394.7 5.6 collective-permute-start.96
  395.8 4.6 collective-permute-start.97
  411.6 5.6 collective-permute-start.100
  412.2 5.0 collective-permute-start.101
  433.9 5.7 %collective-permute-start.106 = (f32[1,4096]{1,0:T(1,128)S(1)}, f32[1,4096]{1,0:T(1,128)S(1)}, u32[]{:S(2)}, u32[]{:S(2)}) collective-permute-start(f32[1,4096]{1,0:T(1,128)S(1)} %get-tuple-element.17), channel_id=1, source_target_pairs={{0,2},{1,3},{2,4},{3,5},{4,6},{5,7},{6,0},{7,1},{8,10},{9,11},{10,... | collective-permute-start | bytes 49160 | tf_op jit(solution)/shard_map/ppermute | solution.py:22
  434.9 4.8 collective-permute-start.107
  449.5 5.6 collective-permute-start.110
  465.9 5.6 collective-permute-start.114
  466.9 4.9 collective-permute-start.115
  481.8 5.6 collective-permute-start.118
  483.2 4.6 collective-permute-start.119
  498.1 5.6 collective-permute-start.122
  499.1 4.9 collective-permute-start.123
  514.2 5.6 collective-permute-start.126
  530.4 5.6 collective-permute-start.130
  531.5 4.6 collective-permute-start.131
  547.4 5.4 collective-permute-start.134
  (86 other events, 724.5 us)

commit v2 on v0

--- a/solution.py
+++ b/solution.py
@@ -51,7 +51,8 @@
     rows_here = blocks.shape[1]
     local_count = rows_here * width
     offset = lax.axis_index("sub") * local_count
-    diag = jnp.diagonal(blocks[..., :width], axis1=2, axis2=3).reshape(1, local_count)
+    eye = jnp.arange(width)[:, None] == jnp.arange(width)[None, :]
+    diag = jnp.sum(jnp.where(eye, blocks[0, :, :, :width], 0.0), axis=2).reshape(1, local_count)
     system_diag = diag + capacity
     count = lax.axis_size("sub")
     me = lax.axis_index("sub")

time: 561 us -> 558 us (level)
  starting transfers between devices: 163 us -> 129 us
  waiting for transfers between devices: 207 us -> 240 us
    ppermute x99, waiting for transfers between devices: 98.9 us -> 133 us  [collect(): parts.append(lax.ppermute(pair, 'sub', moves))]
    ppermute x99, starting transfers between devices: 135 us -> 103 us  [collect(): parts.append(lax.ppermute(pair, 'sub', moves))]
  transfers between devices with their start and end apart: 140 -> 140, of which waited for: 130 -> 134; matrix products, arithmetic and copies ran while one was open for 4% -> 4% of each run, Pallas kernels for 0% -> 0%
where the time goes in v2:
time: 558 us; the launch traced here: 548 us
  waiting for transfers between devices  240 us (43%)
  other arithmetic  131 us (23%)
  starting transfers between devices  129 us (23%)
  local copies, waits for them, and re-layouts  45.3 us (8%)
    ppermute x99, waiting for transfers between devices, collect(): parts.append(lax.ppermute(pair, 'sub', moves))  133 us
    ppermute x33, waiting for transfers between devices, collect(): partner = lax.ppermute(value, 'sub', [(i, i ^ 1) for i in range(count)])  103 us
    ppermute x99, starting transfers between devices, collect(): parts.append(lax.ppermute(pair, 'sub', moves))  103 us
    reduce_sum x32, other arithmetic, apply_blocks(): result = jnp.sum(blocks[0] * picked[:, None, :], axis=2)  89.8 us
    gather x32, local copies, waits for them, and re-layouts, on_device(): others = whole.reshape(-1, width)[remote_cols]  24.2 us
    add x32, other arithmetic, on_device(): field = field + (rhs - result - capacity * field) / system_diag  22.3 us
    ppermute x33, starting transfers between devices, collect(): partner = lax.ppermute(value, 'sub', [(i, i ^ 1) for i in range(count)])  21.3 us
  transfers between devices with their start and end apart: 140, of which 134 were waited for; matrix products, arithmetic and copies ran while one was open for 4% of the time, Pallas kernels for 0%

profile of v2, /device:TPU:0, one launch (start us, length us, event | category | flops | bytes accessed | tf_op | source)
XLA Modules:
  0.0 547.9 jit_solution(7278586869886559841)
XLA Ops:
  0.6 3.1 collective-permute-start
  11.2 3.7 collective-permute-start.3
  21.7 2.8 fusion
  25.9 3.2 collective-permute-done.4
  37.3 2.8 fusion.1
  41.5 3.2 collective-permute-done.8
  53.3 2.8 fusion.2
  57.5 3.2 collective-permute-done.12
  68.8 2.8 fusion.3
  73.0 3.2 collective-permute-done.16
  84.9 2.8 fusion.4
  89.1 3.2 collective-permute-done.20
  100.5 2.8 fusion.5
  104.7 3.2 collective-permute-done.24
  116.5 2.8 fusion.6
  120.7 3.2 collective-permute-done.28
  132.3 2.8 fusion.7
  136.5 3.2 collective-permute-done.32
  151.3 2.8 fusion.8
  157.0 3.2 collective-permute-done.38
  168.7 2.8 fusion.9
  172.9 3.2 collective-permute-done.42
  184.5 2.8 fusion.10
  188.7 3.2 collective-permute-done.46
  200.4 2.8 fusion.11
  204.6 3.2 collective-permute-done.50
  216.6 2.8 fusion.12
  220.9 3.2 collective-permute-done.54
  228.1 3.6 collective-permute-done.56
  233.0 2.8 fusion.13
  237.2 3.2 collective-permute-done.58
  249.2 2.8 fusion.14
  253.4 3.2 collective-permute-done.62
  264.9 2.8 fusion.15
  269.1 3.2 collective-permute-done.66
  288.9 3.2 collective-permute-done.72
  300.3 2.8 fusion.17
  304.5 3.2 collective-permute-done.76
  316.5 2.8 fusion.18
  320.7 3.2 collective-permute-done.80
  332.2 2.8 fusion.19
  336.4 3.2 collective-permute-done.84
  343.6 2.8 collective-permute-done.86
  348.4 2.8 fusion.20
  352.6 3.2 collective-permute-done.88
  364.5 2.8 fusion.21
  368.7 3.2 collective-permute-done.92
  380.6 2.8 fusion.22
  384.8 3.2 collective-permute-done.96
  396.3 2.8 fusion.23
  400.5 3.2 collective-permute-done.100
  421.4 3.2 collective-permute-done.106
  432.7 2.8 fusion.25
  436.9 3.2 collective-permute-done.110
  448.6 2.8 fusion.26
  452.8 3.2 collective-permute-done.114
  468.4 3.2 collective-permute-done.118
  475.6 2.8 collective-permute-done.120
  484.6 3.2 collective-permute-done.122
  500.4 3.2 collective-permute-done.126
  512.2 2.8 fusion.30
  516.4 3.2 collective-permute-done.130
  527.7 2.8 fusion.31
  532.5 3.1 collective-permute-done.134
  (619 shorter events, 350.5 us)
Async XLA Ops:
  0.6 9.8 %collective-permute-start = (f32[1,4096]{1,0:T(1,128)}, f32[1,4096]{1,0:T(1,128)S(1)}, u32[]{:S(2)}, u32[]{:S(2)}) collective-permute-start(f32[1,4096]{1,0:T(1,128)} %param.13), channel_id=1, source_target_pairs={{0,1},{1,0},{2,3},{3,2},{4,5},{5,4},{6,7},{7,6},{8,9},{9,8},{10,11... | collective-permute-start | bytes 49160 | tf_op jit(solution)/shard_map/ppermute | solution.py:19
  11.2 6.4 %collective-permute-start.3 = (f32[2,1,4096]{2,0,1:T(2,128)S(1)}, f32[2,1,4096]{2,0,1:T(2,128)S(1)}, u32[]{:S(2)}, u32[]{:S(2)}) collective-permute-start(f32[2,1,4096]{2,0,1:T(2,128)S(1)} %get-tuple-element.140), channel_id=1, source_target_pairs={{0,6},{1,7},{2,0},{3,1},{4,2},{5,3},{6,4},{7,5},{8,14},{9,15},{10,... | collective-permute-start | bytes 98312 | tf_op jit(solution)/shard_map/ppermute | solution.py:24
  14.9 4.8 collective-permute-start.2
  14.9 5.7 %collective-permute-start.1 = (f32[2,1,4096]{2,0,1:T(2,128)S(1)}, f32[2,1,4096]{2,0,1:T(2,128)S(1)}, u32[]{:S(2)}, u32[]{:S(2)}) collective-permute-start(f32[2,1,4096]{2,0,1:T(2,128)S(1)} %get-tuple-element.140), channel_id=1, source_target_pairs={{0,2},{1,3},{2,4},{3,5},{4,6},{5,7},{6,0},{7,1},{8,10},{9,11},{10,... | collective-permute-start | bytes 98312 | tf_op jit(solution)/shard_map/ppermute | solution.py:24
  29.8 4.8 collective-permute-start.6
  30.5 5.7 %collective-permute-start.5 = (f32[2,1,4096]{2,0,1:T(2,128)S(1)}, f32[2,1,4096]{2,0,1:T(2,128)S(1)}, u32[]{:S(2)}, u32[]{:S(2)}) collective-permute-start(f32[2,1,4096]{2,0,1:T(2,128)S(1)} %get-tuple-element.138), channel_id=1, source_target_pairs={{0,2},{1,3},{2,4},{3,5},{4,6},{5,7},{6,0},{7,1},{8,10},{9,11},{10,... | collective-permute-start | bytes 98312 | tf_op jit(solution)/shard_map/ppermute | solution.py:24
  46.2 5.2 collective-permute-start.10
  46.5 5.7 %collective-permute-start.9 = (f32[2,1,4096]{2,0,1:T(2,128)S(1)}, f32[2,1,4096]{2,0,1:T(2,128)S(1)}, u32[]{:S(2)}, u32[]{:S(2)}) collective-permute-start(f32[2,1,4096]{2,0,1:T(2,128)S(1)} %get-tuple-element.136), channel_id=1, source_target_pairs={{0,2},{1,3},{2,4},{3,5},{4,6},{5,7},{6,0},{7,1},{8,10},{9,11},{10,... | collective-permute-start | bytes 98312 | tf_op jit(solution)/shard_map/ppermute | solution.py:24
  61.8 4.8 collective-permute-start.14
  61.9 5.7 %collective-permute-start.13 = (f32[2,1,4096]{2,0,1:T(2,128)S(1)}, f32[2,1,4096]{2,0,1:T(2,128)S(1)}, u32[]{:S(2)}, u32[]{:S(2)}) collective-permute-start(f32[2,1,4096]{2,0,1:T(2,128)S(1)} %get-tuple-element.134), channel_id=1, source_target_pairs={{0,2},{1,3},{2,4},{3,5},{4,6},{5,7},{6,0},{7,1},{8,10},{9,11},{10,... | collective-permute-start | bytes 98312 | tf_op jit(solution)/shard_map/ppermute | solution.py:24
  77.8 5.2 collective-permute-start.18
  77.8 5.9 %collective-permute-start.17 = (f32[2,1,4096]{2,0,1:T(2,128)S(1)}, f32[2,1,4096]{2,0,1:T(2,128)S(1)}, u32[]{:S(2)}, u32[]{:S(2)}) collective-permute-start(f32[2,1,4096]{2,0,1:T(2,128)S(1)} %get-tuple-element.132), channel_id=1, source_target_pairs={{0,2},{1,3},{2,4},{3,5},{4,6},{5,7},{6,0},{7,1},{8,10},{9,11},{10,... | collective-permute-start | bytes 98312 | tf_op jit(solution)/shard_map/ppermute | solution.py:24
  93.7 5.2 collective-permute-start.22
  93.7 5.7 %collective-permute-start.21 = (f32[2,1,4096]{2,0,1:T(2,128)S(1)}, f32[2,1,4096]{2,0,1:T(2,128)S(1)}, u32[]{:S(2)}, u32[]{:S(2)}) collective-permute-start(f32[2,1,4096]{2,0,1:T(2,128)S(1)} %get-tuple-element.130), channel_id=1, source_target_pairs={{0,2},{1,3},{2,4},{3,5},{4,6},{5,7},{6,0},{7,1},{8,10},{9,11},{10,... | collective-permute-start | bytes 98312 | tf_op jit(solution)/shard_map/ppermute | solution.py:24
  109.4 5.2 collective-permute-start.26
  109.5 5.9 %collective-permute-start.25 = (f32[2,1,4096]{2,0,1:T(2,128)S(1)}, f32[2,1,4096]{2,0,1:T(2,128)S(1)}, u32[]{:S(2)}, u32[]{:S(2)}) collective-permute-start(f32[2,1,4096]{2,0,1:T(2,128)S(1)} %get-tuple-element.128), channel_id=1, source_target_pairs={{0,2},{1,3},{2,4},{3,5},{4,6},{5,7},{6,0},{7,1},{8,10},{9,11},{10,... | collective-permute-start | bytes 98312 | tf_op jit(solution)/shard_map/ppermute | solution.py:24
  125.2 4.8 collective-permute-start.30
  125.4 5.7 %collective-permute-start.29 = (f32[2,1,4096]{2,0,1:T(2,128)S(1)}, f32[2,1,4096]{2,0,1:T(2,128)S(1)}, u32[]{:S(2)}, u32[]{:S(2)}) collective-permute-start(f32[2,1,4096]{2,0,1:T(2,128)S(1)} %get-tuple-element.126), channel_id=1, source_target_pairs={{0,2},{1,3},{2,4},{3,5},{4,6},{5,7},{6,0},{7,1},{8,10},{9,11},{10,... | collective-permute-start | bytes 98312 | tf_op jit(solution)/shard_map/ppermute | solution.py:24
  141.0 4.8 collective-permute-start.34
  141.2 5.7 %collective-permute-start.33 = (f32[2,1,4096]{2,0,1:T(2,128)S(1)}, f32[2,1,4096]{2,0,1:T(2,128)S(1)}, u32[]{:S(2)}, u32[]{:S(2)}) collective-permute-start(f32[2,1,4096]{2,0,1:T(2,128)S(1)} %get-tuple-element.124), channel_id=1, source_target_pairs={{0,2},{1,3},{2,4},{3,5},{4,6},{5,7},{6,0},{7,1},{8,10},{9,11},{10,... | collective-permute-start | bytes 98312 | tf_op jit(solution)/shard_map/ppermute | solution.py:24
  161.6 5.2 collective-permute-start.40
  161.7 5.7 %collective-permute-start.39 = (f32[2,1,4096]{2,0,1:T(2,128)S(1)}, f32[2,1,4096]{2,0,1:T(2,128)S(1)}, u32[]{:S(2)}, u32[]{:S(2)}) collective-permute-start(f32[2,1,4096]{2,0,1:T(2,128)S(1)} %get-tuple-element.122), channel_id=1, source_target_pairs={{0,2},{1,3},{2,4},{3,5},{4,6},{5,7},{6,0},{7,1},{8,10},{9,11},{10,... | collective-permute-start | bytes 98312 | tf_op jit(solution)/shard_map/ppermute | solution.py:24
  177.4 5.2 collective-permute-start.44
  177.5 5.7 %collective-permute-start.43 = (f32[2,1,4096]{2,0,1:T(2,128)S(1)}, f32[2,1,4096]{2,0,1:T(2,128)S(1)}, u32[]{:S(2)}, u32[]{:S(2)}) collective-permute-start(f32[2,1,4096]{2,0,1:T(2,128)S(1)} %get-tuple-element.120), channel_id=1, source_target_pairs={{0,2},{1,3},{2,4},{3,5},{4,6},{5,7},{6,0},{7,1},{8,10},{9,11},{10,... | collective-permute-start | bytes 98312 | tf_op jit(solution)/shard_map/ppermute | solution.py:24
  193.3 5.2 collective-permute-start.48
  193.4 5.7 %collective-permute-start.47 = (f32[2,1,4096]{2,0,1:T(2,128)S(1)}, f32[2,1,4096]{2,0,1:T(2,128)S(1)}, u32[]{:S(2)}, u32[]{:S(2)}) collective-permute-start(f32[2,1,4096]{2,0,1:T(2,128)S(1)} %get-tuple-element.118), channel_id=1, source_target_pairs={{0,2},{1,3},{2,4},{3,5},{4,6},{5,7},{6,0},{7,1},{8,10},{9,11},{10,... | collective-permute-start | bytes 98312 | tf_op jit(solution)/shard_map/ppermute | solution.py:24
  209.2 4.8 collective-permute-start.52
  209.3 6.1 %collective-permute-start.51 = (f32[2,1,4096]{2,0,1:T(2,128)S(1)}, f32[2,1,4096]{2,0,1:T(2,128)S(1)}, u32[]{:S(2)}, u32[]{:S(2)}) collective-permute-start(f32[2,1,4096]{2,0,1:T(2,128)S(1)} %get-tuple-element.116), channel_id=1, source_target_pairs={{0,2},{1,3},{2,4},{3,5},{4,6},{5,7},{6,0},{7,1},{8,10},{9,11},{10,... | collective-permute-start | bytes 98312 | tf_op jit(solution)/shard_map/ppermute | solution.py:24
  225.4 6.3 %collective-permute-start.56 = (f32[2,1,4096]{2,0,1:T(2,128)S(1)}, f32[2,1,4096]{2,0,1:T(2,128)S(1)}, u32[]{:S(2)}, u32[]{:S(2)}) collective-permute-start(f32[2,1,4096]{2,0,1:T(2,128)S(1)} %get-tuple-element.114), channel_id=1, source_target_pairs={{0,4},{1,5},{2,6},{3,7},{4,0},{5,1},{6,2},{7,3},{8,12},{9,13},{10,... | collective-permute-start | bytes 98312 | tf_op jit(solution)/shard_map/ppermute | solution.py:24
  225.5 6.2 %collective-permute-start.55 = (f32[2,1,4096]{2,0,1:T(2,128)S(1)}, f32[2,1,4096]{2,0,1:T(2,128)S(1)}, u32[]{:S(2)}, u32[]{:S(2)}) collective-permute-start(f32[2,1,4096]{2,0,1:T(2,128)S(1)} %get-tuple-element.114), channel_id=1, source_target_pairs={{0,2},{1,3},{2,4},{3,5},{4,6},{5,7},{6,0},{7,1},{8,10},{9,11},{10,... | collective-permute-start | bytes 98312 | tf_op jit(solution)/shard_map/ppermute | solution.py:24
  242.2 5.0 collective-permute-start.60
  242.2 5.7 %collective-permute-start.59 = (f32[2,1,4096]{2,0,1:T(2,128)S(1)}, f32[2,1,4096]{2,0,1:T(2,128)S(1)}, u32[]{:S(2)}, u32[]{:S(2)}) collective-permute-start(f32[2,1,4096]{2,0,1:T(2,128)S(1)} %get-tuple-element.112), channel_id=1, source_target_pairs={{0,2},{1,3},{2,4},{3,5},{4,6},{5,7},{6,0},{7,1},{8,10},{9,11},{10,... | collective-permute-start | bytes 98312 | tf_op jit(solution)/shard_map/ppermute | solution.py:24
  257.6 4.8 collective-permute-start.64
  257.9 5.7 %collective-permute-start.63 = (f32[2,1,4096]{2,0,1:T(2,128)S(1)}, f32[2,1,4096]{2,0,1:T(2,128)S(1)}, u32[]{:S(2)}, u32[]{:S(2)}) collective-permute-start(f32[2,1,4096]{2,0,1:T(2,128)S(1)} %get-tuple-element.110), channel_id=1, source_target_pairs={{0,2},{1,3},{2,4},{3,5},{4,6},{5,7},{6,0},{7,1},{8,10},{9,11},{10,... | collective-permute-start | bytes 98312 | tf_op jit(solution)/shard_map/ppermute | solution.py:24
  273.8 5.2 collective-permute-start.68
  274.0 5.7 %collective-permute-start.67 = (f32[2,1,4096]{2,0,1:T(2,128)S(1)}, f32[2,1,4096]{2,0,1:T(2,128)S(1)}, u32[]{:S(2)}, u32[]{:S(2)}) collective-permute-start(f32[2,1,4096]{2,0,1:T(2,128)S(1)} %get-tuple-element.108), channel_id=1, source_target_pairs={{0,2},{1,3},{2,4},{3,5},{4,6},{5,7},{6,0},{7,1},{8,10},{9,11},{10,... | collective-permute-start | bytes 98312 | tf_op jit(solution)/shard_map/ppermute | solution.py:24
  293.2 4.8 collective-permute-start.74
  293.3 5.7 %collective-permute-start.73 = (f32[2,1,4096]{2,0,1:T(2,128)S(1)}, f32[2,1,4096]{2,0,1:T(2,128)S(1)}, u32[]{:S(2)}, u32[]{:S(2)}) collective-permute-start(f32[2,1,4096]{2,0,1:T(2,128)S(1)} %get-tuple-element.106), channel_id=1, source_target_pairs={{0,2},{1,3},{2,4},{3,5},{4,6},{5,7},{6,0},{7,1},{8,10},{9,11},{10,... | collective-permute-start | bytes 98312 | tf_op jit(solution)/shard_map/ppermute | solution.py:24
  309.3 5.1 collective-permute-start.78
  309.3 5.9 %collective-permute-start.77 = (f32[2,1,4096]{2,0,1:T(2,128)S(1)}, f32[2,1,4096]{2,0,1:T(2,128)S(1)}, u32[]{:S(2)}, u32[]{:S(2)}) collective-permute-start(f32[2,1,4096]{2,0,1:T(2,128)S(1)} %get-tuple-element.104), channel_id=1, source_target_pairs={{0,2},{1,3},{2,4},{3,5},{4,6},{5,7},{6,0},{7,1},{8,10},{9,11},{10,... | collective-permute-start | bytes 98312 | tf_op jit(solution)/shard_map/ppermute | solution.py:24
  325.1 4.8 collective-permute-start.82
  325.2 5.7 %collective-permute-start.81 = (f32[2,1,4096]{2,0,1:T(2,128)S(1)}, f32[2,1,4096]{2,0,1:T(2,128)S(1)}, u32[]{:S(2)}, u32[]{:S(2)}) collective-permute-start(f32[2,1,4096]{2,0,1:T(2,128)S(1)} %get-tuple-element.102), channel_id=1, source_target_pairs={{0,2},{1,3},{2,4},{3,5},{4,6},{5,7},{6,0},{7,1},{8,10},{9,11},{10,... | collective-permute-start | bytes 98312 | tf_op jit(solution)/shard_map/ppermute | solution.py:24
  341.1 5.3 collective-permute-start.86
  341.3 5.9 %collective-permute-start.85 = (f32[2,1,4096]{2,0,1:T(2,128)S(1)}, f32[2,1,4096]{2,0,1:T(2,128)S(1)}, u32[]{:S(2)}, u32[]{:S(2)}) collective-permute-start(f32[2,1,4096]{2,0,1:T(2,128)S(1)} %get-tuple-element.100), channel_id=1, source_target_pairs={{0,2},{1,3},{2,4},{3,5},{4,6},{5,7},{6,0},{7,1},{8,10},{9,11},{10,... | collective-permute-start | bytes 98312 | tf_op jit(solution)/shard_map/ppermute | solution.py:24
  356.8 4.8 collective-permute-start.90
  356.9 6.3 %collective-permute-start.89 = (f32[2,1,4096]{2,0,1:T(2,128)S(1)}, f32[2,1,4096]{2,0,1:T(2,128)S(1)}, u32[]{:S(2)}, u32[]{:S(2)}) collective-permute-start(f32[2,1,4096]{2,0,1:T(2,128)S(1)} %get-tuple-element.98), channel_id=1, source_target_pairs={{0,2},{1,3},{2,4},{3,5},{4,6},{5,7},{6,0},{7,1},{8,10},{9,11},{10,... | collective-permute-start | bytes 98312 | tf_op jit(solution)/shard_map/ppermute | solution.py:24
  373.6 5.0 collective-permute-start.94
  373.6 5.7 %collective-permute-start.93 = (f32[2,1,4096]{2,0,1:T(2,128)S(1)}, f32[2,1,4096]{2,0,1:T(2,128)S(1)}, u32[]{:S(2)}, u32[]{:S(2)}) collective-permute-start(f32[2,1,4096]{2,0,1:T(2,128)S(1)} %get-tuple-element.96), channel_id=1, source_target_pairs={{0,2},{1,3},{2,4},{3,5},{4,6},{5,7},{6,0},{7,1},{8,10},{9,11},{10,... | collective-permute-start | bytes 98312 | tf_op jit(solution)/shard_map/ppermute | solution.py:24
  389.1 4.8 collective-permute-start.98
  389.3 5.7 %collective-permute-start.97 = (f32[2,1,4096]{2,0,1:T(2,128)S(1)}, f32[2,1,4096]{2,0,1:T(2,128)S(1)}, u32[]{:S(2)}, u32[]{:S(2)}) collective-permute-start(f32[2,1,4096]{2,0,1:T(2,128)S(1)} %get-tuple-element.94), channel_id=1, source_target_pairs={{0,2},{1,3},{2,4},{3,5},{4,6},{5,7},{6,0},{7,1},{8,10},{9,11},{10,... | collective-permute-start | bytes 98312 | tf_op jit(solution)/shard_map/ppermute | solution.py:24
  405.2 5.2 collective-permute-start.102
  405.4 5.7 %collective-permute-start.101 = (f32[2,1,4096]{2,0,1:T(2,128)S(1)}, f32[2,1,4096]{2,0,1:T(2,128)S(1)}, u32[]{:S(2)}, u32[]{:S(2)}) collective-permute-start(f32[2,1,4096]{2,0,1:T(2,128)S(1)} %get-tuple-element.92), channel_id=1, source_target_pairs={{0,2},{1,3},{2,4},{3,5},{4,6},{5,7},{6,0},{7,1},{8,10},{9,11},{10,... | collective-permute-start | bytes 98312 | tf_op jit(solution)/shard_map/ppermute | solution.py:24
  425.9 5.7 %collective-permute-start.107 = (f32[2,1,4096]{2,0,1:T(2,128)S(1)}, f32[2,1,4096]{2,0,1:T(2,128)S(1)}, u32[]{:S(2)}, u32[]{:S(2)}) collective-permute-start(f32[2,1,4096]{2,0,1:T(2,128)S(1)} %get-tuple-element.90), channel_id=1, source_target_pairs={{0,2},{1,3},{2,4},{3,5},{4,6},{5,7},{6,0},{7,1},{8,10},{9,11},{10,... | collective-permute-start | bytes 98312 | tf_op jit(solution)/shard_map/ppermute | solution.py:24
  441.7 5.1 collective-permute-start.112
  441.7 5.7 %collective-permute-start.111 = (f32[2,1,4096]{2,0,1:T(2,128)S(1)}, f32[2,1,4096]{2,0,1:T(2,128)S(1)}, u32[]{:S(2)}, u32[]{:S(2)}) collective-permute-start(f32[2,1,4096]{2,0,1:T(2,128)S(1)} %get-tuple-element.88), channel_id=1, source_target_pairs={{0,2},{1,3},{2,4},{3,5},{4,6},{5,7},{6,0},{7,1},{8,10},{9,11},{10,... | collective-permute-start | bytes 98312 | tf_op jit(solution)/shard_map/ppermute | solution.py:24
  457.3 5.7 %collective-permute-start.115 = (f32[2,1,4096]{2,0,1:T(2,128)S(1)}, f32[2,1,4096]{2,0,1:T(2,128)S(1)}, u32[]{:S(2)}, u32[]{:S(2)}) collective-permute-start(f32[2,1,4096]{2,0,1:T(2,128)S(1)} %get-tuple-element.86), channel_id=1, source_target_pairs={{0,2},{1,3},{2,4},{3,5},{4,6},{5,7},{6,0},{7,1},{8,10},{9,11},{10,... | collective-permute-start | bytes 98312 | tf_op jit(solution)/shard_map/ppermute | solution.py:24
  473.1 5.3 collective-permute-start.120
  473.3 5.9 %collective-permute-start.119 = (f32[2,1,4096]{2,0,1:T(2,128)S(1)}, f32[2,1,4096]{2,0,1:T(2,128)S(1)}, u32[]{:S(2)}, u32[]{:S(2)}) collective-permute-start(f32[2,1,4096]{2,0,1:T(2,128)S(1)} %get-tuple-element.84), channel_id=1, source_target_pairs={{0,2},{1,3},{2,4},{3,5},{4,6},{5,7},{6,0},{7,1},{8,10},{9,11},{10,... | collective-permute-start | bytes 98312 | tf_op jit(solution)/shard_map/ppermute | solution.py:24
  488.6 4.9 collective-permute-start.124
  488.7 6.4 %collective-permute-start.123 = (f32[2,1,4096]{2,0,1:T(2,128)S(1)}, f32[2,1,4096]{2,0,1:T(2,128)S(1)}, u32[]{:S(2)}, u32[]{:S(2)}) collective-permute-start(f32[2,1,4096]{2,0,1:T(2,128)S(1)} %get-tuple-element.82), channel_id=1, source_target_pairs={{0,2},{1,3},{2,4},{3,5},{4,6},{5,7},{6,0},{7,1},{8,10},{9,11},{10,... | collective-permute-start | bytes 98312 | tf_op jit(solution)/shard_map/ppermute | solution.py:24
  505.3 5.1 collective-permute-start.128
  505.3 5.7 %collective-permute-start.127 = (f32[2,1,4096]{2,0,1:T(2,128)S(1)}, f32[2,1,4096]{2,0,1:T(2,128)S(1)}, u32[]{:S(2)}, u32[]{:S(2)}) collective-permute-start(f32[2,1,4096]{2,0,1:T(2,128)S(1)} %get-tuple-element.80), channel_id=1, source_target_pairs={{0,2},{1,3},{2,4},{3,5},{4,6},{5,7},{6,0},{7,1},{8,10},{9,11},{10,... | collective-permute-start | bytes 98312 | tf_op jit(solution)/shard_map/ppermute | solution.py:24
  520.9 5.7 %collective-permute-start.131 = (f32[2,1,4096]{2,0,1:T(2,128)S(1)}, f32[2,1,4096]{2,0,1:T(2,128)S(1)}, u32[]{:S(2)}, u32[]{:S(2)}) collective-permute-start(f32[2,1,4096]{2,0,1:T(2,128)S(1)} %get-tuple-element.78), channel_id=1, source_target_pairs={{0,2},{1,3},{2,4},{3,5},{4,6},{5,7},{6,0},{7,1},{8,10},{9,11},{10,... | collective-permute-start | bytes 98312 | tf_op jit(solution)/shard_map/ppermute | solution.py:24
  537.1 5.4 collective-permute-start.135
  (85 other events, 560.3 us)

commit v3 on v2

--- a/solution.py
+++ b/solution.py
@@ -67,7 +67,7 @@
         field = volt
         rhs = None
         for sweep in range(SWEEPS):
-            whole = collect(field)
+            whole = collect(field.reshape(-1, 128))
             if rhs is None:
                 if step > 0:
                     end_volt = whole.reshape(-1)[end_index][None]

time: 558 us -> 551 us (0.987)
  transfers between devices with their start and end apart: 140 -> 140, of which waited for: 134 -> 132; matrix products, arithmetic and copies ran while one was open for 4% -> 4% of each run, Pallas kernels for 0% -> 0%
where the time goes in v3:
time: 551 us; the launch traced here: 541 us
  waiting for transfers between devices  241 us (44%)
  other arithmetic  128 us (23%)
  starting transfers between devices  127 us (23%)
  local copies, waits for them, and re-layouts  42 us (8%)
    ppermute x99, waiting for transfers between devices, collect(): parts.append(lax.ppermute(pair, 'sub', moves))  133 us
    ppermute x33, waiting for transfers between devices, collect(): partner = lax.ppermute(value, 'sub', [(i, i ^ 1) for i in range(count)])  104 us
    ppermute x99, starting transfers between devices, collect(): parts.append(lax.ppermute(pair, 'sub', moves))  101 us
    reduce_sum x32, other arithmetic, apply_blocks(): result = jnp.sum(blocks[0] * picked[:, None, :], axis=2)  89.8 us
    gather x32, local copies, waits for them, and re-layouts, on_device(): others = whole.reshape(-1, width)[remote_cols]  24.2 us
    add x32, other arithmetic, on_device(): field = field + (rhs - result - capacity * field) / system_diag  22.3 us
    ppermute x33, starting transfers between devices, collect(): partner = lax.ppermute(value, 'sub', [(i, i ^ 1) for i in range(count)])  20.8 us
  transfers between devices with their start and end apart: 140, of which 132 were waited for; matrix products, arithmetic and copies ran while one was open for 4% of the time, Pallas kernels for 0%

profile of v3, /device:TPU:0, one launch (start us, length us, event | category | flops | bytes accessed | tf_op | source)
XLA Modules:
  0.0 540.8 jit_solution(911303856882971890)
XLA Ops:
  0.6 3.1 collective-permute-start
  11.2 3.6 collective-permute-start.3
  21.5 2.8 fusion
  25.7 3.2 collective-permute-done.4
  36.8 2.8 fusion.1
  41.0 3.2 collective-permute-done.8
  52.6 2.8 fusion.2
  56.8 3.2 collective-permute-done.12
  67.8 2.8 fusion.3
  72.0 3.2 collective-permute-done.16
  79.2 2.9 collective-permute-done.18
  83.8 2.8 fusion.4
  88.0 3.2 collective-permute-done.20
  99.3 2.8 fusion.5
  103.4 3.2 collective-permute-done.24
  114.9 2.8 fusion.6
  119.1 3.2 collective-permute-done.28
  130.9 2.8 fusion.7
  135.1 3.2 collective-permute-done.32
  149.7 2.8 fusion.8
  155.4 3.3 collective-permute-done.38
  166.9 2.8 fusion.9
  171.1 3.2 collective-permute-done.42
  182.6 2.8 fusion.10
  186.8 3.3 collective-permute-done.46
  198.2 2.8 fusion.11
  202.4 3.2 collective-permute-done.50
  213.9 2.8 fusion.12
  218.1 3.3 collective-permute-done.54
  225.5 3.5 collective-permute-done.56
  230.1 2.8 fusion.13
  234.3 3.2 collective-permute-done.58
  245.9 2.8 fusion.14
  250.1 3.3 collective-permute-done.62
  261.5 2.8 fusion.15
  265.7 3.2 collective-permute-done.66
  285.3 3.2 collective-permute-done.72
  296.7 2.8 fusion.17
  300.8 3.3 collective-permute-done.76
  312.3 2.8 fusion.18
  316.4 3.2 collective-permute-done.80
  327.9 2.8 fusion.19
  332.1 3.3 collective-permute-done.84
  343.7 2.8 fusion.20
  347.9 3.3 collective-permute-done.88
  355.2 3.5 collective-permute-done.90
  359.8 2.8 fusion.21
  364.0 3.3 collective-permute-done.92
  379.7 3.3 collective-permute-done.96
  391.0 2.8 fusion.23
  395.2 3.3 collective-permute-done.100
  415.8 3.3 collective-permute-done.106
  426.9 2.8 fusion.25
  431.1 3.2 collective-permute-done.110
  446.7 3.3 collective-permute-done.114
  462.0 3.3 collective-permute-done.118
  469.2 2.8 collective-permute-done.120
  474.1 2.8 fusion.28
  478.3 3.2 collective-permute-done.122
  485.5 3.2 collective-permute-done.124
  494.0 3.2 collective-permute-done.126
  509.4 3.2 collective-permute-done.130
  520.7 2.8 fusion.31
  525.5 3.1 collective-permute-done.134
  (613 shorter events, 341.5 us)
Async XLA Ops:
  0.6 9.8 %collective-permute-start = (f32[32,128]{1,0:T(8,128)}, f32[32,128]{1,0:T(8,128)S(1)}, u32[]{:S(2)}, u32[]{:S(2)}) collective-permute-start(f32[32,128]{1,0:T(8,128)} %bitcast.659), channel_id=1, source_target_pairs={{0,1},{1,0},{2,3},{3,2},{4,5},{5,4},{6,7},{7,6},{8,9},{9,8},{10,11... | collective-permute-start | bytes 49160 | tf_op jit(solution)/shard_map/ppermute | solution.py:19
  11.2 6.3 %collective-permute-start.3 = (f32[2,32,128]{2,1,0:T(8,128)S(1)}, f32[2,32,128]{2,1,0:T(8,128)S(1)}, u32[]{:S(2)}, u32[]{:S(2)}) collective-permute-start(f32[2,32,128]{2,1,0:T(8,128)S(1)} %get-tuple-element.140), channel_id=1, source_target_pairs={{0,6},{1,7},{2,0},{3,1},{4,2},{5,3},{6,4},{7,5},{8,14},{9,15},{10,... | collective-permute-start | bytes 98312 | tf_op jit(solution)/shard_map/ppermute | solution.py:24
  14.8 4.8 collective-permute-start.2
  14.8 5.7 %collective-permute-start.1 = (f32[2,32,128]{2,1,0:T(8,128)S(1)}, f32[2,32,128]{2,1,0:T(8,128)S(1)}, u32[]{:S(2)}, u32[]{:S(2)}) collective-permute-start(f32[2,32,128]{2,1,0:T(8,128)S(1)} %get-tuple-element.140), channel_id=1, source_target_pairs={{0,2},{1,3},{2,4},{3,5},{4,6},{5,7},{6,0},{7,1},{8,10},{9,11},{10,... | collective-permute-start | bytes 98312 | tf_op jit(solution)/shard_map/ppermute | solution.py:24
  29.5 4.8 collective-permute-start.6
  30.2 5.7 %collective-permute-start.5 = (f32[2,32,128]{2,1,0:T(8,128)S(1)}, f32[2,32,128]{2,1,0:T(8,128)S(1)}, u32[]{:S(2)}, u32[]{:S(2)}) collective-permute-start(f32[2,32,128]{2,1,0:T(8,128)S(1)} %get-tuple-element.138), channel_id=1, source_target_pairs={{0,2},{1,3},{2,4},{3,5},{4,6},{5,7},{6,0},{7,1},{8,10},{9,11},{10,... | collective-permute-start | bytes 98312 | tf_op jit(solution)/shard_map/ppermute | solution.py:24
  45.7 5.2 collective-permute-start.10
  45.9 5.7 %collective-permute-start.9 = (f32[2,32,128]{2,1,0:T(8,128)S(1)}, f32[2,32,128]{2,1,0:T(8,128)S(1)}, u32[]{:S(2)}, u32[]{:S(2)}) collective-permute-start(f32[2,32,128]{2,1,0:T(8,128)S(1)} %get-tuple-element.136), channel_id=1, source_target_pairs={{0,2},{1,3},{2,4},{3,5},{4,6},{5,7},{6,0},{7,1},{8,10},{9,11},{10,... | collective-permute-start | bytes 98312 | tf_op jit(solution)/shard_map/ppermute | solution.py:24
  61.0 4.8 collective-permute-start.14
  61.1 5.7 %collective-permute-start.13 = (f32[2,32,128]{2,1,0:T(8,128)S(1)}, f32[2,32,128]{2,1,0:T(8,128)S(1)}, u32[]{:S(2)}, u32[]{:S(2)}) collective-permute-start(f32[2,32,128]{2,1,0:T(8,128)S(1)} %get-tuple-element.134), channel_id=1, source_target_pairs={{0,2},{1,3},{2,4},{3,5},{4,6},{5,7},{6,0},{7,1},{8,10},{9,11},{10,... | collective-permute-start | bytes 98312 | tf_op jit(solution)/shard_map/ppermute | solution.py:24
  76.8 5.3 collective-permute-start.18
  76.8 6.0 %collective-permute-start.17 = (f32[2,32,128]{2,1,0:T(8,128)S(1)}, f32[2,32,128]{2,1,0:T(8,128)S(1)}, u32[]{:S(2)}, u32[]{:S(2)}) collective-permute-start(f32[2,32,128]{2,1,0:T(8,128)S(1)} %get-tuple-element.132), channel_id=1, source_target_pairs={{0,2},{1,3},{2,4},{3,5},{4,6},{5,7},{6,0},{7,1},{8,10},{9,11},{10,... | collective-permute-start | bytes 98312 | tf_op jit(solution)/shard_map/ppermute | solution.py:24
  92.6 5.2 collective-permute-start.22
  92.6 5.7 %collective-permute-start.21 = (f32[2,32,128]{2,1,0:T(8,128)S(1)}, f32[2,32,128]{2,1,0:T(8,128)S(1)}, u32[]{:S(2)}, u32[]{:S(2)}) collective-permute-start(f32[2,32,128]{2,1,0:T(8,128)S(1)} %get-tuple-element.130), channel_id=1, source_target_pairs={{0,2},{1,3},{2,4},{3,5},{4,6},{5,7},{6,0},{7,1},{8,10},{9,11},{10,... | collective-permute-start | bytes 98312 | tf_op jit(solution)/shard_map/ppermute | solution.py:24
  107.9 5.2 collective-permute-start.26
  108.2 5.7 %collective-permute-start.25 = (f32[2,32,128]{2,1,0:T(8,128)S(1)}, f32[2,32,128]{2,1,0:T(8,128)S(1)}, u32[]{:S(2)}, u32[]{:S(2)}) collective-permute-start(f32[2,32,128]{2,1,0:T(8,128)S(1)} %get-tuple-element.128), channel_id=1, source_target_pairs={{0,2},{1,3},{2,4},{3,5},{4,6},{5,7},{6,0},{7,1},{8,10},{9,11},{10,... | collective-permute-start | bytes 98312 | tf_op jit(solution)/shard_map/ppermute | solution.py:24
  123.5 4.8 collective-permute-start.30
  123.7 6.2 %collective-permute-start.29 = (f32[2,32,128]{2,1,0:T(8,128)S(1)}, f32[2,32,128]{2,1,0:T(8,128)S(1)}, u32[]{:S(2)}, u32[]{:S(2)}) collective-permute-start(f32[2,32,128]{2,1,0:T(8,128)S(1)} %get-tuple-element.126), channel_id=1, source_target_pairs={{0,2},{1,3},{2,4},{3,5},{4,6},{5,7},{6,0},{7,1},{8,10},{9,11},{10,... | collective-permute-start | bytes 98312 | tf_op jit(solution)/shard_map/ppermute | solution.py:24
  139.6 5.2 collective-permute-start.34
  139.6 5.7 %collective-permute-start.33 = (f32[2,32,128]{2,1,0:T(8,128)S(1)}, f32[2,32,128]{2,1,0:T(8,128)S(1)}, u32[]{:S(2)}, u32[]{:S(2)}) collective-permute-start(f32[2,32,128]{2,1,0:T(8,128)S(1)} %get-tuple-element.124), channel_id=1, source_target_pairs={{0,2},{1,3},{2,4},{3,5},{4,6},{5,7},{6,0},{7,1},{8,10},{9,11},{10,... | collective-permute-start | bytes 98312 | tf_op jit(solution)/shard_map/ppermute | solution.py:24
  160.0 5.2 collective-permute-start.40
  160.1 5.7 %collective-permute-start.39 = (f32[2,32,128]{2,1,0:T(8,128)S(1)}, f32[2,32,128]{2,1,0:T(8,128)S(1)}, u32[]{:S(2)}, u32[]{:S(2)}) collective-permute-start(f32[2,32,128]{2,1,0:T(8,128)S(1)} %get-tuple-element.122), channel_id=1, source_target_pairs={{0,2},{1,3},{2,4},{3,5},{4,6},{5,7},{6,0},{7,1},{8,10},{9,11},{10,... | collective-permute-start | bytes 98312 | tf_op jit(solution)/shard_map/ppermute | solution.py:24
  175.5 4.8 collective-permute-start.44
  175.8 5.7 %collective-permute-start.43 = (f32[2,32,128]{2,1,0:T(8,128)S(1)}, f32[2,32,128]{2,1,0:T(8,128)S(1)}, u32[]{:S(2)}, u32[]{:S(2)}) collective-permute-start(f32[2,32,128]{2,1,0:T(8,128)S(1)} %get-tuple-element.120), channel_id=1, source_target_pairs={{0,2},{1,3},{2,4},{3,5},{4,6},{5,7},{6,0},{7,1},{8,10},{9,11},{10,... | collective-permute-start | bytes 98312 | tf_op jit(solution)/shard_map/ppermute | solution.py:24
  191.2 4.8 collective-permute-start.48
  191.3 5.7 %collective-permute-start.47 = (f32[2,32,128]{2,1,0:T(8,128)S(1)}, f32[2,32,128]{2,1,0:T(8,128)S(1)}, u32[]{:S(2)}, u32[]{:S(2)}) collective-permute-start(f32[2,32,128]{2,1,0:T(8,128)S(1)} %get-tuple-element.118), channel_id=1, source_target_pairs={{0,2},{1,3},{2,4},{3,5},{4,6},{5,7},{6,0},{7,1},{8,10},{9,11},{10,... | collective-permute-start | bytes 98312 | tf_op jit(solution)/shard_map/ppermute | solution.py:24
  206.9 5.3 collective-permute-start.52
  207.0 5.8 %collective-permute-start.51 = (f32[2,32,128]{2,1,0:T(8,128)S(1)}, f32[2,32,128]{2,1,0:T(8,128)S(1)}, u32[]{:S(2)}, u32[]{:S(2)}) collective-permute-start(f32[2,32,128]{2,1,0:T(8,128)S(1)} %get-tuple-element.116), channel_id=1, source_target_pairs={{0,2},{1,3},{2,4},{3,5},{4,6},{5,7},{6,0},{7,1},{8,10},{9,11},{10,... | collective-permute-start | bytes 98312 | tf_op jit(solution)/shard_map/ppermute | solution.py:24
  222.5 6.5 %collective-permute-start.56 = (f32[2,32,128]{2,1,0:T(8,128)S(1)}, f32[2,32,128]{2,1,0:T(8,128)S(1)}, u32[]{:S(2)}, u32[]{:S(2)}) collective-permute-start(f32[2,32,128]{2,1,0:T(8,128)S(1)} %get-tuple-element.114), channel_id=1, source_target_pairs={{0,4},{1,5},{2,6},{3,7},{4,0},{5,1},{6,2},{7,3},{8,12},{9,13},{10,... | collective-permute-start | bytes 98312 | tf_op jit(solution)/shard_map/ppermute | solution.py:24
  222.6 6.4 %collective-permute-start.55 = (f32[2,32,128]{2,1,0:T(8,128)S(1)}, f32[2,32,128]{2,1,0:T(8,128)S(1)}, u32[]{:S(2)}, u32[]{:S(2)}) collective-permute-start(f32[2,32,128]{2,1,0:T(8,128)S(1)} %get-tuple-element.114), channel_id=1, source_target_pairs={{0,2},{1,3},{2,4},{3,5},{4,6},{5,7},{6,0},{7,1},{8,10},{9,11},{10,... | collective-permute-start | bytes 98312 | tf_op jit(solution)/shard_map/ppermute | solution.py:24
  238.9 5.2 collective-permute-start.60
  238.9 5.9 %collective-permute-start.59 = (f32[2,32,128]{2,1,0:T(8,128)S(1)}, f32[2,32,128]{2,1,0:T(8,128)S(1)}, u32[]{:S(2)}, u32[]{:S(2)}) collective-permute-start(f32[2,32,128]{2,1,0:T(8,128)S(1)} %get-tuple-element.112), channel_id=1, source_target_pairs={{0,2},{1,3},{2,4},{3,5},{4,6},{5,7},{6,0},{7,1},{8,10},{9,11},{10,... | collective-permute-start | bytes 98312 | tf_op jit(solution)/shard_map/ppermute | solution.py:24
  254.6 5.2 collective-permute-start.64
  254.7 5.7 %collective-permute-start.63 = (f32[2,32,128]{2,1,0:T(8,128)S(1)}, f32[2,32,128]{2,1,0:T(8,128)S(1)}, u32[]{:S(2)}, u32[]{:S(2)}) collective-permute-start(f32[2,32,128]{2,1,0:T(8,128)S(1)} %get-tuple-element.110), channel_id=1, source_target_pairs={{0,2},{1,3},{2,4},{3,5},{4,6},{5,7},{6,0},{7,1},{8,10},{9,11},{10,... | collective-permute-start | bytes 98312 | tf_op jit(solution)/shard_map/ppermute | solution.py:24
  270.3 5.2 collective-permute-start.68
  270.5 5.7 %collective-permute-start.67 = (f32[2,32,128]{2,1,0:T(8,128)S(1)}, f32[2,32,128]{2,1,0:T(8,128)S(1)}, u32[]{:S(2)}, u32[]{:S(2)}) collective-permute-start(f32[2,32,128]{2,1,0:T(8,128)S(1)} %get-tuple-element.108), channel_id=1, source_target_pairs={{0,2},{1,3},{2,4},{3,5},{4,6},{5,7},{6,0},{7,1},{8,10},{9,11},{10,... | collective-permute-start | bytes 98312 | tf_op jit(solution)/shard_map/ppermute | solution.py:24
  289.8 5.7 %collective-permute-start.73 = (f32[2,32,128]{2,1,0:T(8,128)S(1)}, f32[2,32,128]{2,1,0:T(8,128)S(1)}, u32[]{:S(2)}, u32[]{:S(2)}) collective-permute-start(f32[2,32,128]{2,1,0:T(8,128)S(1)} %get-tuple-element.106), channel_id=1, source_target_pairs={{0,2},{1,3},{2,4},{3,5},{4,6},{5,7},{6,0},{7,1},{8,10},{9,11},{10,... | collective-permute-start | bytes 98312 | tf_op jit(solution)/shard_map/ppermute | solution.py:24
  305.4 5.2 collective-permute-start.78
  305.4 5.7 %collective-permute-start.77 = (f32[2,32,128]{2,1,0:T(8,128)S(1)}, f32[2,32,128]{2,1,0:T(8,128)S(1)}, u32[]{:S(2)}, u32[]{:S(2)}) collective-permute-start(f32[2,32,128]{2,1,0:T(8,128)S(1)} %get-tuple-element.104), channel_id=1, source_target_pairs={{0,2},{1,3},{2,4},{3,5},{4,6},{5,7},{6,0},{7,1},{8,10},{9,11},{10,... | collective-permute-start | bytes 98312 | tf_op jit(solution)/shard_map/ppermute | solution.py:24
  321.0 5.2 collective-permute-start.82
  321.1 5.7 %collective-permute-start.81 = (f32[2,32,128]{2,1,0:T(8,128)S(1)}, f32[2,32,128]{2,1,0:T(8,128)S(1)}, u32[]{:S(2)}, u32[]{:S(2)}) collective-permute-start(f32[2,32,128]{2,1,0:T(8,128)S(1)} %get-tuple-element.102), channel_id=1, source_target_pairs={{0,2},{1,3},{2,4},{3,5},{4,6},{5,7},{6,0},{7,1},{8,10},{9,11},{10,... | collective-permute-start | bytes 98312 | tf_op jit(solution)/shard_map/ppermute | solution.py:24
  336.6 4.8 collective-permute-start.86
  336.8 5.8 %collective-permute-start.85 = (f32[2,32,128]{2,1,0:T(8,128)S(1)}, f32[2,32,128]{2,1,0:T(8,128)S(1)}, u32[]{:S(2)}, u32[]{:S(2)}) collective-permute-start(f32[2,32,128]{2,1,0:T(8,128)S(1)} %get-tuple-element.100), channel_id=1, source_target_pairs={{0,2},{1,3},{2,4},{3,5},{4,6},{5,7},{6,0},{7,1},{8,10},{9,11},{10,... | collective-permute-start | bytes 98312 | tf_op jit(solution)/shard_map/ppermute | solution.py:24
  352.2 6.4 %collective-permute-start.90 = (f32[2,32,128]{2,1,0:T(8,128)S(1)}, f32[2,32,128]{2,1,0:T(8,128)S(1)}, u32[]{:S(2)}, u32[]{:S(2)}) collective-permute-start(f32[2,32,128]{2,1,0:T(8,128)S(1)} %get-tuple-element.98), channel_id=1, source_target_pairs={{0,4},{1,5},{2,6},{3,7},{4,0},{5,1},{6,2},{7,3},{8,12},{9,13},{10,... | collective-permute-start | bytes 98312 | tf_op jit(solution)/shard_map/ppermute | solution.py:24
  352.3 6.3 %collective-permute-start.89 = (f32[2,32,128]{2,1,0:T(8,128)S(1)}, f32[2,32,128]{2,1,0:T(8,128)S(1)}, u32[]{:S(2)}, u32[]{:S(2)}) collective-permute-start(f32[2,32,128]{2,1,0:T(8,128)S(1)} %get-tuple-element.98), channel_id=1, source_target_pairs={{0,2},{1,3},{2,4},{3,5},{4,6},{5,7},{6,0},{7,1},{8,10},{9,11},{10,... | collective-permute-start | bytes 98312 | tf_op jit(solution)/shard_map/ppermute | solution.py:24
  368.7 5.1 collective-permute-start.94
  368.7 5.7 %collective-permute-start.93 = (f32[2,32,128]{2,1,0:T(8,128)S(1)}, f32[2,32,128]{2,1,0:T(8,128)S(1)}, u32[]{:S(2)}, u32[]{:S(2)}) collective-permute-start(f32[2,32,128]{2,1,0:T(8,128)S(1)} %get-tuple-element.96), channel_id=1, source_target_pairs={{0,2},{1,3},{2,4},{3,5},{4,6},{5,7},{6,0},{7,1},{8,10},{9,11},{10,... | collective-permute-start | bytes 98312 | tf_op jit(solution)/shard_map/ppermute | solution.py:24
  384.2 5.7 %collective-permute-start.97 = (f32[2,32,128]{2,1,0:T(8,128)S(1)}, f32[2,32,128]{2,1,0:T(8,128)S(1)}, u32[]{:S(2)}, u32[]{:S(2)}) collective-permute-start(f32[2,32,128]{2,1,0:T(8,128)S(1)} %get-tuple-element.94), channel_id=1, source_target_pairs={{0,2},{1,3},{2,4},{3,5},{4,6},{5,7},{6,0},{7,1},{8,10},{9,11},{10,... | collective-permute-start | bytes 98312 | tf_op jit(solution)/shard_map/ppermute | solution.py:24
  399.8 5.2 collective-permute-start.102
  400.1 5.7 %collective-permute-start.101 = (f32[2,32,128]{2,1,0:T(8,128)S(1)}, f32[2,32,128]{2,1,0:T(8,128)S(1)}, u32[]{:S(2)}, u32[]{:S(2)}) collective-permute-start(f32[2,32,128]{2,1,0:T(8,128)S(1)} %get-tuple-element.92), channel_id=1, source_target_pairs={{0,2},{1,3},{2,4},{3,5},{4,6},{5,7},{6,0},{7,1},{8,10},{9,11},{10,... | collective-permute-start | bytes 98312 | tf_op jit(solution)/shard_map/ppermute | solution.py:24
  420.1 4.8 collective-permute-start.108
  420.2 5.7 %collective-permute-start.107 = (f32[2,32,128]{2,1,0:T(8,128)S(1)}, f32[2,32,128]{2,1,0:T(8,128)S(1)}, u32[]{:S(2)}, u32[]{:S(2)}) collective-permute-start(f32[2,32,128]{2,1,0:T(8,128)S(1)} %get-tuple-element.90), channel_id=1, source_target_pairs={{0,2},{1,3},{2,4},{3,5},{4,6},{5,7},{6,0},{7,1},{8,10},{9,11},{10,... | collective-permute-start | bytes 98312 | tf_op jit(solution)/shard_map/ppermute | solution.py:24
  435.8 5.1 collective-permute-start.112
  435.8 5.7 %collective-permute-start.111 = (f32[2,32,128]{2,1,0:T(8,128)S(1)}, f32[2,32,128]{2,1,0:T(8,128)S(1)}, u32[]{:S(2)}, u32[]{:S(2)}) collective-permute-start(f32[2,32,128]{2,1,0:T(8,128)S(1)} %get-tuple-element.88), channel_id=1, source_target_pairs={{0,2},{1,3},{2,4},{3,5},{4,6},{5,7},{6,0},{7,1},{8,10},{9,11},{10,... | collective-permute-start | bytes 98312 | tf_op jit(solution)/shard_map/ppermute | solution.py:24
  451.2 5.7 %collective-permute-start.115 = (f32[2,32,128]{2,1,0:T(8,128)S(1)}, f32[2,32,128]{2,1,0:T(8,128)S(1)}, u32[]{:S(2)}, u32[]{:S(2)}) collective-permute-start(f32[2,32,128]{2,1,0:T(8,128)S(1)} %get-tuple-element.86), channel_id=1, source_target_pairs={{0,2},{1,3},{2,4},{3,5},{4,6},{5,7},{6,0},{7,1},{8,10},{9,11},{10,... | collective-permute-start | bytes 98312 | tf_op jit(solution)/shard_map/ppermute | solution.py:24
  466.7 5.3 collective-permute-start.120
  466.9 6.2 %collective-permute-start.119 = (f32[2,32,128]{2,1,0:T(8,128)S(1)}, f32[2,32,128]{2,1,0:T(8,128)S(1)}, u32[]{:S(2)}, u32[]{:S(2)}) collective-permute-start(f32[2,32,128]{2,1,0:T(8,128)S(1)} %get-tuple-element.84), channel_id=1, source_target_pairs={{0,2},{1,3},{2,4},{3,5},{4,6},{5,7},{6,0},{7,1},{8,10},{9,11},{10,... | collective-permute-start | bytes 98312 | tf_op jit(solution)/shard_map/ppermute | solution.py:24
  482.3 6.5 %collective-permute-start.124 = (f32[2,32,128]{2,1,0:T(8,128)S(1)}, f32[2,32,128]{2,1,0:T(8,128)S(1)}, u32[]{:S(2)}, u32[]{:S(2)}) collective-permute-start(f32[2,32,128]{2,1,0:T(8,128)S(1)} %get-tuple-element.82), channel_id=1, source_target_pairs={{0,4},{1,5},{2,6},{3,7},{4,0},{5,1},{6,2},{7,3},{8,12},{9,13},{10,... | collective-permute-start | bytes 98312 | tf_op jit(solution)/shard_map/ppermute | solution.py:24
  482.4 6.4 %collective-permute-start.123 = (f32[2,32,128]{2,1,0:T(8,128)S(1)}, f32[2,32,128]{2,1,0:T(8,128)S(1)}, u32[]{:S(2)}, u32[]{:S(2)}) collective-permute-start(f32[2,32,128]{2,1,0:T(8,128)S(1)} %get-tuple-element.82), channel_id=1, source_target_pairs={{0,2},{1,3},{2,4},{3,5},{4,6},{5,7},{6,0},{7,1},{8,10},{9,11},{10,... | collective-permute-start | bytes 98312 | tf_op jit(solution)/shard_map/ppermute | solution.py:24
  498.5 5.2 collective-permute-start.128
  498.5 5.7 %collective-permute-start.127 = (f32[2,32,128]{2,1,0:T(8,128)S(1)}, f32[2,32,128]{2,1,0:T(8,128)S(1)}, u32[]{:S(2)}, u32[]{:S(2)}) collective-permute-start(f32[2,32,128]{2,1,0:T(8,128)S(1)} %get-tuple-element.80), channel_id=1, source_target_pairs={{0,2},{1,3},{2,4},{3,5},{4,6},{5,7},{6,0},{7,1},{8,10},{9,11},{10,... | collective-permute-start | bytes 98312 | tf_op jit(solution)/shard_map/ppermute | solution.py:24
  513.9 5.2 collective-permute-start.132
  514.0 5.7 %collective-permute-start.131 = (f32[2,32,128]{2,1,0:T(8,128)S(1)}, f32[2,32,128]{2,1,0:T(8,128)S(1)}, u32[]{:S(2)}, u32[]{:S(2)}) collective-permute-start(f32[2,32,128]{2,1,0:T(8,128)S(1)} %get-tuple-element.78), channel_id=1, source_target_pairs={{0,2},{1,3},{2,4},{3,5},{4,6},{5,7},{6,0},{7,1},{8,10},{9,11},{10,... | collective-permute-start | bytes 98312 | tf_op jit(solution)/shard_map/ppermute | solution.py:24
  530.0 5.4 collective-permute-start.135
  (85 other events, 570.0 us)

commit v4 on v3

--- a/solution.py
+++ b/solution.py
@@ -61,6 +61,8 @@
     local_ends = line_ends - offset
     inside = (local_ends >= 0) & (local_ends < local_count)
     safe_ends = jnp.clip(local_ends, 0, local_count - 1)
+    buses = jnp.arange(local_count)[None, :]
+    at_bus = (safe_ends.reshape(-1, 1) == buses) & inside.reshape(-1, 1)
     volt = start_volt
     hist = start_hist
     for step in range(STEPS):
@@ -73,8 +75,8 @@
                     end_volt = whole.reshape(-1)[end_index][None]
                     hist = next_hist(end_volt, hist, surge)
                 rhs = sources[step] + capacity * volt
-                inject = jnp.where(inside, -hist, 0.0)
-                rhs = rhs.at[0, safe_ends.reshape(-1)].add(inject.reshape(-1))
+                inject = jnp.where(at_bus, -hist.reshape(-1, 1), 0.0)
+                rhs = rhs + jnp.sum(inject, axis=0, keepdims=True)
             own_part = field.reshape(rows_here, width)
             others = whole.reshape(-1, width)[remote_cols]
             others = others.reshape(rows_here, -1)

time: 551 us -> 549 us (level)
  starting transfers between devices: 127 us -> 158 us
  waiting for transfers between devices: 241 us -> 211 us
    ppermute x99, starting transfers between devices: 101 us -> 132 us  [collect(): parts.append(lax.ppermute(pair, 'sub', moves))]
    ppermute x99, waiting for transfers between devices: 133 us -> 103 us  [collect(): parts.append(lax.ppermute(pair, 'sub', moves))]
    scatter-add x4 -> x0, other arithmetic: 5.74 us -> none  [on_device(): rhs = rhs.at[0, safe_ends.reshape(-1)].add(inject.reshape(-1))]
  transfers between devices with their start and end apart: 140 -> 140, of which waited for: 132 -> 136; matrix products, arithmetic and copies ran while one was open for 4% -> 4% of each run, Pallas kernels for 0% -> 0%
where the time goes in v4:
time: 549 us; the launch traced here: 539 us
  waiting for transfers between devices  211 us (38%)
  starting transfers between devices  158 us (29%)
  other arithmetic  125 us (23%)
  local copies, waits for them, and re-layouts  41.9 us (8%)
    ppermute x99, starting transfers between devices, collect(): parts.append(lax.ppermute(pair, 'sub', moves))  132 us
    ppermute x33, waiting for transfers between devices, collect(): partner = lax.ppermute(value, 'sub', [(i, i ^ 1) for i in range(count)])  103 us
    ppermute x99, waiting for transfers between devices, collect(): parts.append(lax.ppermute(pair, 'sub', moves))  103 us
    reduce_sum x32, other arithmetic, apply_blocks(): result = jnp.sum(blocks[0] * picked[:, None, :], axis=2)  89.8 us
    gather x32, local copies, waits for them, and re-layouts, on_device(): others = whole.reshape(-1, width)[remote_cols]  24.1 us
    add x32, other arithmetic, on_device(): field = field + (rhs - result - capacity * field) / system_diag  22.4 us
    ppermute x33, starting transfers between devices, collect(): partner = lax.ppermute(value, 'sub', [(i, i ^ 1) for i in range(count)])  21.1 us
  transfers between devices with their start and end apart: 140, of which 136 were waited for; matrix products, arithmetic and copies ran while one was open for 4% of the time, Pallas kernels for 0%

profile of v4, /device:TPU:0, one launch (start us, length us, event | category | flops | bytes accessed | tf_op | source)
XLA Modules:
  0.0 538.8 jit_solution(1425791839209409113)
XLA Ops:
  0.6 3.1 collective-permute-start
  21.6 2.8 fusion
  25.9 3.2 collective-permute-done.4
  29.4 3.5 collective-permute-start.6
  37.8 2.8 fusion.1
  41.9 3.2 collective-permute-done.8
  52.9 2.8 fusion.2
  57.1 3.2 collective-permute-done.12
  68.9 2.8 fusion.3
  73.1 3.2 collective-permute-done.16
  85.1 2.8 fusion.4
  89.3 3.2 collective-permute-done.20
  100.6 2.8 fusion.5
  104.8 3.2 collective-permute-done.24
  116.3 2.8 fusion.6
  120.5 3.2 collective-permute-done.28
  132.5 2.8 fusion.7
  136.8 3.2 collective-permute-done.32
  151.5 2.8 fusion.8
  156.4 3.2 collective-permute-done.38
  167.6 2.8 fusion.9
  171.8 3.2 collective-permute-done.42
  183.2 2.8 fusion.10
  187.4 3.2 collective-permute-done.46
  198.8 2.8 fusion.11
  203.0 3.2 collective-permute-done.50
  214.6 2.8 fusion.12
  218.8 3.2 collective-permute-done.54
  230.9 2.8 fusion.13
  235.1 3.2 collective-permute-done.58
  246.7 2.8 fusion.14
  250.9 3.2 collective-permute-done.62
  262.2 2.8 fusion.15
  266.4 3.2 collective-permute-done.66
  285.0 3.2 collective-permute-done.72
  296.4 2.8 fusion.17
  300.6 3.2 collective-permute-done.76
  311.9 2.8 fusion.18
  316.1 3.2 collective-permute-done.80
  327.3 2.8 fusion.19
  331.5 3.2 collective-permute-done.84
  342.9 2.8 fusion.20
  347.1 3.2 collective-permute-done.88
  359.2 2.8 fusion.21
  363.3 3.2 collective-permute-done.92
  374.5 2.8 fusion.22
  378.7 3.2 collective-permute-done.96
  390.0 2.8 fusion.23
  394.2 3.2 collective-permute-done.100
  413.7 3.2 collective-permute-done.106
  425.2 2.8 fusion.25
  429.4 3.3 collective-permute-done.110
  440.5 2.8 fusion.26
  444.7 3.2 collective-permute-done.114
  456.0 2.8 fusion.27
  460.2 3.3 collective-permute-done.118
  471.7 2.8 fusion.28
  475.9 3.2 collective-permute-done.122
  487.9 2.8 fusion.29
  492.1 3.2 collective-permute-done.126
  503.4 2.8 fusion.30
  507.6 3.2 collective-permute-done.130
  518.8 2.8 fusion.31
  523.5 3.1 collective-permute-done.134
  (613 shorter events, 342.0 us)
Async XLA Ops:
  0.6 11.2 %collective-permute-start = (f32[32,128]{1,0:T(8,128)}, f32[32,128]{1,0:T(8,128)S(1)}, u32[]{:S(2)}, u32[]{:S(2)}) collective-permute-start(f32[32,128]{1,0:T(8,128)} %bitcast.631), channel_id=1, source_target_pairs={{0,1},{1,0},{2,3},{3,2},{4,5},{5,4},{6,7},{7,6},{8,9},{9,8},{10,11... | collective-permute-start | bytes 49160 | tf_op jit(solution)/shard_map/ppermute | solution.py:19
  12.6 6.2 %collective-permute-start.1 = (f32[2,32,128]{2,1,0:T(8,128)S(1)}, f32[2,32,128]{2,1,0:T(8,128)S(1)}, u32[]{:S(2)}, u32[]{:S(2)}) collective-permute-start(f32[2,32,128]{2,1,0:T(8,128)S(1)} %get-tuple-element.134), channel_id=1, source_target_pairs={{0,2},{1,3},{2,4},{3,5},{4,6},{5,7},{6,0},{7,1},{8,10},{9,11},{10,... | collective-permute-start | bytes 98312 | tf_op jit(solution)/shard_map/ppermute | solution.py:24
  14.2 5.2 collective-permute-start.2
  29.1 5.8 %collective-permute-start.5 = (f32[2,32,128]{2,1,0:T(8,128)S(1)}, f32[2,32,128]{2,1,0:T(8,128)S(1)}, u32[]{:S(2)}, u32[]{:S(2)}) collective-permute-start(f32[2,32,128]{2,1,0:T(8,128)S(1)} %get-tuple-element.132), channel_id=1, source_target_pairs={{0,2},{1,3},{2,4},{3,5},{4,6},{5,7},{6,0},{7,1},{8,10},{9,11},{10,... | collective-permute-start | bytes 98312 | tf_op jit(solution)/shard_map/ppermute | solution.py:24
  29.4 6.1 %collective-permute-start.6 = (f32[2,32,128]{2,1,0:T(8,128)S(1)}, f32[2,32,128]{2,1,0:T(8,128)S(1)}, u32[]{:S(2)}, u32[]{:S(2)}) collective-permute-start(f32[2,32,128]{2,1,0:T(8,128)S(1)} %get-tuple-element.132), channel_id=1, source_target_pairs={{0,4},{1,5},{2,6},{3,7},{4,0},{5,1},{6,2},{7,3},{8,12},{9,13},{10,... | collective-permute-start | bytes 98312 | tf_op jit(solution)/shard_map/ppermute | solution.py:24
  45.2 5.8 %collective-permute-start.9 = (f32[2,32,128]{2,1,0:T(8,128)S(1)}, f32[2,32,128]{2,1,0:T(8,128)S(1)}, u32[]{:S(2)}, u32[]{:S(2)}) collective-permute-start(f32[2,32,128]{2,1,0:T(8,128)S(1)} %get-tuple-element.130), channel_id=1, source_target_pairs={{0,2},{1,3},{2,4},{3,5},{4,6},{5,7},{6,0},{7,1},{8,10},{9,11},{10,... | collective-permute-start | bytes 98312 | tf_op jit(solution)/shard_map/ppermute | solution.py:24
  45.9 5.5 %collective-permute-start.10 = (f32[2,32,128]{2,1,0:T(8,128)S(1)}, f32[2,32,128]{2,1,0:T(8,128)S(1)}, u32[]{:S(2)}, u32[]{:S(2)}) collective-permute-start(f32[2,32,128]{2,1,0:T(8,128)S(1)} %get-tuple-element.130), channel_id=1, source_target_pairs={{0,4},{1,5},{2,6},{3,7},{4,0},{5,1},{6,2},{7,3},{8,12},{9,13},{10,... | collective-permute-start | bytes 98312 | tf_op jit(solution)/shard_map/ppermute | solution.py:24
  60.4 5.7 %collective-permute-start.13 = (f32[2,32,128]{2,1,0:T(8,128)S(1)}, f32[2,32,128]{2,1,0:T(8,128)S(1)}, u32[]{:S(2)}, u32[]{:S(2)}) collective-permute-start(f32[2,32,128]{2,1,0:T(8,128)S(1)} %get-tuple-element.128), channel_id=1, source_target_pairs={{0,2},{1,3},{2,4},{3,5},{4,6},{5,7},{6,0},{7,1},{8,10},{9,11},{10,... | collective-permute-start | bytes 98312 | tf_op jit(solution)/shard_map/ppermute | solution.py:24
  76.3 5.7 %collective-permute-start.17 = (f32[2,32,128]{2,1,0:T(8,128)S(1)}, f32[2,32,128]{2,1,0:T(8,128)S(1)}, u32[]{:S(2)}, u32[]{:S(2)}) collective-permute-start(f32[2,32,128]{2,1,0:T(8,128)S(1)} %get-tuple-element.126), channel_id=1, source_target_pairs={{0,2},{1,3},{2,4},{3,5},{4,6},{5,7},{6,0},{7,1},{8,10},{9,11},{10,... | collective-permute-start | bytes 98312 | tf_op jit(solution)/shard_map/ppermute | solution.py:24
  77.2 6.6 %collective-permute-start.18 = (f32[2,32,128]{2,1,0:T(8,128)S(1)}, f32[2,32,128]{2,1,0:T(8,128)S(1)}, u32[]{:S(2)}, u32[]{:S(2)}) collective-permute-start(f32[2,32,128]{2,1,0:T(8,128)S(1)} %get-tuple-element.126), channel_id=1, source_target_pairs={{0,4},{1,5},{2,6},{3,7},{4,0},{5,1},{6,2},{7,3},{8,12},{9,13},{10,... | collective-permute-start | bytes 98312 | tf_op jit(solution)/shard_map/ppermute | solution.py:24
  92.6 5.7 %collective-permute-start.21 = (f32[2,32,128]{2,1,0:T(8,128)S(1)}, f32[2,32,128]{2,1,0:T(8,128)S(1)}, u32[]{:S(2)}, u32[]{:S(2)}) collective-permute-start(f32[2,32,128]{2,1,0:T(8,128)S(1)} %get-tuple-element.124), channel_id=1, source_target_pairs={{0,2},{1,3},{2,4},{3,5},{4,6},{5,7},{6,0},{7,1},{8,10},{9,11},{10,... | collective-permute-start | bytes 98312 | tf_op jit(solution)/shard_map/ppermute | solution.py:24
  93.5 5.4 %collective-permute-start.22 = (f32[2,32,128]{2,1,0:T(8,128)S(1)}, f32[2,32,128]{2,1,0:T(8,128)S(1)}, u32[]{:S(2)}, u32[]{:S(2)}) collective-permute-start(f32[2,32,128]{2,1,0:T(8,128)S(1)} %get-tuple-element.124), channel_id=1, source_target_pairs={{0,4},{1,5},{2,6},{3,7},{4,0},{5,1},{6,2},{7,3},{8,12},{9,13},{10,... | collective-permute-start | bytes 98312 | tf_op jit(solution)/shard_map/ppermute | solution.py:24
  108.1 5.7 %collective-permute-start.25 = (f32[2,32,128]{2,1,0:T(8,128)S(1)}, f32[2,32,128]{2,1,0:T(8,128)S(1)}, u32[]{:S(2)}, u32[]{:S(2)}) collective-permute-start(f32[2,32,128]{2,1,0:T(8,128)S(1)} %get-tuple-element.122), channel_id=1, source_target_pairs={{0,2},{1,3},{2,4},{3,5},{4,6},{5,7},{6,0},{7,1},{8,10},{9,11},{10,... | collective-permute-start | bytes 98312 | tf_op jit(solution)/shard_map/ppermute | solution.py:24
  109.4 5.0 collective-permute-start.26
  123.7 5.7 %collective-permute-start.29 = (f32[2,32,128]{2,1,0:T(8,128)S(1)}, f32[2,32,128]{2,1,0:T(8,128)S(1)}, u32[]{:S(2)}, u32[]{:S(2)}) collective-permute-start(f32[2,32,128]{2,1,0:T(8,128)S(1)} %get-tuple-element.120), channel_id=1, source_target_pairs={{0,2},{1,3},{2,4},{3,5},{4,6},{5,7},{6,0},{7,1},{8,10},{9,11},{10,... | collective-permute-start | bytes 98312 | tf_op jit(solution)/shard_map/ppermute | solution.py:24
  124.9 5.2 collective-permute-start.30
  139.9 5.7 %collective-permute-start.33 = (f32[2,32,128]{2,1,0:T(8,128)S(1)}, f32[2,32,128]{2,1,0:T(8,128)S(1)}, u32[]{:S(2)}, u32[]{:S(2)}) collective-permute-start(f32[2,32,128]{2,1,0:T(8,128)S(1)} %get-tuple-element.118), channel_id=1, source_target_pairs={{0,2},{1,3},{2,4},{3,5},{4,6},{5,7},{6,0},{7,1},{8,10},{9,11},{10,... | collective-permute-start | bytes 98312 | tf_op jit(solution)/shard_map/ppermute | solution.py:24
  141.2 5.2 collective-permute-start.34
  159.6 5.7 %collective-permute-start.39 = (f32[2,32,128]{2,1,0:T(8,128)S(1)}, f32[2,32,128]{2,1,0:T(8,128)S(1)}, u32[]{:S(2)}, u32[]{:S(2)}) collective-permute-start(f32[2,32,128]{2,1,0:T(8,128)S(1)} %get-tuple-element.116), channel_id=1, source_target_pairs={{0,2},{1,3},{2,4},{3,5},{4,6},{5,7},{6,0},{7,1},{8,10},{9,11},{10,... | collective-permute-start | bytes 98312 | tf_op jit(solution)/shard_map/ppermute | solution.py:24
  160.7 5.3 collective-permute-start.40
  175.0 5.7 %collective-permute-start.43 = (f32[2,32,128]{2,1,0:T(8,128)S(1)}, f32[2,32,128]{2,1,0:T(8,128)S(1)}, u32[]{:S(2)}, u32[]{:S(2)}) collective-permute-start(f32[2,32,128]{2,1,0:T(8,128)S(1)} %get-tuple-element.114), channel_id=1, source_target_pairs={{0,2},{1,3},{2,4},{3,5},{4,6},{5,7},{6,0},{7,1},{8,10},{9,11},{10,... | collective-permute-start | bytes 98312 | tf_op jit(solution)/shard_map/ppermute | solution.py:24
  176.4 5.1 collective-permute-start.44
  190.6 5.7 %collective-permute-start.47 = (f32[2,32,128]{2,1,0:T(8,128)S(1)}, f32[2,32,128]{2,1,0:T(8,128)S(1)}, u32[]{:S(2)}, u32[]{:S(2)}) collective-permute-start(f32[2,32,128]{2,1,0:T(8,128)S(1)} %get-tuple-element.112), channel_id=1, source_target_pairs={{0,2},{1,3},{2,4},{3,5},{4,6},{5,7},{6,0},{7,1},{8,10},{9,11},{10,... | collective-permute-start | bytes 98312 | tf_op jit(solution)/shard_map/ppermute | solution.py:24
  191.9 5.2 collective-permute-start.48
  206.2 5.7 %collective-permute-start.51 = (f32[2,32,128]{2,1,0:T(8,128)S(1)}, f32[2,32,128]{2,1,0:T(8,128)S(1)}, u32[]{:S(2)}, u32[]{:S(2)}) collective-permute-start(f32[2,32,128]{2,1,0:T(8,128)S(1)} %get-tuple-element.110), channel_id=1, source_target_pairs={{0,2},{1,3},{2,4},{3,5},{4,6},{5,7},{6,0},{7,1},{8,10},{9,11},{10,... | collective-permute-start | bytes 98312 | tf_op jit(solution)/shard_map/ppermute | solution.py:24
  207.5 5.1 collective-permute-start.52
  222.0 5.8 %collective-permute-start.55 = (f32[2,32,128]{2,1,0:T(8,128)S(1)}, f32[2,32,128]{2,1,0:T(8,128)S(1)}, u32[]{:S(2)}, u32[]{:S(2)}) collective-permute-start(f32[2,32,128]{2,1,0:T(8,128)S(1)} %get-tuple-element.108), channel_id=1, source_target_pairs={{0,2},{1,3},{2,4},{3,5},{4,6},{5,7},{6,0},{7,1},{8,10},{9,11},{10,... | collective-permute-start | bytes 98312 | tf_op jit(solution)/shard_map/ppermute | solution.py:24
  223.1 6.5 %collective-permute-start.56 = (f32[2,32,128]{2,1,0:T(8,128)S(1)}, f32[2,32,128]{2,1,0:T(8,128)S(1)}, u32[]{:S(2)}, u32[]{:S(2)}) collective-permute-start(f32[2,32,128]{2,1,0:T(8,128)S(1)} %get-tuple-element.108), channel_id=1, source_target_pairs={{0,4},{1,5},{2,6},{3,7},{4,0},{5,1},{6,2},{7,3},{8,12},{9,13},{10,... | collective-permute-start | bytes 98312 | tf_op jit(solution)/shard_map/ppermute | solution.py:24
  238.4 5.7 %collective-permute-start.59 = (f32[2,32,128]{2,1,0:T(8,128)S(1)}, f32[2,32,128]{2,1,0:T(8,128)S(1)}, u32[]{:S(2)}, u32[]{:S(2)}) collective-permute-start(f32[2,32,128]{2,1,0:T(8,128)S(1)} %get-tuple-element.106), channel_id=1, source_target_pairs={{0,2},{1,3},{2,4},{3,5},{4,6},{5,7},{6,0},{7,1},{8,10},{9,11},{10,... | collective-permute-start | bytes 98312 | tf_op jit(solution)/shard_map/ppermute | solution.py:24
  239.3 5.5 %collective-permute-start.60 = (f32[2,32,128]{2,1,0:T(8,128)S(1)}, f32[2,32,128]{2,1,0:T(8,128)S(1)}, u32[]{:S(2)}, u32[]{:S(2)}) collective-permute-start(f32[2,32,128]{2,1,0:T(8,128)S(1)} %get-tuple-element.106), channel_id=1, source_target_pairs={{0,4},{1,5},{2,6},{3,7},{4,0},{5,1},{6,2},{7,3},{8,12},{9,13},{10,... | collective-permute-start | bytes 98312 | tf_op jit(solution)/shard_map/ppermute | solution.py:24
  254.1 5.7 %collective-permute-start.63 = (f32[2,32,128]{2,1,0:T(8,128)S(1)}, f32[2,32,128]{2,1,0:T(8,128)S(1)}, u32[]{:S(2)}, u32[]{:S(2)}) collective-permute-start(f32[2,32,128]{2,1,0:T(8,128)S(1)} %get-tuple-element.104), channel_id=1, source_target_pairs={{0,2},{1,3},{2,4},{3,5},{4,6},{5,7},{6,0},{7,1},{8,10},{9,11},{10,... | collective-permute-start | bytes 98312 | tf_op jit(solution)/shard_map/ppermute | solution.py:24
  255.4 5.2 collective-permute-start.64
  269.7 5.7 %collective-permute-start.67 = (f32[2,32,128]{2,1,0:T(8,128)S(1)}, f32[2,32,128]{2,1,0:T(8,128)S(1)}, u32[]{:S(2)}, u32[]{:S(2)}) collective-permute-start(f32[2,32,128]{2,1,0:T(8,128)S(1)} %get-tuple-element.102), channel_id=1, source_target_pairs={{0,2},{1,3},{2,4},{3,5},{4,6},{5,7},{6,0},{7,1},{8,10},{9,11},{10,... | collective-permute-start | bytes 98312 | tf_op jit(solution)/shard_map/ppermute | solution.py:24
  271.0 5.1 collective-permute-start.68
  288.3 5.7 %collective-permute-start.73 = (f32[2,32,128]{2,1,0:T(8,128)S(1)}, f32[2,32,128]{2,1,0:T(8,128)S(1)}, u32[]{:S(2)}, u32[]{:S(2)}) collective-permute-start(f32[2,32,128]{2,1,0:T(8,128)S(1)} %get-tuple-element.100), channel_id=1, source_target_pairs={{0,2},{1,3},{2,4},{3,5},{4,6},{5,7},{6,0},{7,1},{8,10},{9,11},{10,... | collective-permute-start | bytes 98312 | tf_op jit(solution)/shard_map/ppermute | solution.py:24
  289.5 5.2 collective-permute-start.74
  303.9 5.7 %collective-permute-start.77 = (f32[2,32,128]{2,1,0:T(8,128)S(1)}, f32[2,32,128]{2,1,0:T(8,128)S(1)}, u32[]{:S(2)}, u32[]{:S(2)}) collective-permute-start(f32[2,32,128]{2,1,0:T(8,128)S(1)} %get-tuple-element.98), channel_id=1, source_target_pairs={{0,2},{1,3},{2,4},{3,5},{4,6},{5,7},{6,0},{7,1},{8,10},{9,11},{10,... | collective-permute-start | bytes 98312 | tf_op jit(solution)/shard_map/ppermute | solution.py:24
  305.0 5.3 collective-permute-start.78
  319.3 5.7 %collective-permute-start.81 = (f32[2,32,128]{2,1,0:T(8,128)S(1)}, f32[2,32,128]{2,1,0:T(8,128)S(1)}, u32[]{:S(2)}, u32[]{:S(2)}) collective-permute-start(f32[2,32,128]{2,1,0:T(8,128)S(1)} %get-tuple-element.96), channel_id=1, source_target_pairs={{0,2},{1,3},{2,4},{3,5},{4,6},{5,7},{6,0},{7,1},{8,10},{9,11},{10,... | collective-permute-start | bytes 98312 | tf_op jit(solution)/shard_map/ppermute | solution.py:24
  320.6 5.2 collective-permute-start.82
  334.7 5.7 %collective-permute-start.85 = (f32[2,32,128]{2,1,0:T(8,128)S(1)}, f32[2,32,128]{2,1,0:T(8,128)S(1)}, u32[]{:S(2)}, u32[]{:S(2)}) collective-permute-start(f32[2,32,128]{2,1,0:T(8,128)S(1)} %get-tuple-element.94), channel_id=1, source_target_pairs={{0,2},{1,3},{2,4},{3,5},{4,6},{5,7},{6,0},{7,1},{8,10},{9,11},{10,... | collective-permute-start | bytes 98312 | tf_op jit(solution)/shard_map/ppermute | solution.py:24
  336.1 5.1 collective-permute-start.86
  350.3 5.7 %collective-permute-start.89 = (f32[2,32,128]{2,1,0:T(8,128)S(1)}, f32[2,32,128]{2,1,0:T(8,128)S(1)}, u32[]{:S(2)}, u32[]{:S(2)}) collective-permute-start(f32[2,32,128]{2,1,0:T(8,128)S(1)} %get-tuple-element.92), channel_id=1, source_target_pairs={{0,2},{1,3},{2,4},{3,5},{4,6},{5,7},{6,0},{7,1},{8,10},{9,11},{10,... | collective-permute-start | bytes 98312 | tf_op jit(solution)/shard_map/ppermute | solution.py:24
  351.5 6.4 %collective-permute-start.90 = (f32[2,32,128]{2,1,0:T(8,128)S(1)}, f32[2,32,128]{2,1,0:T(8,128)S(1)}, u32[]{:S(2)}, u32[]{:S(2)}) collective-permute-start(f32[2,32,128]{2,1,0:T(8,128)S(1)} %get-tuple-element.92), channel_id=1, source_target_pairs={{0,4},{1,5},{2,6},{3,7},{4,0},{5,1},{6,2},{7,3},{8,12},{9,13},{10,... | collective-permute-start | bytes 98312 | tf_op jit(solution)/shard_map/ppermute | solution.py:24
  366.6 5.8 %collective-permute-start.93 = (f32[2,32,128]{2,1,0:T(8,128)S(1)}, f32[2,32,128]{2,1,0:T(8,128)S(1)}, u32[]{:S(2)}, u32[]{:S(2)}) collective-permute-start(f32[2,32,128]{2,1,0:T(8,128)S(1)} %get-tuple-element.90), channel_id=1, source_target_pairs={{0,2},{1,3},{2,4},{3,5},{4,6},{5,7},{6,0},{7,1},{8,10},{9,11},{10,... | collective-permute-start | bytes 98312 | tf_op jit(solution)/shard_map/ppermute | solution.py:24
  367.5 5.5 %collective-permute-start.94 = (f32[2,32,128]{2,1,0:T(8,128)S(1)}, f32[2,32,128]{2,1,0:T(8,128)S(1)}, u32[]{:S(2)}, u32[]{:S(2)}) collective-permute-start(f32[2,32,128]{2,1,0:T(8,128)S(1)} %get-tuple-element.90), channel_id=1, source_target_pairs={{0,4},{1,5},{2,6},{3,7},{4,0},{5,1},{6,2},{7,3},{8,12},{9,13},{10,... | collective-permute-start | bytes 98312 | tf_op jit(solution)/shard_map/ppermute | solution.py:24
  381.9 5.7 %collective-permute-start.97 = (f32[2,32,128]{2,1,0:T(8,128)S(1)}, f32[2,32,128]{2,1,0:T(8,128)S(1)}, u32[]{:S(2)}, u32[]{:S(2)}) collective-permute-start(f32[2,32,128]{2,1,0:T(8,128)S(1)} %get-tuple-element.88), channel_id=1, source_target_pairs={{0,2},{1,3},{2,4},{3,5},{4,6},{5,7},{6,0},{7,1},{8,10},{9,11},{10,... | collective-permute-start | bytes 98312 | tf_op jit(solution)/shard_map/ppermute | solution.py:24
  383.3 5.0 collective-permute-start.98
  397.4 5.7 %collective-permute-start.101 = (f32[2,32,128]{2,1,0:T(8,128)S(1)}, f32[2,32,128]{2,1,0:T(8,128)S(1)}, u32[]{:S(2)}, u32[]{:S(2)}) collective-permute-start(f32[2,32,128]{2,1,0:T(8,128)S(1)} %get-tuple-element.86), channel_id=1, source_target_pairs={{0,2},{1,3},{2,4},{3,5},{4,6},{5,7},{6,0},{7,1},{8,10},{9,11},{10,... | collective-permute-start | bytes 98312 | tf_op jit(solution)/shard_map/ppermute | solution.py:24
  398.6 5.2 collective-permute-start.102
  416.9 5.7 %collective-permute-start.107 = (f32[2,32,128]{2,1,0:T(8,128)S(1)}, f32[2,32,128]{2,1,0:T(8,128)S(1)}, u32[]{:S(2)}, u32[]{:S(2)}) collective-permute-start(f32[2,32,128]{2,1,0:T(8,128)S(1)} %get-tuple-element.84), channel_id=1, source_target_pairs={{0,2},{1,3},{2,4},{3,5},{4,6},{5,7},{6,0},{7,1},{8,10},{9,11},{10,... | collective-permute-start | bytes 98312 | tf_op jit(solution)/shard_map/ppermute | solution.py:24
  418.3 5.1 collective-permute-start.108
  432.6 5.7 %collective-permute-start.111 = (f32[2,32,128]{2,1,0:T(8,128)S(1)}, f32[2,32,128]{2,1,0:T(8,128)S(1)}, u32[]{:S(2)}, u32[]{:S(2)}) collective-permute-start(f32[2,32,128]{2,1,0:T(8,128)S(1)} %get-tuple-element.82), channel_id=1, source_target_pairs={{0,2},{1,3},{2,4},{3,5},{4,6},{5,7},{6,0},{7,1},{8,10},{9,11},{10,... | collective-permute-start | bytes 98312 | tf_op jit(solution)/shard_map/ppermute | solution.py:24
  433.7 5.4 collective-permute-start.112
  447.9 5.7 %collective-permute-start.115 = (f32[2,32,128]{2,1,0:T(8,128)S(1)}, f32[2,32,128]{2,1,0:T(8,128)S(1)}, u32[]{:S(2)}, u32[]{:S(2)}) collective-permute-start(f32[2,32,128]{2,1,0:T(8,128)S(1)} %get-tuple-element.80), channel_id=1, source_target_pairs={{0,2},{1,3},{2,4},{3,5},{4,6},{5,7},{6,0},{7,1},{8,10},{9,11},{10,... | collective-permute-start | bytes 98312 | tf_op jit(solution)/shard_map/ppermute | solution.py:24
  463.5 5.7 %collective-permute-start.119 = (f32[2,32,128]{2,1,0:T(8,128)S(1)}, f32[2,32,128]{2,1,0:T(8,128)S(1)}, u32[]{:S(2)}, u32[]{:S(2)}) collective-permute-start(f32[2,32,128]{2,1,0:T(8,128)S(1)} %get-tuple-element.78), channel_id=1, source_target_pairs={{0,2},{1,3},{2,4},{3,5},{4,6},{5,7},{6,0},{7,1},{8,10},{9,11},{10,... | collective-permute-start | bytes 98312 | tf_op jit(solution)/shard_map/ppermute | solution.py:24
  464.6 5.3 collective-permute-start.120
  479.1 5.9 %collective-permute-start.123 = (f32[2,32,128]{2,1,0:T(8,128)S(1)}, f32[2,32,128]{2,1,0:T(8,128)S(1)}, u32[]{:S(2)}, u32[]{:S(2)}) collective-permute-start(f32[2,32,128]{2,1,0:T(8,128)S(1)} %get-tuple-element.76), channel_id=1, source_target_pairs={{0,2},{1,3},{2,4},{3,5},{4,6},{5,7},{6,0},{7,1},{8,10},{9,11},{10,... | collective-permute-start | bytes 98312 | tf_op jit(solution)/shard_map/ppermute | solution.py:24
  480.4 6.2 %collective-permute-start.124 = (f32[2,32,128]{2,1,0:T(8,128)S(1)}, f32[2,32,128]{2,1,0:T(8,128)S(1)}, u32[]{:S(2)}, u32[]{:S(2)}) collective-permute-start(f32[2,32,128]{2,1,0:T(8,128)S(1)} %get-tuple-element.76), channel_id=1, source_target_pairs={{0,4},{1,5},{2,6},{3,7},{4,0},{5,1},{6,2},{7,3},{8,12},{9,13},{10,... | collective-permute-start | bytes 98312 | tf_op jit(solution)/shard_map/ppermute | solution.py:24
  495.4 5.7 %collective-permute-start.127 = (f32[2,32,128]{2,1,0:T(8,128)S(1)}, f32[2,32,128]{2,1,0:T(8,128)S(1)}, u32[]{:S(2)}, u32[]{:S(2)}) collective-permute-start(f32[2,32,128]{2,1,0:T(8,128)S(1)} %get-tuple-element.74), channel_id=1, source_target_pairs={{0,2},{1,3},{2,4},{3,5},{4,6},{5,7},{6,0},{7,1},{8,10},{9,11},{10,... | collective-permute-start | bytes 98312 | tf_op jit(solution)/shard_map/ppermute | solution.py:24
  496.3 5.5 %collective-permute-start.128 = (f32[2,32,128]{2,1,0:T(8,128)S(1)}, f32[2,32,128]{2,1,0:T(8,128)S(1)}, u32[]{:S(2)}, u32[]{:S(2)}) collective-permute-start(f32[2,32,128]{2,1,0:T(8,128)S(1)} %get-tuple-element.74), channel_id=1, source_target_pairs={{0,4},{1,5},{2,6},{3,7},{4,0},{5,1},{6,2},{7,3},{8,12},{9,13},{10,... | collective-permute-start | bytes 98312 | tf_op jit(solution)/shard_map/ppermute | solution.py:24
  510.8 5.7 %collective-permute-start.131 = (f32[2,32,128]{2,1,0:T(8,128)S(1)}, f32[2,32,128]{2,1,0:T(8,128)S(1)}, u32[]{:S(2)}, u32[]{:S(2)}) collective-permute-start(f32[2,32,128]{2,1,0:T(8,128)S(1)} %get-tuple-element.72), channel_id=1, source_target_pairs={{0,2},{1,3},{2,4},{3,5},{4,6},{5,7},{6,0},{7,1},{8,10},{9,11},{10,... | collective-permute-start | bytes 98312 | tf_op jit(solution)/shard_map/ppermute | solution.py:24
  512.1 5.1 collective-permute-start.132
  526.6 5.4 collective-permute-start.135
  (86 other events, 483.1 us)

commit v5 on v4

--- a/solution.py
+++ b/solution.py
@@ -20,14 +20,14 @@
     pair = jnp.stack([value, partner])
     parts = [pair]
     for k in range(1, half):
-        moves = [(i, ((i // 2 + k) % half) * 2 + i % 2) for i in range(count)]
+        moves = [(i, ((i // 2) ^ k) * 2 + i % 2) for i in range(count)]
         parts.append(lax.ppermute(pair, "sub", moves))
     return jnp.stack(parts).reshape((count,) + value.shape)
 
 
 def slot_of(index, me, count, chunk):
     owner = index // chunk
-    slot = ((me // 2 - owner // 2) % (count // 2)) * 2 + ((owner % 2) ^ (me % 2))
+    slot = ((me // 2) ^ (owner // 2)) * 2 + ((owner % 2) ^ (me % 2))
     return slot * chunk + index % chunk
 
 

time: 549 us -> 584 us (1.064)
  waiting for transfers between devices: 211 us -> 232 us
  starting transfers between devices: 158 us -> 171 us
    ppermute x99, waiting for transfers between devices: 103 us -> 124 us  [collect(): parts.append(lax.ppermute(pair, 'sub', moves))]
    ppermute x99, starting transfers between devices: 132 us -> 145 us  [collect(): parts.append(lax.ppermute(pair, 'sub', moves))]
  transfers between devices with their start and end apart: 140 -> 140, of which waited for: 136 -> 103; matrix products, arithmetic and copies ran while one was open for 4% -> 4% of each run, Pallas kernels for 0% -> 0%
where the time goes in v5:
time: 584 us; the launch traced here: 573 us
  waiting for transfers between devices  232 us (40%)
  starting transfers between devices  171 us (29%)
  other arithmetic  125 us (21%)
  local copies, waits for them, and re-layouts  41.9 us (7%)
    ppermute x99, starting transfers between devices, collect(): parts.append(lax.ppermute(pair, 'sub', moves))  145 us
    ppermute x99, waiting for transfers between devices, collect(): parts.append(lax.ppermute(pair, 'sub', moves))  124 us
    ppermute x33, waiting for transfers between devices, collect(): partner = lax.ppermute(value, 'sub', [(i, i ^ 1) for i in range(count)])  103 us
    reduce_sum x32, other arithmetic, apply_blocks(): result = jnp.sum(blocks[0] * picked[:, None, :], axis=2)  90.1 us
    gather x32, local copies, waits for them, and re-layouts, on_device(): others = whole.reshape(-1, width)[remote_cols]  24 us
    add x32, other arithmetic, on_device(): field = field + (rhs - result - capacity * field) / system_diag  22.4 us
    ppermute x33, starting transfers between devices, collect(): partner = lax.ppermute(value, 'sub', [(i, i ^ 1) for i in range(count)])  21.6 us
  transfers between devices with their start and end apart: 140, of which 103 were waited for; matrix products, arithmetic and copies ran while one was open for 4% of the time, Pallas kernels for 0%

profile of v5, /device:TPU:0, one launch (start us, length us, event | category | flops | bytes accessed | tf_op | source)
XLA Modules:
  0.0 573.5 jit_solution(11026959210008401158)
XLA Ops:
  27.7 3.2 collective-permute-done.4
  31.8 3.5 collective-permute-start.7
  42.7 3.2 collective-permute-done.8
  46.2 3.8 collective-permute-start.10
  51.9 3.8 collective-permute-done.11
  61.1 3.2 collective-permute-done.12
  65.2 3.5 collective-permute-start.15
  76.2 3.2 collective-permute-done.16
  79.7 3.9 collective-permute-start.18
  85.9 3.5 collective-permute-done.19
  94.7 3.2 collective-permute-done.20
  99.0 3.3 collective-permute-start.23
  110.1 3.2 collective-permute-done.24
  113.5 3.6 collective-permute-start.26
  119.0 3.8 collective-permute-done.27
  128.2 3.2 collective-permute-done.28
  132.6 3.2 collective-permute-start.31
  147.4 3.8 collective-permute-start.34
  153.0 3.8 collective-permute-done.35
  166.1 3.2 collective-permute-done.38
  170.5 3.2 collective-permute-start.41
  181.4 3.2 collective-permute-done.42
  184.7 3.8 collective-permute-start.44
  190.3 3.8 collective-permute-done.45
  199.5 3.2 collective-permute-done.46
  203.9 3.2 collective-permute-start.49
  214.9 3.2 collective-permute-done.50
  218.2 3.8 collective-permute-start.52
  223.8 3.8 collective-permute-done.53
  233.0 3.2 collective-permute-done.54
  237.4 3.2 collective-permute-start.57
  248.4 3.2 collective-permute-done.58
  251.7 3.8 collective-permute-start.60
  266.5 3.2 collective-permute-done.62
  281.9 3.2 collective-permute-done.66
  285.2 3.8 collective-permute-start.68
  290.8 3.8 collective-permute-done.69
  303.1 3.2 collective-permute-done.72
  318.4 3.2 collective-permute-done.76
  321.7 3.8 collective-permute-start.78
  327.4 3.8 collective-permute-done.79
  336.4 3.2 collective-permute-done.80
  354.9 3.8 collective-permute-start.86
  360.6 3.8 collective-permute-done.87
  369.6 3.2 collective-permute-done.88
  374.0 3.2 collective-permute-start.91
  384.9 3.2 collective-permute-done.92
  388.2 3.7 collective-permute-start.94
  402.8 3.2 collective-permute-done.96
  407.2 3.2 collective-permute-start.99
  418.1 3.2 collective-permute-done.100
  421.3 3.8 collective-permute-start.102
  427.0 3.8 collective-permute-done.103
  444.7 3.2 collective-permute-start.109
  458.9 3.8 collective-permute-start.112
  464.5 3.8 collective-permute-done.113
  477.9 3.2 collective-permute-start.117
  492.1 3.8 collective-permute-start.120
  497.7 3.8 collective-permute-done.121
  511.2 3.2 collective-permute-start.125
  525.4 3.7 collective-permute-start.128
  544.4 3.2 collective-permute-start.133
  558.9 3.8 collective-permute-start.136
  564.3 3.8 collective-permute-done.137
  (613 shorter events, 347.5 us)
Async XLA Ops:
  0.6 11.2 %collective-permute-start = (f32[32,128]{1,0:T(8,128)}, f32[32,128]{1,0:T(8,128)S(1)}, u32[]{:S(2)}, u32[]{:S(2)}) collective-permute-start(f32[32,128]{1,0:T(8,128)} %bitcast.631), channel_id=1, source_target_pairs={{0,1},{1,0},{2,3},{3,2},{4,5},{5,4},{6,7},{7,6},{8,9},{9,8},{10,11... | collective-permute-start | bytes 49160 | tf_op jit(solution)/shard_map/ppermute | solution.py:19
  14.1 5.1 collective-permute-start.2
  16.7 5.7 collective-permute-start.3
  30.9 4.9 collective-permute-start.6
  31.8 5.7 collective-permute-start.7
  46.2 5.7 collective-permute-start.10
  50.0 5.7 collective-permute-start.11
  64.3 4.9 collective-permute-start.14
  65.2 5.7 collective-permute-start.15
  79.7 6.2 %collective-permute-start.18 = (f32[2,32,128]{2,1,0:T(8,128)S(1)}, f32[2,32,128]{2,1,0:T(8,128)S(1)}, u32[]{:S(2)}, u32[]{:S(2)}) collective-permute-start(f32[2,32,128]{2,1,0:T(8,128)S(1)} %get-tuple-element.126), channel_id=1, source_target_pairs={{0,4},{1,5},{2,6},{3,7},{4,0},{5,1},{6,2},{7,3},{8,12},{9,13},{10,... | collective-permute-start | bytes 98312 | tf_op jit(solution)/shard_map/ppermute | solution.py:24
  83.6 5.7 collective-permute-start.19
  99.0 5.7 %collective-permute-start.23 = (f32[2,32,128]{2,1,0:T(8,128)S(1)}, f32[2,32,128]{2,1,0:T(8,128)S(1)}, u32[]{:S(2)}, u32[]{:S(2)}) collective-permute-start(f32[2,32,128]{2,1,0:T(8,128)S(1)} %get-tuple-element.124), channel_id=1, source_target_pairs={{0,6},{1,7},{2,4},{3,5},{4,2},{5,3},{6,0},{7,1},{8,14},{9,15},{10,... | collective-permute-start | bytes 98312 | tf_op jit(solution)/shard_map/ppermute | solution.py:24
  113.5 5.5 collective-permute-start.26
  117.1 5.7 collective-permute-start.27
  131.4 4.9 collective-permute-start.30
  132.6 5.7 collective-permute-start.31
  147.4 5.7 collective-permute-start.34
  151.1 5.7 collective-permute-start.35
  169.4 4.9 collective-permute-start.40
  170.5 5.7 collective-permute-start.41
  184.7 5.7 collective-permute-start.44
  188.5 5.7 collective-permute-start.45
  202.7 4.9 collective-permute-start.48
  203.9 5.7 collective-permute-start.49
  218.2 5.7 collective-permute-start.52
  222.0 5.7 collective-permute-start.53
  236.2 5.0 collective-permute-start.56
  237.4 5.7 collective-permute-start.57
  251.7 6.5 %collective-permute-start.60 = (f32[2,32,128]{2,1,0:T(8,128)S(1)}, f32[2,32,128]{2,1,0:T(8,128)S(1)}, u32[]{:S(2)}, u32[]{:S(2)}) collective-permute-start(f32[2,32,128]{2,1,0:T(8,128)S(1)} %get-tuple-element.106), channel_id=1, source_target_pairs={{0,4},{1,5},{2,6},{3,7},{4,0},{5,1},{6,2},{7,3},{8,12},{9,13},{10,... | collective-permute-start | bytes 98312 | tf_op jit(solution)/shard_map/ppermute | solution.py:24
  255.4 5.7 collective-permute-start.61
  269.7 4.9 collective-permute-start.64
  270.9 5.7 collective-permute-start.65
  285.2 5.7 collective-permute-start.68
  288.9 5.7 collective-permute-start.69
  306.4 4.9 collective-permute-start.74
  307.5 5.7 collective-permute-start.75
  321.7 5.7 collective-permute-start.78
  325.5 5.7 collective-permute-start.79
  339.6 4.9 collective-permute-start.82
  340.8 5.7 collective-permute-start.83
  354.9 5.7 collective-permute-start.86
  358.7 5.7 collective-permute-start.87
  372.8 5.5 collective-permute-start.90
  374.0 5.7 collective-permute-start.91
  388.2 6.4 %collective-permute-start.94 = (f32[2,32,128]{2,1,0:T(8,128)S(1)}, f32[2,32,128]{2,1,0:T(8,128)S(1)}, u32[]{:S(2)}, u32[]{:S(2)}) collective-permute-start(f32[2,32,128]{2,1,0:T(8,128)S(1)} %get-tuple-element.90), channel_id=1, source_target_pairs={{0,4},{1,5},{2,6},{3,7},{4,0},{5,1},{6,2},{7,3},{8,12},{9,13},{10,... | collective-permute-start | bytes 98312 | tf_op jit(solution)/shard_map/ppermute | solution.py:24
  391.9 5.7 collective-permute-start.95
  406.1 4.9 collective-permute-start.98
  407.2 5.7 collective-permute-start.99
  421.3 5.7 collective-permute-start.102
  425.1 5.7 collective-permute-start.103
  444.7 5.7 collective-permute-start.109
  458.9 5.7 collective-permute-start.112
  462.6 5.7 collective-permute-start.113
  477.9 5.7 collective-permute-start.117
  492.1 5.7 collective-permute-start.120
  495.9 5.7 collective-permute-start.121
  510.0 5.5 collective-permute-start.124
  511.2 5.7 collective-permute-start.125
  525.4 6.4 %collective-permute-start.128 = (f32[2,32,128]{2,1,0:T(8,128)S(1)}, f32[2,32,128]{2,1,0:T(8,128)S(1)}, u32[]{:S(2)}, u32[]{:S(2)}) collective-permute-start(f32[2,32,128]{2,1,0:T(8,128)S(1)} %get-tuple-element.74), channel_id=1, source_target_pairs={{0,4},{1,5},{2,6},{3,7},{4,0},{5,1},{6,2},{7,3},{8,12},{9,13},{10,... | collective-permute-start | bytes 98312 | tf_op jit(solution)/shard_map/ppermute | solution.py:24
  529.1 5.7 collective-permute-start.129
  543.2 4.9 collective-permute-start.132
  544.4 5.7 collective-permute-start.133
  558.9 5.4 collective-permute-start.136
  562.7 5.4 collective-permute-start.137
  (86 other events, 518.0 us)

commit v6 on v4

--- a/solution.py
+++ b/solution.py
@@ -33,7 +33,12 @@
 
 def apply_blocks(blocks, own_part, others):
     picked = jnp.concatenate([own_part, others], axis=1)
-    result = jnp.sum(blocks[0] * picked[:, None, :], axis=2)
+    terms = blocks[0] * picked[:, None, :]
+    lanes = 128
+    folded = terms[..., :lanes]
+    for start in range(lanes, terms.shape[2], lanes):
+        folded = folded + terms[..., start:start + lanes]
+    result = jnp.sum(folded, axis=2)
     return result.reshape(1, -1)
 
 

time: 549 us -> 569 us (1.036)
  other arithmetic: 125 us -> 142 us
    mul x0 -> x32, other arithmetic: none -> 87.6 us  [apply_blocks(): terms = blocks[0] * picked[:, None, :]]
    reduce_sum x32, other arithmetic: 89.8 us -> 19.6 us  [apply_blocks(): result = jnp.sum(folded, axis=2)]
  transfers between devices with their start and end apart: 140 -> 140, of which waited for: 136 -> 135; matrix products, arithmetic and copies ran while one was open for 4% -> 4% of each run, Pallas kernels for 0% -> 0%
where the time goes in v6:
time: 569 us; the launch traced here: 558 us
  waiting for transfers between devices  214 us (38%)
  starting transfers between devices  157 us (28%)
  other arithmetic  142 us (25%)
  local copies, waits for them, and re-layouts  41.9 us (7%)
    ppermute x99, starting transfers between devices, collect(): parts.append(lax.ppermute(pair, 'sub', moves))  133 us
    ppermute x33, waiting for transfers between devices, collect(): partner = lax.ppermute(value, 'sub', [(i, i ^ 1) for i in range(count)])  103 us
    ppermute x99, waiting for transfers between devices, collect(): parts.append(lax.ppermute(pair, 'sub', moves))  102 us
    mul x32, other arithmetic, apply_blocks(): terms = blocks[0] * picked[:, None, :]  87.6 us
    gather x32, local copies, waits for them, and re-layouts, on_device(): others = whole.reshape(-1, width)[remote_cols]  23.9 us
    add x32, other arithmetic, on_device(): field = field + (rhs - result - capacity * field) / system_diag  22.4 us
    ppermute x33, starting transfers between devices, collect(): partner = lax.ppermute(value, 'sub', [(i, i ^ 1) for i in range(count)])  21.1 us
    reduce_sum x32, other arithmetic, apply_blocks(): result = jnp.sum(folded, axis=2)  19.6 us
  transfers between devices with their start and end apart: 140, of which 135 were waited for; matrix products, arithmetic and copies ran while one was open for 4% of the time, Pallas kernels for 0%

profile of v6, /device:TPU:0, one launch (start us, length us, event | category | flops | bytes accessed | tf_op | source)
XLA Modules:
  0.0 558.2 jit_solution(9672328365504575690)
XLA Ops:
  0.6 3.1 collective-permute-start
  21.6 2.7 bitcast_multiply_fusion.31
  26.5 3.2 collective-permute-done.4
  30.0 3.5 collective-permute-start.6
  38.4 2.7 bitcast_multiply_fusion.30
  43.1 3.2 collective-permute-done.8
  54.1 2.7 bitcast_multiply_fusion.29
  58.9 3.2 collective-permute-done.12
  70.6 2.7 bitcast_multiply_fusion.28
  75.4 3.2 collective-permute-done.16
  87.3 2.7 bitcast_multiply_fusion.27
  92.0 3.3 collective-permute-done.20
  103.4 2.7 bitcast_multiply_fusion.26
  108.1 3.3 collective-permute-done.24
  119.7 2.7 bitcast_multiply_fusion.25
  124.4 3.3 collective-permute-done.28
  135.8 2.7 bitcast_multiply_fusion.24
  140.5 3.3 collective-permute-done.32
  153.4 2.7 bitcast_multiply_fusion.23
  161.2 3.3 collective-permute-done.38
  172.3 2.7 bitcast_multiply_fusion.22
  177.0 3.3 collective-permute-done.42
  189.0 2.7 bitcast_multiply_fusion.21
  193.7 3.3 collective-permute-done.46
  205.1 2.7 bitcast_multiply_fusion.20
  209.8 3.3 collective-permute-done.50
  221.5 2.7 bitcast_multiply_fusion.19
  226.2 3.3 collective-permute-done.54
  238.2 2.7 bitcast_multiply_fusion.18
  243.0 3.2 collective-permute-done.58
  254.5 2.7 bitcast_multiply_fusion.17
  259.2 3.3 collective-permute-done.62
  270.4 2.7 bitcast_multiply_fusion.16
  275.3 3.2 collective-permute-done.66
  288.1 2.7 bitcast_multiply_fusion.15
  296.0 3.2 collective-permute-done.72
  307.2 2.7 bitcast_multiply_fusion.14
  312.0 3.2 collective-permute-done.76
  323.4 2.7 bitcast_multiply_fusion.13
  328.0 3.3 collective-permute-done.80
  339.3 2.7 bitcast_multiply_fusion.12
  344.1 3.2 collective-permute-done.84
  355.3 2.7 bitcast_multiply_fusion.11
  360.1 3.2 collective-permute-done.88
  372.0 2.7 bitcast_multiply_fusion.10
  376.7 3.2 collective-permute-done.92
  388.1 2.7 bitcast_multiply_fusion.9
  392.9 3.2 collective-permute-done.96
  408.7 3.2 collective-permute-done.100
  429.3 3.2 collective-permute-done.106
  440.6 2.7 bitcast_multiply_fusion.6
  445.4 3.2 collective-permute-done.110
  456.9 2.7 bitcast_multiply_fusion.5
  461.7 3.2 collective-permute-done.114
  473.1 2.7 bitcast_multiply_fusion.4
  477.8 3.2 collective-permute-done.118
  488.9 2.7 bitcast_multiply_fusion.3
  493.7 3.2 collective-permute-done.122
  505.6 2.7 bitcast_multiply_fusion.2
  510.4 3.2 collective-permute-done.126
  521.6 2.7 bitcast_multiply_fusion.1
  526.5 3.1 collective-permute-done.130
  537.6 2.7 bitcast_multiply_fusion
  543.0 3.0 collective-permute-done.134
  (645 shorter events, 363.2 us)
Async XLA Ops:
  0.6 11.1 %collective-permute-start = (f32[32,128]{1,0:T(8,128)}, f32[32,128]{1,0:T(8,128)S(1)}, u32[]{:S(2)}, u32[]{:S(2)}) collective-permute-start(f32[32,128]{1,0:T(8,128)} %bitcast.567), channel_id=1, source_target_pairs={{0,1},{1,0},{2,3},{3,2},{4,5},{5,4},{6,7},{7,6},{8,9},{9,8},{10,11... | collective-permute-start | bytes 49160 | tf_op jit(solution)/shard_map/ppermute | solution.py:19
  12.5 6.2 %collective-permute-start.1 = (f32[2,32,128]{2,1,0:T(8,128)S(1)}, f32[2,32,128]{2,1,0:T(8,128)S(1)}, u32[]{:S(2)}, u32[]{:S(2)}) collective-permute-start(f32[2,32,128]{2,1,0:T(8,128)S(1)} %get-tuple-element.134), channel_id=1, source_target_pairs={{0,2},{1,3},{2,4},{3,5},{4,6},{5,7},{6,0},{7,1},{8,10},{9,11},{10,... | collective-permute-start | bytes 98312 | tf_op jit(solution)/shard_map/ppermute | solution.py:24
  14.1 5.2 collective-permute-start.2
  29.8 5.8 %collective-permute-start.5 = (f32[2,32,128]{2,1,0:T(8,128)S(1)}, f32[2,32,128]{2,1,0:T(8,128)S(1)}, u32[]{:S(2)}, u32[]{:S(2)}) collective-permute-start(f32[2,32,128]{2,1,0:T(8,128)S(1)} %get-tuple-element.132), channel_id=1, source_target_pairs={{0,2},{1,3},{2,4},{3,5},{4,6},{5,7},{6,0},{7,1},{8,10},{9,11},{10,... | collective-permute-start | bytes 98312 | tf_op jit(solution)/shard_map/ppermute | solution.py:24
  30.0 6.1 %collective-permute-start.6 = (f32[2,32,128]{2,1,0:T(8,128)S(1)}, f32[2,32,128]{2,1,0:T(8,128)S(1)}, u32[]{:S(2)}, u32[]{:S(2)}) collective-permute-start(f32[2,32,128]{2,1,0:T(8,128)S(1)} %get-tuple-element.132), channel_id=1, source_target_pairs={{0,4},{1,5},{2,6},{3,7},{4,0},{5,1},{6,2},{7,3},{8,12},{9,13},{10,... | collective-permute-start | bytes 98312 | tf_op jit(solution)/shard_map/ppermute | solution.py:24
  46.4 5.8 %collective-permute-start.9 = (f32[2,32,128]{2,1,0:T(8,128)S(1)}, f32[2,32,128]{2,1,0:T(8,128)S(1)}, u32[]{:S(2)}, u32[]{:S(2)}) collective-permute-start(f32[2,32,128]{2,1,0:T(8,128)S(1)} %get-tuple-element.130), channel_id=1, source_target_pairs={{0,2},{1,3},{2,4},{3,5},{4,6},{5,7},{6,0},{7,1},{8,10},{9,11},{10,... | collective-permute-start | bytes 98312 | tf_op jit(solution)/shard_map/ppermute | solution.py:24
  47.0 5.5 collective-permute-start.10
  62.1 5.7 %collective-permute-start.13 = (f32[2,32,128]{2,1,0:T(8,128)S(1)}, f32[2,32,128]{2,1,0:T(8,128)S(1)}, u32[]{:S(2)}, u32[]{:S(2)}) collective-permute-start(f32[2,32,128]{2,1,0:T(8,128)S(1)} %get-tuple-element.128), channel_id=1, source_target_pairs={{0,2},{1,3},{2,4},{3,5},{4,6},{5,7},{6,0},{7,1},{8,10},{9,11},{10,... | collective-permute-start | bytes 98312 | tf_op jit(solution)/shard_map/ppermute | solution.py:24
  78.6 5.7 %collective-permute-start.17 = (f32[2,32,128]{2,1,0:T(8,128)S(1)}, f32[2,32,128]{2,1,0:T(8,128)S(1)}, u32[]{:S(2)}, u32[]{:S(2)}) collective-permute-start(f32[2,32,128]{2,1,0:T(8,128)S(1)} %get-tuple-element.126), channel_id=1, source_target_pairs={{0,2},{1,3},{2,4},{3,5},{4,6},{5,7},{6,0},{7,1},{8,10},{9,11},{10,... | collective-permute-start | bytes 98312 | tf_op jit(solution)/shard_map/ppermute | solution.py:24
  79.5 5.5 collective-permute-start.18
  95.3 5.8 %collective-permute-start.21 = (f32[2,32,128]{2,1,0:T(8,128)S(1)}, f32[2,32,128]{2,1,0:T(8,128)S(1)}, u32[]{:S(2)}, u32[]{:S(2)}) collective-permute-start(f32[2,32,128]{2,1,0:T(8,128)S(1)} %get-tuple-element.124), channel_id=1, source_target_pairs={{0,2},{1,3},{2,4},{3,5},{4,6},{5,7},{6,0},{7,1},{8,10},{9,11},{10,... | collective-permute-start | bytes 98312 | tf_op jit(solution)/shard_map/ppermute | solution.py:24
  96.3 5.6 %collective-permute-start.22 = (f32[2,32,128]{2,1,0:T(8,128)S(1)}, f32[2,32,128]{2,1,0:T(8,128)S(1)}, u32[]{:S(2)}, u32[]{:S(2)}) collective-permute-start(f32[2,32,128]{2,1,0:T(8,128)S(1)} %get-tuple-element.124), channel_id=1, source_target_pairs={{0,4},{1,5},{2,6},{3,7},{4,0},{5,1},{6,2},{7,3},{8,12},{9,13},{10,... | collective-permute-start | bytes 98312 | tf_op jit(solution)/shard_map/ppermute | solution.py:24
  111.4 5.7 %collective-permute-start.25 = (f32[2,32,128]{2,1,0:T(8,128)S(1)}, f32[2,32,128]{2,1,0:T(8,128)S(1)}, u32[]{:S(2)}, u32[]{:S(2)}) collective-permute-start(f32[2,32,128]{2,1,0:T(8,128)S(1)} %get-tuple-element.122), channel_id=1, source_target_pairs={{0,2},{1,3},{2,4},{3,5},{4,6},{5,7},{6,0},{7,1},{8,10},{9,11},{10,... | collective-permute-start | bytes 98312 | tf_op jit(solution)/shard_map/ppermute | solution.py:24
  127.7 5.7 %collective-permute-start.29 = (f32[2,32,128]{2,1,0:T(8,128)S(1)}, f32[2,32,128]{2,1,0:T(8,128)S(1)}, u32[]{:S(2)}, u32[]{:S(2)}) collective-permute-start(f32[2,32,128]{2,1,0:T(8,128)S(1)} %get-tuple-element.120), channel_id=1, source_target_pairs={{0,2},{1,3},{2,4},{3,5},{4,6},{5,7},{6,0},{7,1},{8,10},{9,11},{10,... | collective-permute-start | bytes 98312 | tf_op jit(solution)/shard_map/ppermute | solution.py:24
  128.8 5.4 collective-permute-start.30
  143.8 5.7 %collective-permute-start.33 = (f32[2,32,128]{2,1,0:T(8,128)S(1)}, f32[2,32,128]{2,1,0:T(8,128)S(1)}, u32[]{:S(2)}, u32[]{:S(2)}) collective-permute-start(f32[2,32,128]{2,1,0:T(8,128)S(1)} %get-tuple-element.118), channel_id=1, source_target_pairs={{0,2},{1,3},{2,4},{3,5},{4,6},{5,7},{6,0},{7,1},{8,10},{9,11},{10,... | collective-permute-start | bytes 98312 | tf_op jit(solution)/shard_map/ppermute | solution.py:24
  145.2 5.1 collective-permute-start.34
  164.5 5.7 %collective-permute-start.39 = (f32[2,32,128]{2,1,0:T(8,128)S(1)}, f32[2,32,128]{2,1,0:T(8,128)S(1)}, u32[]{:S(2)}, u32[]{:S(2)}) collective-permute-start(f32[2,32,128]{2,1,0:T(8,128)S(1)} %get-tuple-element.116), channel_id=1, source_target_pairs={{0,2},{1,3},{2,4},{3,5},{4,6},{5,7},{6,0},{7,1},{8,10},{9,11},{10,... | collective-permute-start | bytes 98312 | tf_op jit(solution)/shard_map/ppermute | solution.py:24
  165.5 5.4 collective-permute-start.40
  180.3 5.7 %collective-permute-start.43 = (f32[2,32,128]{2,1,0:T(8,128)S(1)}, f32[2,32,128]{2,1,0:T(8,128)S(1)}, u32[]{:S(2)}, u32[]{:S(2)}) collective-permute-start(f32[2,32,128]{2,1,0:T(8,128)S(1)} %get-tuple-element.114), channel_id=1, source_target_pairs={{0,2},{1,3},{2,4},{3,5},{4,6},{5,7},{6,0},{7,1},{8,10},{9,11},{10,... | collective-permute-start | bytes 98312 | tf_op jit(solution)/shard_map/ppermute | solution.py:24
  181.8 4.9 collective-permute-start.44
  197.0 5.7 %collective-permute-start.47 = (f32[2,32,128]{2,1,0:T(8,128)S(1)}, f32[2,32,128]{2,1,0:T(8,128)S(1)}, u32[]{:S(2)}, u32[]{:S(2)}) collective-permute-start(f32[2,32,128]{2,1,0:T(8,128)S(1)} %get-tuple-element.112), channel_id=1, source_target_pairs={{0,2},{1,3},{2,4},{3,5},{4,6},{5,7},{6,0},{7,1},{8,10},{9,11},{10,... | collective-permute-start | bytes 98312 | tf_op jit(solution)/shard_map/ppermute | solution.py:24
  198.1 5.3 collective-permute-start.48
  213.1 5.7 %collective-permute-start.51 = (f32[2,32,128]{2,1,0:T(8,128)S(1)}, f32[2,32,128]{2,1,0:T(8,128)S(1)}, u32[]{:S(2)}, u32[]{:S(2)}) collective-permute-start(f32[2,32,128]{2,1,0:T(8,128)S(1)} %get-tuple-element.110), channel_id=1, source_target_pairs={{0,2},{1,3},{2,4},{3,5},{4,6},{5,7},{6,0},{7,1},{8,10},{9,11},{10,... | collective-permute-start | bytes 98312 | tf_op jit(solution)/shard_map/ppermute | solution.py:24
  214.4 5.1 collective-permute-start.52
  229.5 6.0 %collective-permute-start.55 = (f32[2,32,128]{2,1,0:T(8,128)S(1)}, f32[2,32,128]{2,1,0:T(8,128)S(1)}, u32[]{:S(2)}, u32[]{:S(2)}) collective-permute-start(f32[2,32,128]{2,1,0:T(8,128)S(1)} %get-tuple-element.108), channel_id=1, source_target_pairs={{0,2},{1,3},{2,4},{3,5},{4,6},{5,7},{6,0},{7,1},{8,10},{9,11},{10,... | collective-permute-start | bytes 98312 | tf_op jit(solution)/shard_map/ppermute | solution.py:24
  230.5 6.6 %collective-permute-start.56 = (f32[2,32,128]{2,1,0:T(8,128)S(1)}, f32[2,32,128]{2,1,0:T(8,128)S(1)}, u32[]{:S(2)}, u32[]{:S(2)}) collective-permute-start(f32[2,32,128]{2,1,0:T(8,128)S(1)} %get-tuple-element.108), channel_id=1, source_target_pairs={{0,4},{1,5},{2,6},{3,7},{4,0},{5,1},{6,2},{7,3},{8,12},{9,13},{10,... | collective-permute-start | bytes 98312 | tf_op jit(solution)/shard_map/ppermute | solution.py:24
  246.2 5.7 %collective-permute-start.59 = (f32[2,32,128]{2,1,0:T(8,128)S(1)}, f32[2,32,128]{2,1,0:T(8,128)S(1)}, u32[]{:S(2)}, u32[]{:S(2)}) collective-permute-start(f32[2,32,128]{2,1,0:T(8,128)S(1)} %get-tuple-element.106), channel_id=1, source_target_pairs={{0,2},{1,3},{2,4},{3,5},{4,6},{5,7},{6,0},{7,1},{8,10},{9,11},{10,... | collective-permute-start | bytes 98312 | tf_op jit(solution)/shard_map/ppermute | solution.py:24
  247.3 5.3 collective-permute-start.60
  262.5 5.7 %collective-permute-start.63 = (f32[2,32,128]{2,1,0:T(8,128)S(1)}, f32[2,32,128]{2,1,0:T(8,128)S(1)}, u32[]{:S(2)}, u32[]{:S(2)}) collective-permute-start(f32[2,32,128]{2,1,0:T(8,128)S(1)} %get-tuple-element.104), channel_id=1, source_target_pairs={{0,2},{1,3},{2,4},{3,5},{4,6},{5,7},{6,0},{7,1},{8,10},{9,11},{10,... | collective-permute-start | bytes 98312 | tf_op jit(solution)/shard_map/ppermute | solution.py:24
  263.6 5.3 collective-permute-start.64
  278.4 5.7 %collective-permute-start.67 = (f32[2,32,128]{2,1,0:T(8,128)S(1)}, f32[2,32,128]{2,1,0:T(8,128)S(1)}, u32[]{:S(2)}, u32[]{:S(2)}) collective-permute-start(f32[2,32,128]{2,1,0:T(8,128)S(1)} %get-tuple-element.102), channel_id=1, source_target_pairs={{0,2},{1,3},{2,4},{3,5},{4,6},{5,7},{6,0},{7,1},{8,10},{9,11},{10,... | collective-permute-start | bytes 98312 | tf_op jit(solution)/shard_map/ppermute | solution.py:24
  279.9 4.9 collective-permute-start.68
  299.2 5.7 %collective-permute-start.73 = (f32[2,32,128]{2,1,0:T(8,128)S(1)}, f32[2,32,128]{2,1,0:T(8,128)S(1)}, u32[]{:S(2)}, u32[]{:S(2)}) collective-permute-start(f32[2,32,128]{2,1,0:T(8,128)S(1)} %get-tuple-element.100), channel_id=1, source_target_pairs={{0,2},{1,3},{2,4},{3,5},{4,6},{5,7},{6,0},{7,1},{8,10},{9,11},{10,... | collective-permute-start | bytes 98312 | tf_op jit(solution)/shard_map/ppermute | solution.py:24
  300.4 5.2 collective-permute-start.74
  315.2 5.7 %collective-permute-start.77 = (f32[2,32,128]{2,1,0:T(8,128)S(1)}, f32[2,32,128]{2,1,0:T(8,128)S(1)}, u32[]{:S(2)}, u32[]{:S(2)}) collective-permute-start(f32[2,32,128]{2,1,0:T(8,128)S(1)} %get-tuple-element.98), channel_id=1, source_target_pairs={{0,2},{1,3},{2,4},{3,5},{4,6},{5,7},{6,0},{7,1},{8,10},{9,11},{10,... | collective-permute-start | bytes 98312 | tf_op jit(solution)/shard_map/ppermute | solution.py:24
  316.4 5.1 collective-permute-start.78
  331.4 5.7 %collective-permute-start.81 = (f32[2,32,128]{2,1,0:T(8,128)S(1)}, f32[2,32,128]{2,1,0:T(8,128)S(1)}, u32[]{:S(2)}, u32[]{:S(2)}) collective-permute-start(f32[2,32,128]{2,1,0:T(8,128)S(1)} %get-tuple-element.96), channel_id=1, source_target_pairs={{0,2},{1,3},{2,4},{3,5},{4,6},{5,7},{6,0},{7,1},{8,10},{9,11},{10,... | collective-permute-start | bytes 98312 | tf_op jit(solution)/shard_map/ppermute | solution.py:24
  332.4 5.3 collective-permute-start.82
  347.3 5.7 %collective-permute-start.85 = (f32[2,32,128]{2,1,0:T(8,128)S(1)}, f32[2,32,128]{2,1,0:T(8,128)S(1)}, u32[]{:S(2)}, u32[]{:S(2)}) collective-permute-start(f32[2,32,128]{2,1,0:T(8,128)S(1)} %get-tuple-element.94), channel_id=1, source_target_pairs={{0,2},{1,3},{2,4},{3,5},{4,6},{5,7},{6,0},{7,1},{8,10},{9,11},{10,... | collective-permute-start | bytes 98312 | tf_op jit(solution)/shard_map/ppermute | solution.py:24
  348.6 5.0 collective-permute-start.86
  363.3 5.8 %collective-permute-start.89 = (f32[2,32,128]{2,1,0:T(8,128)S(1)}, f32[2,32,128]{2,1,0:T(8,128)S(1)}, u32[]{:S(2)}, u32[]{:S(2)}) collective-permute-start(f32[2,32,128]{2,1,0:T(8,128)S(1)} %get-tuple-element.92), channel_id=1, source_target_pairs={{0,2},{1,3},{2,4},{3,5},{4,6},{5,7},{6,0},{7,1},{8,10},{9,11},{10,... | collective-permute-start | bytes 98312 | tf_op jit(solution)/shard_map/ppermute | solution.py:24
  364.5 6.3 %collective-permute-start.90 = (f32[2,32,128]{2,1,0:T(8,128)S(1)}, f32[2,32,128]{2,1,0:T(8,128)S(1)}, u32[]{:S(2)}, u32[]{:S(2)}) collective-permute-start(f32[2,32,128]{2,1,0:T(8,128)S(1)} %get-tuple-element.92), channel_id=1, source_target_pairs={{0,4},{1,5},{2,6},{3,7},{4,0},{5,1},{6,2},{7,3},{8,12},{9,13},{10,... | collective-permute-start | bytes 98312 | tf_op jit(solution)/shard_map/ppermute | solution.py:24
  380.0 5.7 %collective-permute-start.93 = (f32[2,32,128]{2,1,0:T(8,128)S(1)}, f32[2,32,128]{2,1,0:T(8,128)S(1)}, u32[]{:S(2)}, u32[]{:S(2)}) collective-permute-start(f32[2,32,128]{2,1,0:T(8,128)S(1)} %get-tuple-element.90), channel_id=1, source_target_pairs={{0,2},{1,3},{2,4},{3,5},{4,6},{5,7},{6,0},{7,1},{8,10},{9,11},{10,... | collective-permute-start | bytes 98312 | tf_op jit(solution)/shard_map/ppermute | solution.py:24
  380.9 5.5 collective-permute-start.94
  396.1 5.7 %collective-permute-start.97 = (f32[2,32,128]{2,1,0:T(8,128)S(1)}, f32[2,32,128]{2,1,0:T(8,128)S(1)}, u32[]{:S(2)}, u32[]{:S(2)}) collective-permute-start(f32[2,32,128]{2,1,0:T(8,128)S(1)} %get-tuple-element.88), channel_id=1, source_target_pairs={{0,2},{1,3},{2,4},{3,5},{4,6},{5,7},{6,0},{7,1},{8,10},{9,11},{10,... | collective-permute-start | bytes 98312 | tf_op jit(solution)/shard_map/ppermute | solution.py:24
  397.2 5.3 collective-permute-start.98
  411.9 5.7 %collective-permute-start.101 = (f32[2,32,128]{2,1,0:T(8,128)S(1)}, f32[2,32,128]{2,1,0:T(8,128)S(1)}, u32[]{:S(2)}, u32[]{:S(2)}) collective-permute-start(f32[2,32,128]{2,1,0:T(8,128)S(1)} %get-tuple-element.86), channel_id=1, source_target_pairs={{0,2},{1,3},{2,4},{3,5},{4,6},{5,7},{6,0},{7,1},{8,10},{9,11},{10,... | collective-permute-start | bytes 98312 | tf_op jit(solution)/shard_map/ppermute | solution.py:24
  413.4 5.0 collective-permute-start.102
  432.5 5.7 %collective-permute-start.107 = (f32[2,32,128]{2,1,0:T(8,128)S(1)}, f32[2,32,128]{2,1,0:T(8,128)S(1)}, u32[]{:S(2)}, u32[]{:S(2)}) collective-permute-start(f32[2,32,128]{2,1,0:T(8,128)S(1)} %get-tuple-element.84), channel_id=1, source_target_pairs={{0,2},{1,3},{2,4},{3,5},{4,6},{5,7},{6,0},{7,1},{8,10},{9,11},{10,... | collective-permute-start | bytes 98312 | tf_op jit(solution)/shard_map/ppermute | solution.py:24
  433.9 5.0 collective-permute-start.108
  448.6 5.7 %collective-permute-start.111 = (f32[2,32,128]{2,1,0:T(8,128)S(1)}, f32[2,32,128]{2,1,0:T(8,128)S(1)}, u32[]{:S(2)}, u32[]{:S(2)}) collective-permute-start(f32[2,32,128]{2,1,0:T(8,128)S(1)} %get-tuple-element.82), channel_id=1, source_target_pairs={{0,2},{1,3},{2,4},{3,5},{4,6},{5,7},{6,0},{7,1},{8,10},{9,11},{10,... | collective-permute-start | bytes 98312 | tf_op jit(solution)/shard_map/ppermute | solution.py:24
  449.8 5.3 collective-permute-start.112
  464.9 5.7 %collective-permute-start.115 = (f32[2,32,128]{2,1,0:T(8,128)S(1)}, f32[2,32,128]{2,1,0:T(8,128)S(1)}, u32[]{:S(2)}, u32[]{:S(2)}) collective-permute-start(f32[2,32,128]{2,1,0:T(8,128)S(1)} %get-tuple-element.80), channel_id=1, source_target_pairs={{0,2},{1,3},{2,4},{3,5},{4,6},{5,7},{6,0},{7,1},{8,10},{9,11},{10,... | collective-permute-start | bytes 98312 | tf_op jit(solution)/shard_map/ppermute | solution.py:24
  466.1 5.2 collective-permute-start.116
  481.0 5.7 %collective-permute-start.119 = (f32[2,32,128]{2,1,0:T(8,128)S(1)}, f32[2,32,128]{2,1,0:T(8,128)S(1)}, u32[]{:S(2)}, u32[]{:S(2)}) collective-permute-start(f32[2,32,128]{2,1,0:T(8,128)S(1)} %get-tuple-element.78), channel_id=1, source_target_pairs={{0,2},{1,3},{2,4},{3,5},{4,6},{5,7},{6,0},{7,1},{8,10},{9,11},{10,... | collective-permute-start | bytes 98312 | tf_op jit(solution)/shard_map/ppermute | solution.py:24
  482.2 5.3 collective-permute-start.120
  496.9 6.0 %collective-permute-start.123 = (f32[2,32,128]{2,1,0:T(8,128)S(1)}, f32[2,32,128]{2,1,0:T(8,128)S(1)}, u32[]{:S(2)}, u32[]{:S(2)}) collective-permute-start(f32[2,32,128]{2,1,0:T(8,128)S(1)} %get-tuple-element.76), channel_id=1, source_target_pairs={{0,2},{1,3},{2,4},{3,5},{4,6},{5,7},{6,0},{7,1},{8,10},{9,11},{10,... | collective-permute-start | bytes 98312 | tf_op jit(solution)/shard_map/ppermute | solution.py:24
  498.3 6.1 %collective-permute-start.124 = (f32[2,32,128]{2,1,0:T(8,128)S(1)}, f32[2,32,128]{2,1,0:T(8,128)S(1)}, u32[]{:S(2)}, u32[]{:S(2)}) collective-permute-start(f32[2,32,128]{2,1,0:T(8,128)S(1)} %get-tuple-element.76), channel_id=1, source_target_pairs={{0,4},{1,5},{2,6},{3,7},{4,0},{5,1},{6,2},{7,3},{8,12},{9,13},{10,... | collective-permute-start | bytes 98312 | tf_op jit(solution)/shard_map/ppermute | solution.py:24
  513.6 5.7 %collective-permute-start.127 = (f32[2,32,128]{2,1,0:T(8,128)S(1)}, f32[2,32,128]{2,1,0:T(8,128)S(1)}, u32[]{:S(2)}, u32[]{:S(2)}) collective-permute-start(f32[2,32,128]{2,1,0:T(8,128)S(1)} %get-tuple-element.74), channel_id=1, source_target_pairs={{0,2},{1,3},{2,4},{3,5},{4,6},{5,7},{6,0},{7,1},{8,10},{9,11},{10,... | collective-permute-start | bytes 98312 | tf_op jit(solution)/shard_map/ppermute | solution.py:24
  514.5 5.5 collective-permute-start.128
  529.6 5.7 %collective-permute-start.131 = (f32[2,32,128]{2,1,0:T(8,128)S(1)}, f32[2,32,128]{2,1,0:T(8,128)S(1)}, u32[]{:S(2)}, u32[]{:S(2)}) collective-permute-start(f32[2,32,128]{2,1,0:T(8,128)S(1)} %get-tuple-element.72), channel_id=1, source_target_pairs={{0,2},{1,3},{2,4},{3,5},{4,6},{5,7},{6,0},{7,1},{8,10},{9,11},{10,... | collective-permute-start | bytes 98312 | tf_op jit(solution)/shard_map/ppermute | solution.py:24
  530.9 5.1 collective-permute-start.132
  546.0 5.4 collective-permute-start.135
  (86 other events, 366.4 us)

commit v7 on v4

--- a/solution.py
+++ b/solution.py
@@ -38,10 +38,10 @@
 
 
 def next_hist(end_volt, hist, surge):
+    outgoing_ends = jnp.stack([end_volt[:, 0], hist[:, 0]], axis=1)
     message = -2.0 * surge * end_volt[:, 1] - hist[:, 1]
-    new_left = shifted(message, "area", 1)
-    outgoing_ends = jnp.stack([end_volt[:, 0], hist[:, 0]], axis=1)
-    from_right = shifted(outgoing_ends, "area", -1)
+    from_right, new_left = lax.optimization_barrier(
+        (shifted(outgoing_ends, "area", -1), shifted(message, "area", 1)))
     new_right = -2.0 * surge * from_right[:, 0] - from_right[:, 1]
     return jnp.stack([new_left, new_right], axis=1)
 

time: 549 us -> 547 us (level)
  transfers between devices with their start and end apart: 140 -> 140, of which waited for: 136 -> 132; matrix products, arithmetic and copies ran while one was open for 4% -> 4% of each run, Pallas kernels for 0% -> 0%
where the time goes in v7:
time: 547 us; the launch traced here: 537 us
  waiting for transfers between devices  207 us (38%)
  starting transfers between devices  160 us (29%)
  other arithmetic  125 us (23%)
  local copies, waits for them, and re-layouts  42.6 us (8%)
    ppermute x99, starting transfers between devices, collect(): parts.append(lax.ppermute(pair, 'sub', moves))  134 us
    ppermute x33, waiting for transfers between devices, collect(): partner = lax.ppermute(value, 'sub', [(i, i ^ 1) for i in range(count)])  103 us
    ppermute x99, waiting for transfers between devices, collect(): parts.append(lax.ppermute(pair, 'sub', moves))  101 us
    reduce_sum x32, other arithmetic, apply_blocks(): result = jnp.sum(blocks[0] * picked[:, None, :], axis=2)  89.8 us
    gather x32, local copies, waits for them, and re-layouts, on_device(): others = whole.reshape(-1, width)[remote_cols]  24.8 us
    add x32, other arithmetic, on_device(): field = field + (rhs - result - capacity * field) / system_diag  22.4 us
    ppermute x33, starting transfers between devices, collect(): partner = lax.ppermute(value, 'sub', [(i, i ^ 1) for i in range(count)])  21.6 us
  transfers between devices with their start and end apart: 140, of which 132 were waited for; matrix products, arithmetic and copies ran while one was open for 4% of the time, Pallas kernels for 0%

profile of v7, /device:TPU:0, one launch (start us, length us, event | category | flops | bytes accessed | tf_op | source)
XLA Modules:
  0.0 537.2 jit_solution(11934985397233846826)
XLA Ops:
  0.6 3.1 collective-permute-start
  21.6 2.8 fusion
  25.9 3.2 collective-permute-done.4
  29.4 3.5 collective-permute-start.6
  41.9 3.2 collective-permute-done.8
  52.9 2.8 fusion.2
  57.1 3.2 collective-permute-done.12
  68.9 2.8 fusion.3
  73.1 3.2 collective-permute-done.16
  85.1 2.8 fusion.4
  89.3 3.2 collective-permute-done.20
  100.6 2.8 fusion.5
  104.8 3.2 collective-permute-done.24
  116.3 2.8 fusion.6
  120.5 3.2 collective-permute-done.28
  132.3 2.8 fusion.7
  136.6 3.1 collective-permute-done.32
  149.9 2.8 fusion.8
  154.8 3.2 collective-permute-done.38
  166.0 2.8 fusion.9
  170.3 3.2 collective-permute-done.42
  181.6 2.8 fusion.10
  185.8 3.2 collective-permute-done.46
  197.2 2.8 fusion.11
  201.4 3.2 collective-permute-done.50
  213.0 2.8 fusion.12
  217.2 3.2 collective-permute-done.54
  228.5 2.8 fusion.13
  232.8 3.2 collective-permute-done.58
  244.6 2.8 fusion.14
  248.8 3.2 collective-permute-done.62
  260.7 2.8 fusion.15
  264.9 3.2 collective-permute-done.66
  279.5 2.8 fusion.16
  284.4 3.2 collective-permute-done.72
  295.4 2.8 fusion.17
  299.6 3.2 collective-permute-done.76
  311.2 2.8 fusion.18
  315.4 3.2 collective-permute-done.80
  326.7 2.8 fusion.19
  330.9 3.2 collective-permute-done.84
  342.6 2.8 fusion.20
  346.8 3.2 collective-permute-done.88
  358.8 2.8 fusion.21
  362.9 3.3 collective-permute-done.92
  374.6 2.8 fusion.22
  378.8 3.2 collective-permute-done.96
  389.9 2.8 fusion.23
  394.1 3.2 collective-permute-done.100
  408.6 2.8 fusion.24
  413.6 3.2 collective-permute-done.106
  424.8 2.8 fusion.25
  429.0 3.3 collective-permute-done.110
  440.4 2.8 fusion.26
  444.7 3.2 collective-permute-done.114
  455.7 2.8 fusion.27
  459.9 3.3 collective-permute-done.118
  471.5 2.8 fusion.28
  475.8 3.2 collective-permute-done.122
  487.5 2.8 fusion.29
  491.7 3.2 collective-permute-done.126
  507.3 3.1 collective-permute-done.130
  518.4 2.8 fusion.31
  523.2 3.1 collective-permute-done.134
  (617 shorter events, 340.8 us)
Async XLA Ops:
  0.6 11.2 %collective-permute-start = (f32[32,128]{1,0:T(8,128)}, f32[32,128]{1,0:T(8,128)S(1)}, u32[]{:S(2)}, u32[]{:S(2)}) collective-permute-start(f32[32,128]{1,0:T(8,128)} %bitcast.631), channel_id=1, source_target_pairs={{0,1},{1,0},{2,3},{3,2},{4,5},{5,4},{6,7},{7,6},{8,9},{9,8},{10,11... | collective-permute-start | bytes 49160 | tf_op jit(solution)/shard_map/ppermute | solution.py:19
  12.6 6.2 %collective-permute-start.1 = (f32[2,32,128]{2,1,0:T(8,128)S(1)}, f32[2,32,128]{2,1,0:T(8,128)S(1)}, u32[]{:S(2)}, u32[]{:S(2)}) collective-permute-start(f32[2,32,128]{2,1,0:T(8,128)S(1)} %get-tuple-element.150), channel_id=1, source_target_pairs={{0,2},{1,3},{2,4},{3,5},{4,6},{5,7},{6,0},{7,1},{8,10},{9,11},{10,... | collective-permute-start | bytes 98312 | tf_op jit(solution)/shard_map/ppermute | solution.py:24
  14.2 5.2 collective-permute-start.2
  29.1 5.8 %collective-permute-start.5 = (f32[2,32,128]{2,1,0:T(8,128)S(1)}, f32[2,32,128]{2,1,0:T(8,128)S(1)}, u32[]{:S(2)}, u32[]{:S(2)}) collective-permute-start(f32[2,32,128]{2,1,0:T(8,128)S(1)} %get-tuple-element.148), channel_id=1, source_target_pairs={{0,2},{1,3},{2,4},{3,5},{4,6},{5,7},{6,0},{7,1},{8,10},{9,11},{10,... | collective-permute-start | bytes 98312 | tf_op jit(solution)/shard_map/ppermute | solution.py:24
  29.4 6.1 %collective-permute-start.6 = (f32[2,32,128]{2,1,0:T(8,128)S(1)}, f32[2,32,128]{2,1,0:T(8,128)S(1)}, u32[]{:S(2)}, u32[]{:S(2)}) collective-permute-start(f32[2,32,128]{2,1,0:T(8,128)S(1)} %get-tuple-element.148), channel_id=1, source_target_pairs={{0,4},{1,5},{2,6},{3,7},{4,0},{5,1},{6,2},{7,3},{8,12},{9,13},{10,... | collective-permute-start | bytes 98312 | tf_op jit(solution)/shard_map/ppermute | solution.py:24
  45.2 5.8 %collective-permute-start.9 = (f32[2,32,128]{2,1,0:T(8,128)S(1)}, f32[2,32,128]{2,1,0:T(8,128)S(1)}, u32[]{:S(2)}, u32[]{:S(2)}) collective-permute-start(f32[2,32,128]{2,1,0:T(8,128)S(1)} %get-tuple-element.146), channel_id=1, source_target_pairs={{0,2},{1,3},{2,4},{3,5},{4,6},{5,7},{6,0},{7,1},{8,10},{9,11},{10,... | collective-permute-start | bytes 98312 | tf_op jit(solution)/shard_map/ppermute | solution.py:24
  45.9 5.5 %collective-permute-start.10 = (f32[2,32,128]{2,1,0:T(8,128)S(1)}, f32[2,32,128]{2,1,0:T(8,128)S(1)}, u32[]{:S(2)}, u32[]{:S(2)}) collective-permute-start(f32[2,32,128]{2,1,0:T(8,128)S(1)} %get-tuple-element.146), channel_id=1, source_target_pairs={{0,4},{1,5},{2,6},{3,7},{4,0},{5,1},{6,2},{7,3},{8,12},{9,13},{10,... | collective-permute-start | bytes 98312 | tf_op jit(solution)/shard_map/ppermute | solution.py:24
  60.4 5.7 %collective-permute-start.13 = (f32[2,32,128]{2,1,0:T(8,128)S(1)}, f32[2,32,128]{2,1,0:T(8,128)S(1)}, u32[]{:S(2)}, u32[]{:S(2)}) collective-permute-start(f32[2,32,128]{2,1,0:T(8,128)S(1)} %get-tuple-element.144), channel_id=1, source_target_pairs={{0,2},{1,3},{2,4},{3,5},{4,6},{5,7},{6,0},{7,1},{8,10},{9,11},{10,... | collective-permute-start | bytes 98312 | tf_op jit(solution)/shard_map/ppermute | solution.py:24
  76.3 5.7 %collective-permute-start.17 = (f32[2,32,128]{2,1,0:T(8,128)S(1)}, f32[2,32,128]{2,1,0:T(8,128)S(1)}, u32[]{:S(2)}, u32[]{:S(2)}) collective-permute-start(f32[2,32,128]{2,1,0:T(8,128)S(1)} %get-tuple-element.142), channel_id=1, source_target_pairs={{0,2},{1,3},{2,4},{3,5},{4,6},{5,7},{6,0},{7,1},{8,10},{9,11},{10,... | collective-permute-start | bytes 98312 | tf_op jit(solution)/shard_map/ppermute | solution.py:24
  77.2 6.6 %collective-permute-start.18 = (f32[2,32,128]{2,1,0:T(8,128)S(1)}, f32[2,32,128]{2,1,0:T(8,128)S(1)}, u32[]{:S(2)}, u32[]{:S(2)}) collective-permute-start(f32[2,32,128]{2,1,0:T(8,128)S(1)} %get-tuple-element.142), channel_id=1, source_target_pairs={{0,4},{1,5},{2,6},{3,7},{4,0},{5,1},{6,2},{7,3},{8,12},{9,13},{10,... | collective-permute-start | bytes 98312 | tf_op jit(solution)/shard_map/ppermute | solution.py:24
  92.6 5.7 %collective-permute-start.21 = (f32[2,32,128]{2,1,0:T(8,128)S(1)}, f32[2,32,128]{2,1,0:T(8,128)S(1)}, u32[]{:S(2)}, u32[]{:S(2)}) collective-permute-start(f32[2,32,128]{2,1,0:T(8,128)S(1)} %get-tuple-element.140), channel_id=1, source_target_pairs={{0,2},{1,3},{2,4},{3,5},{4,6},{5,7},{6,0},{7,1},{8,10},{9,11},{10,... | collective-permute-start | bytes 98312 | tf_op jit(solution)/shard_map/ppermute | solution.py:24
  93.5 5.4 %collective-permute-start.22 = (f32[2,32,128]{2,1,0:T(8,128)S(1)}, f32[2,32,128]{2,1,0:T(8,128)S(1)}, u32[]{:S(2)}, u32[]{:S(2)}) collective-permute-start(f32[2,32,128]{2,1,0:T(8,128)S(1)} %get-tuple-element.140), channel_id=1, source_target_pairs={{0,4},{1,5},{2,6},{3,7},{4,0},{5,1},{6,2},{7,3},{8,12},{9,13},{10,... | collective-permute-start | bytes 98312 | tf_op jit(solution)/shard_map/ppermute | solution.py:24
  108.0 5.7 %collective-permute-start.25 = (f32[2,32,128]{2,1,0:T(8,128)S(1)}, f32[2,32,128]{2,1,0:T(8,128)S(1)}, u32[]{:S(2)}, u32[]{:S(2)}) collective-permute-start(f32[2,32,128]{2,1,0:T(8,128)S(1)} %get-tuple-element.138), channel_id=1, source_target_pairs={{0,2},{1,3},{2,4},{3,5},{4,6},{5,7},{6,0},{7,1},{8,10},{9,11},{10,... | collective-permute-start | bytes 98312 | tf_op jit(solution)/shard_map/ppermute | solution.py:24
  123.7 5.7 %collective-permute-start.29 = (f32[2,32,128]{2,1,0:T(8,128)S(1)}, f32[2,32,128]{2,1,0:T(8,128)S(1)}, u32[]{:S(2)}, u32[]{:S(2)}) collective-permute-start(f32[2,32,128]{2,1,0:T(8,128)S(1)} %get-tuple-element.136), channel_id=1, source_target_pairs={{0,2},{1,3},{2,4},{3,5},{4,6},{5,7},{6,0},{7,1},{8,10},{9,11},{10,... | collective-permute-start | bytes 98312 | tf_op jit(solution)/shard_map/ppermute | solution.py:24
  125.0 5.2 collective-permute-start.30
  139.8 5.7 %collective-permute-start.33 = (f32[2,32,128]{2,1,0:T(8,128)S(1)}, f32[2,32,128]{2,1,0:T(8,128)S(1)}, u32[]{:S(2)}, u32[]{:S(2)}) collective-permute-start(f32[2,32,128]{2,1,0:T(8,128)S(1)} %get-tuple-element.134), channel_id=1, source_target_pairs={{0,2},{1,3},{2,4},{3,5},{4,6},{5,7},{6,0},{7,1},{8,10},{9,11},{10,... | collective-permute-start | bytes 98312 | tf_op jit(solution)/shard_map/ppermute | solution.py:24
  141.0 5.2 collective-permute-start.34
  158.0 5.9 %collective-permute-start.39 = (f32[2,32,128]{2,1,0:T(8,128)S(1)}, f32[2,32,128]{2,1,0:T(8,128)S(1)}, u32[]{:S(2)}, u32[]{:S(2)}) collective-permute-start(f32[2,32,128]{2,1,0:T(8,128)S(1)} %get-tuple-element.132), channel_id=1, source_target_pairs={{0,2},{1,3},{2,4},{3,5},{4,6},{5,7},{6,0},{7,1},{8,10},{9,11},{10,... | collective-permute-start | bytes 98312 | tf_op jit(solution)/shard_map/ppermute | solution.py:24
  159.1 5.7 %collective-permute-start.40 = (f32[2,32,128]{2,1,0:T(8,128)S(1)}, f32[2,32,128]{2,1,0:T(8,128)S(1)}, u32[]{:S(2)}, u32[]{:S(2)}) collective-permute-start(f32[2,32,128]{2,1,0:T(8,128)S(1)} %get-tuple-element.132), channel_id=1, source_target_pairs={{0,4},{1,5},{2,6},{3,7},{4,0},{5,1},{6,2},{7,3},{8,12},{9,13},{10,... | collective-permute-start | bytes 98312 | tf_op jit(solution)/shard_map/ppermute | solution.py:24
  173.5 5.7 %collective-permute-start.43 = (f32[2,32,128]{2,1,0:T(8,128)S(1)}, f32[2,32,128]{2,1,0:T(8,128)S(1)}, u32[]{:S(2)}, u32[]{:S(2)}) collective-permute-start(f32[2,32,128]{2,1,0:T(8,128)S(1)} %get-tuple-element.130), channel_id=1, source_target_pairs={{0,2},{1,3},{2,4},{3,5},{4,6},{5,7},{6,0},{7,1},{8,10},{9,11},{10,... | collective-permute-start | bytes 98312 | tf_op jit(solution)/shard_map/ppermute | solution.py:24
  174.8 5.1 collective-permute-start.44
  189.0 5.7 %collective-permute-start.47 = (f32[2,32,128]{2,1,0:T(8,128)S(1)}, f32[2,32,128]{2,1,0:T(8,128)S(1)}, u32[]{:S(2)}, u32[]{:S(2)}) collective-permute-start(f32[2,32,128]{2,1,0:T(8,128)S(1)} %get-tuple-element.128), channel_id=1, source_target_pairs={{0,2},{1,3},{2,4},{3,5},{4,6},{5,7},{6,0},{7,1},{8,10},{9,11},{10,... | collective-permute-start | bytes 98312 | tf_op jit(solution)/shard_map/ppermute | solution.py:24
  190.3 5.1 collective-permute-start.48
  204.6 5.7 %collective-permute-start.51 = (f32[2,32,128]{2,1,0:T(8,128)S(1)}, f32[2,32,128]{2,1,0:T(8,128)S(1)}, u32[]{:S(2)}, u32[]{:S(2)}) collective-permute-start(f32[2,32,128]{2,1,0:T(8,128)S(1)} %get-tuple-element.126), channel_id=1, source_target_pairs={{0,2},{1,3},{2,4},{3,5},{4,6},{5,7},{6,0},{7,1},{8,10},{9,11},{10,... | collective-permute-start | bytes 98312 | tf_op jit(solution)/shard_map/ppermute | solution.py:24
  205.9 5.2 collective-permute-start.52
  220.4 5.7 %collective-permute-start.55 = (f32[2,32,128]{2,1,0:T(8,128)S(1)}, f32[2,32,128]{2,1,0:T(8,128)S(1)}, u32[]{:S(2)}, u32[]{:S(2)}) collective-permute-start(f32[2,32,128]{2,1,0:T(8,128)S(1)} %get-tuple-element.124), channel_id=1, source_target_pairs={{0,2},{1,3},{2,4},{3,5},{4,6},{5,7},{6,0},{7,1},{8,10},{9,11},{10,... | collective-permute-start | bytes 98312 | tf_op jit(solution)/shard_map/ppermute | solution.py:24
  221.5 5.3 collective-permute-start.56
  236.0 6.1 %collective-permute-start.59 = (f32[2,32,128]{2,1,0:T(8,128)S(1)}, f32[2,32,128]{2,1,0:T(8,128)S(1)}, u32[]{:S(2)}, u32[]{:S(2)}) collective-permute-start(f32[2,32,128]{2,1,0:T(8,128)S(1)} %get-tuple-element.122), channel_id=1, source_target_pairs={{0,2},{1,3},{2,4},{3,5},{4,6},{5,7},{6,0},{7,1},{8,10},{9,11},{10,... | collective-permute-start | bytes 98312 | tf_op jit(solution)/shard_map/ppermute | solution.py:24
  238.2 5.1 collective-permute-start.60
  252.0 5.7 %collective-permute-start.63 = (f32[2,32,128]{2,1,0:T(8,128)S(1)}, f32[2,32,128]{2,1,0:T(8,128)S(1)}, u32[]{:S(2)}, u32[]{:S(2)}) collective-permute-start(f32[2,32,128]{2,1,0:T(8,128)S(1)} %get-tuple-element.120), channel_id=1, source_target_pairs={{0,2},{1,3},{2,4},{3,5},{4,6},{5,7},{6,0},{7,1},{8,10},{9,11},{10,... | collective-permute-start | bytes 98312 | tf_op jit(solution)/shard_map/ppermute | solution.py:24
  253.0 5.1 collective-permute-start.64
  268.1 5.8 %collective-permute-start.67 = (f32[2,32,128]{2,1,0:T(8,128)S(1)}, f32[2,32,128]{2,1,0:T(8,128)S(1)}, u32[]{:S(2)}, u32[]{:S(2)}) collective-permute-start(f32[2,32,128]{2,1,0:T(8,128)S(1)} %get-tuple-element.118), channel_id=1, source_target_pairs={{0,2},{1,3},{2,4},{3,5},{4,6},{5,7},{6,0},{7,1},{8,10},{9,11},{10,... | collective-permute-start | bytes 98312 | tf_op jit(solution)/shard_map/ppermute | solution.py:24
  268.9 5.5 %collective-permute-start.68 = (f32[2,32,128]{2,1,0:T(8,128)S(1)}, f32[2,32,128]{2,1,0:T(8,128)S(1)}, u32[]{:S(2)}, u32[]{:S(2)}) collective-permute-start(f32[2,32,128]{2,1,0:T(8,128)S(1)} %get-tuple-element.118), channel_id=1, source_target_pairs={{0,4},{1,5},{2,6},{3,7},{4,0},{5,1},{6,2},{7,3},{8,12},{9,13},{10,... | collective-permute-start | bytes 98312 | tf_op jit(solution)/shard_map/ppermute | solution.py:24
  276.8 5.6 %collective-permute-start.71 = (f32[1,64]{1,0:T(1,128)S(1)}, f32[1,64]{1,0:T(1,128)S(1)}, u32[]{:S(2)}, u32[]{:S(2)}) collective-permute-start(f32[1,64]{1,0:T(1,128)S(1)} %fusion.51), channel_id=1, source_target_pairs={{0,8},{8,16},{16,24},{24,0},{1,9},{9,17},{17,25},{25,1},{2,10},{10... | collective-permute-start | bytes 776 | tf_op jit(solution)/shard_map/ppermute | solution.py:13
  276.9 5.5 %collective-permute-start.70 = (f32[1,2,64]{2,1,0:T(2,128)S(1)}, f32[1,2,64]{2,1,0:T(2,128)S(1)}, u32[]{:S(2)}, u32[]{:S(2)}) collective-permute-start(f32[1,2,64]{2,1,0:T(2,128)S(1)} %pad_maximum_fusion.98), channel_id=1, source_target_pairs={{0,24},{8,0},{16,8},{24,16},{1,25},{9,1},{17,9},{25,17},{2,26},{10... | collective-permute-start | bytes 1544 | tf_op jit(solution)/shard_map/ppermute | solution.py:13
  287.7 5.7 %collective-permute-start.73 = (f32[2,32,128]{2,1,0:T(8,128)S(1)}, f32[2,32,128]{2,1,0:T(8,128)S(1)}, u32[]{:S(2)}, u32[]{:S(2)}) collective-permute-start(f32[2,32,128]{2,1,0:T(8,128)S(1)} %get-tuple-element.116), channel_id=1, source_target_pairs={{0,2},{1,3},{2,4},{3,5},{4,6},{5,7},{6,0},{7,1},{8,10},{9,11},{10,... | collective-permute-start | bytes 98312 | tf_op jit(solution)/shard_map/ppermute | solution.py:24
  288.6 5.4 %collective-permute-start.74 = (f32[2,32,128]{2,1,0:T(8,128)S(1)}, f32[2,32,128]{2,1,0:T(8,128)S(1)}, u32[]{:S(2)}, u32[]{:S(2)}) collective-permute-start(f32[2,32,128]{2,1,0:T(8,128)S(1)} %get-tuple-element.116), channel_id=1, source_target_pairs={{0,4},{1,5},{2,6},{3,7},{4,0},{5,1},{6,2},{7,3},{8,12},{9,13},{10,... | collective-permute-start | bytes 98312 | tf_op jit(solution)/shard_map/ppermute | solution.py:24
  302.8 5.7 %collective-permute-start.77 = (f32[2,32,128]{2,1,0:T(8,128)S(1)}, f32[2,32,128]{2,1,0:T(8,128)S(1)}, u32[]{:S(2)}, u32[]{:S(2)}) collective-permute-start(f32[2,32,128]{2,1,0:T(8,128)S(1)} %get-tuple-element.114), channel_id=1, source_target_pairs={{0,2},{1,3},{2,4},{3,5},{4,6},{5,7},{6,0},{7,1},{8,10},{9,11},{10,... | collective-permute-start | bytes 98312 | tf_op jit(solution)/shard_map/ppermute | solution.py:24
  318.7 5.7 %collective-permute-start.81 = (f32[2,32,128]{2,1,0:T(8,128)S(1)}, f32[2,32,128]{2,1,0:T(8,128)S(1)}, u32[]{:S(2)}, u32[]{:S(2)}) collective-permute-start(f32[2,32,128]{2,1,0:T(8,128)S(1)} %get-tuple-element.112), channel_id=1, source_target_pairs={{0,2},{1,3},{2,4},{3,5},{4,6},{5,7},{6,0},{7,1},{8,10},{9,11},{10,... | collective-permute-start | bytes 98312 | tf_op jit(solution)/shard_map/ppermute | solution.py:24
  319.7 5.4 collective-permute-start.82
  334.1 5.7 %collective-permute-start.85 = (f32[2,32,128]{2,1,0:T(8,128)S(1)}, f32[2,32,128]{2,1,0:T(8,128)S(1)}, u32[]{:S(2)}, u32[]{:S(2)}) collective-permute-start(f32[2,32,128]{2,1,0:T(8,128)S(1)} %get-tuple-element.110), channel_id=1, source_target_pairs={{0,2},{1,3},{2,4},{3,5},{4,6},{5,7},{6,0},{7,1},{8,10},{9,11},{10,... | collective-permute-start | bytes 98312 | tf_op jit(solution)/shard_map/ppermute | solution.py:24
  350.0 5.9 %collective-permute-start.89 = (f32[2,32,128]{2,1,0:T(8,128)S(1)}, f32[2,32,128]{2,1,0:T(8,128)S(1)}, u32[]{:S(2)}, u32[]{:S(2)}) collective-permute-start(f32[2,32,128]{2,1,0:T(8,128)S(1)} %get-tuple-element.108), channel_id=1, source_target_pairs={{0,2},{1,3},{2,4},{3,5},{4,6},{5,7},{6,0},{7,1},{8,10},{9,11},{10,... | collective-permute-start | bytes 98312 | tf_op jit(solution)/shard_map/ppermute | solution.py:24
  351.0 6.6 %collective-permute-start.90 = (f32[2,32,128]{2,1,0:T(8,128)S(1)}, f32[2,32,128]{2,1,0:T(8,128)S(1)}, u32[]{:S(2)}, u32[]{:S(2)}) collective-permute-start(f32[2,32,128]{2,1,0:T(8,128)S(1)} %get-tuple-element.108), channel_id=1, source_target_pairs={{0,4},{1,5},{2,6},{3,7},{4,0},{5,1},{6,2},{7,3},{8,12},{9,13},{10,... | collective-permute-start | bytes 98312 | tf_op jit(solution)/shard_map/ppermute | solution.py:24
  366.2 5.7 %collective-permute-start.93 = (f32[2,32,128]{2,1,0:T(8,128)S(1)}, f32[2,32,128]{2,1,0:T(8,128)S(1)}, u32[]{:S(2)}, u32[]{:S(2)}) collective-permute-start(f32[2,32,128]{2,1,0:T(8,128)S(1)} %get-tuple-element.106), channel_id=1, source_target_pairs={{0,2},{1,3},{2,4},{3,5},{4,6},{5,7},{6,0},{7,1},{8,10},{9,11},{10,... | collective-permute-start | bytes 98312 | tf_op jit(solution)/shard_map/ppermute | solution.py:24
  367.3 5.4 collective-permute-start.94
  382.0 5.7 %collective-permute-start.97 = (f32[2,32,128]{2,1,0:T(8,128)S(1)}, f32[2,32,128]{2,1,0:T(8,128)S(1)}, u32[]{:S(2)}, u32[]{:S(2)}) collective-permute-start(f32[2,32,128]{2,1,0:T(8,128)S(1)} %get-tuple-element.104), channel_id=1, source_target_pairs={{0,2},{1,3},{2,4},{3,5},{4,6},{5,7},{6,0},{7,1},{8,10},{9,11},{10,... | collective-permute-start | bytes 98312 | tf_op jit(solution)/shard_map/ppermute | solution.py:24
  383.1 5.3 collective-permute-start.98
  397.3 5.7 %collective-permute-start.101 = (f32[2,32,128]{2,1,0:T(8,128)S(1)}, f32[2,32,128]{2,1,0:T(8,128)S(1)}, u32[]{:S(2)}, u32[]{:S(2)}) collective-permute-start(f32[2,32,128]{2,1,0:T(8,128)S(1)} %get-tuple-element.102), channel_id=1, source_target_pairs={{0,2},{1,3},{2,4},{3,5},{4,6},{5,7},{6,0},{7,1},{8,10},{9,11},{10,... | collective-permute-start | bytes 98312 | tf_op jit(solution)/shard_map/ppermute | solution.py:24
  405.9 5.6 %collective-permute-start.105 = (f32[1,64]{1,0:T(1,128)S(1)}, f32[1,64]{1,0:T(1,128)S(1)}, u32[]{:S(2)}, u32[]{:S(2)}) collective-permute-start(f32[1,64]{1,0:T(1,128)S(1)} %fusion.50), channel_id=1, source_target_pairs={{0,8},{8,16},{16,24},{24,0},{1,9},{9,17},{17,25},{25,1},{2,10},{10... | collective-permute-start | bytes 776 | tf_op jit(solution)/shard_map/ppermute | solution.py:13
  406.0 5.5 %collective-permute-start.104 = (f32[1,2,64]{2,1,0:T(2,128)S(1)}, f32[1,2,64]{2,1,0:T(2,128)S(1)}, u32[]{:S(2)}, u32[]{:S(2)}) collective-permute-start(f32[1,2,64]{2,1,0:T(2,128)S(1)} %pad_maximum_fusion.99), channel_id=1, source_target_pairs={{0,24},{8,0},{16,8},{24,16},{1,25},{9,1},{17,9},{25,17},{2,26},{10... | collective-permute-start | bytes 1544 | tf_op jit(solution)/shard_map/ppermute | solution.py:13
  416.8 5.7 %collective-permute-start.107 = (f32[2,32,128]{2,1,0:T(8,128)S(1)}, f32[2,32,128]{2,1,0:T(8,128)S(1)}, u32[]{:S(2)}, u32[]{:S(2)}) collective-permute-start(f32[2,32,128]{2,1,0:T(8,128)S(1)} %get-tuple-element.100), channel_id=1, source_target_pairs={{0,2},{1,3},{2,4},{3,5},{4,6},{5,7},{6,0},{7,1},{8,10},{9,11},{10,... | collective-permute-start | bytes 98312 | tf_op jit(solution)/shard_map/ppermute | solution.py:24
  417.9 5.3 collective-permute-start.108
  432.2 5.7 %collective-permute-start.111 = (f32[2,32,128]{2,1,0:T(8,128)S(1)}, f32[2,32,128]{2,1,0:T(8,128)S(1)}, u32[]{:S(2)}, u32[]{:S(2)}) collective-permute-start(f32[2,32,128]{2,1,0:T(8,128)S(1)} %get-tuple-element.98), channel_id=1, source_target_pairs={{0,2},{1,3},{2,4},{3,5},{4,6},{5,7},{6,0},{7,1},{8,10},{9,11},{10,... | collective-permute-start | bytes 98312 | tf_op jit(solution)/shard_map/ppermute | solution.py:24
  433.5 5.1 collective-permute-start.112
  447.9 5.7 %collective-permute-start.115 = (f32[2,32,128]{2,1,0:T(8,128)S(1)}, f32[2,32,128]{2,1,0:T(8,128)S(1)}, u32[]{:S(2)}, u32[]{:S(2)}) collective-permute-start(f32[2,32,128]{2,1,0:T(8,128)S(1)} %get-tuple-element.96), channel_id=1, source_target_pairs={{0,2},{1,3},{2,4},{3,5},{4,6},{5,7},{6,0},{7,1},{8,10},{9,11},{10,... | collective-permute-start | bytes 98312 | tf_op jit(solution)/shard_map/ppermute | solution.py:24
  448.9 5.3 collective-permute-start.116
  463.2 5.7 %collective-permute-start.119 = (f32[2,32,128]{2,1,0:T(8,128)S(1)}, f32[2,32,128]{2,1,0:T(8,128)S(1)}, u32[]{:S(2)}, u32[]{:S(2)}) collective-permute-start(f32[2,32,128]{2,1,0:T(8,128)S(1)} %get-tuple-element.94), channel_id=1, source_target_pairs={{0,2},{1,3},{2,4},{3,5},{4,6},{5,7},{6,0},{7,1},{8,10},{9,11},{10,... | collective-permute-start | bytes 98312 | tf_op jit(solution)/shard_map/ppermute | solution.py:24
  479.0 6.2 %collective-permute-start.123 = (f32[2,32,128]{2,1,0:T(8,128)S(1)}, f32[2,32,128]{2,1,0:T(8,128)S(1)}, u32[]{:S(2)}, u32[]{:S(2)}) collective-permute-start(f32[2,32,128]{2,1,0:T(8,128)S(1)} %get-tuple-element.92), channel_id=1, source_target_pairs={{0,2},{1,3},{2,4},{3,5},{4,6},{5,7},{6,0},{7,1},{8,10},{9,11},{10,... | collective-permute-start | bytes 98312 | tf_op jit(solution)/shard_map/ppermute | solution.py:24
  480.1 6.4 %collective-permute-start.124 = (f32[2,32,128]{2,1,0:T(8,128)S(1)}, f32[2,32,128]{2,1,0:T(8,128)S(1)}, u32[]{:S(2)}, u32[]{:S(2)}) collective-permute-start(f32[2,32,128]{2,1,0:T(8,128)S(1)} %get-tuple-element.92), channel_id=1, source_target_pairs={{0,4},{1,5},{2,6},{3,7},{4,0},{5,1},{6,2},{7,3},{8,12},{9,13},{10,... | collective-permute-start | bytes 98312 | tf_op jit(solution)/shard_map/ppermute | solution.py:24
  495.0 5.7 %collective-permute-start.127 = (f32[2,32,128]{2,1,0:T(8,128)S(1)}, f32[2,32,128]{2,1,0:T(8,128)S(1)}, u32[]{:S(2)}, u32[]{:S(2)}) collective-permute-start(f32[2,32,128]{2,1,0:T(8,128)S(1)} %get-tuple-element.90), channel_id=1, source_target_pairs={{0,2},{1,3},{2,4},{3,5},{4,6},{5,7},{6,0},{7,1},{8,10},{9,11},{10,... | collective-permute-start | bytes 98312 | tf_op jit(solution)/shard_map/ppermute | solution.py:24
  495.9 5.5 %collective-permute-start.128 = (f32[2,32,128]{2,1,0:T(8,128)S(1)}, f32[2,32,128]{2,1,0:T(8,128)S(1)}, u32[]{:S(2)}, u32[]{:S(2)}) collective-permute-start(f32[2,32,128]{2,1,0:T(8,128)S(1)} %get-tuple-element.90), channel_id=1, source_target_pairs={{0,4},{1,5},{2,6},{3,7},{4,0},{5,1},{6,2},{7,3},{8,12},{9,13},{10,... | collective-permute-start | bytes 98312 | tf_op jit(solution)/shard_map/ppermute | solution.py:24
  510.4 5.7 %collective-permute-start.131 = (f32[2,32,128]{2,1,0:T(8,128)S(1)}, f32[2,32,128]{2,1,0:T(8,128)S(1)}, u32[]{:S(2)}, u32[]{:S(2)}) collective-permute-start(f32[2,32,128]{2,1,0:T(8,128)S(1)} %get-tuple-element.88), channel_id=1, source_target_pairs={{0,2},{1,3},{2,4},{3,5},{4,6},{5,7},{6,0},{7,1},{8,10},{9,11},{10,... | collective-permute-start | bytes 98312 | tf_op jit(solution)/shard_map/ppermute | solution.py:24
  511.7 5.1 collective-permute-start.132
  526.2 5.4 %collective-permute-start.135 = (f32[2,1,2,64]{3,2,1,0:T(2,128)S(1)}, f32[2,1,2,64]{3,2,1,0:T(2,128)S(1)}, u32[]{:S(2)}, u32[]{:S(2)}) collective-permute-start(f32[2,1,2,64]{3,2,1,0:T(2,128)S(1)} %pad_maximum_fusion.96), channel_id=1, source_target_pairs={{0,2},{1,3},{2,4},{3,5},{4,6},{5,7},{6,0},{7,1},{8,10},{9,11},{10,... | collective-permute-start | bytes 3080 | tf_op jit(solution)/shard_map/ppermute | solution.py:24
  (86 other events, 515.7 us)

commit v8 on v7

--- a/solution.py
+++ b/solution.py
@@ -84,7 +84,9 @@
             field = field + (rhs - result - capacity * field) / system_diag
         volt = field
     partial_volt = jnp.where(inside, volt[0][safe_ends[0]][None], 0.0)
-    end_volt = jnp.sum(collect(partial_volt), axis=0)
+    count = lax.axis_size("sub")
+    copies = jnp.broadcast_to(partial_volt[None], (count,) + partial_volt.shape)
+    end_volt = jnp.sum(lax.all_to_all(copies, "sub", 0, 0, tiled=True), axis=0)
     hist = next_hist(end_volt, hist, surge)
     return (volt, hist)
 

time: 547 us -> 549 us (level)
  blocking collectives: 0 us -> 10.2 us
  waiting for transfers between devices: 207 us -> 201 us
    all_to_all x0 -> x1, blocking collectives: none -> 10.2 us  [on_device(): end_volt = jnp.sum(lax.all_to_all(copies, 'sub', 0, 0, tiled=True), axis=0)]
    ppermute x99 -> x96, starting transfers between devices: 134 us -> 130 us  [collect(): parts.append(lax.ppermute(pair, 'sub', moves))]
    ppermute x33 -> x32, waiting for transfers between devices: 103 us -> 100 us  [collect(): partner = lax.ppermute(value, 'sub', [(i, i ^ 1) for i in range(count)])]
    ppermute x99 -> x96, waiting for transfers between devices: 101 us -> 98.7 us  [collect(): parts.append(lax.ppermute(pair, 'sub', moves))]
    ppermute x33 -> x32, starting transfers between devices: 21.6 us -> 20.9 us  [collect(): partner = lax.ppermute(value, 'sub', [(i, i ^ 1) for i in range(count)])]
  transfers between devices with their start and end apart: 140 -> 136, of which waited for: 132 -> 126; matrix products, arithmetic and copies ran while one was open for 4% -> 4% of each run, Pallas kernels for 0% -> 0%
where the time goes in v8:
time: 549 us; the launch traced here: 538 us
  waiting for transfers between devices  201 us (37%)
  starting transfers between devices  155 us (28%)
  other arithmetic  126 us (23%)
  local copies, waits for them, and re-layouts  43.3 us (8%)
  blocking collectives  10.2 us (2%)
    ppermute x96, starting transfers between devices, collect(): parts.append(lax.ppermute(pair, 'sub', moves))  130 us
    ppermute x32, waiting for transfers between devices, collect(): partner = lax.ppermute(value, 'sub', [(i, i ^ 1) for i in range(count)])  100 us
    ppermute x96, waiting for transfers between devices, collect(): parts.append(lax.ppermute(pair, 'sub', moves))  98.7 us
    reduce_sum x32, other arithmetic, apply_blocks(): result = jnp.sum(blocks[0] * picked[:, None, :], axis=2)  89.8 us
    gather x32, local copies, waits for them, and re-layouts, on_device(): others = whole.reshape(-1, width)[remote_cols]  24.7 us
    add x32, other arithmetic, on_device(): field = field + (rhs - result - capacity * field) / system_diag  22.4 us
    ppermute x32, starting transfers between devices, collect(): partner = lax.ppermute(value, 'sub', [(i, i ^ 1) for i in range(count)])  20.9 us
  transfers between devices with their start and end apart: 136, of which 126 were waited for; matrix products, arithmetic and copies ran while one was open for 4% of the time, Pallas kernels for 0%

profile of v8, /device:TPU:0, one launch (start us, length us, event | category | flops | bytes accessed | tf_op | source)
XLA Modules:
  0.0 538.4 jit_solution(8666308091249147463)
XLA Ops:
  0.6 3.1 collective-permute-start
  21.6 2.8 fusion
  25.9 3.2 collective-permute-done.4
  29.4 3.5 collective-permute-start.6
  42.0 3.2 collective-permute-done.8
  52.9 2.8 fusion.2
  57.1 3.2 collective-permute-done.12
  68.9 2.8 fusion.3
  73.1 3.2 collective-permute-done.16
  85.1 2.8 fusion.4
  89.3 3.2 collective-permute-done.20
  100.6 2.8 fusion.5
  104.8 3.2 collective-permute-done.24
  116.3 2.8 fusion.6
  120.5 3.2 collective-permute-done.28
  132.4 2.8 fusion.7
  136.6 3.2 collective-permute-done.32
  149.9 2.8 fusion.8
  154.8 3.2 collective-permute-done.38
  166.1 2.8 fusion.9
  170.3 3.2 collective-permute-done.42
  181.6 2.8 fusion.10
  185.8 3.2 collective-permute-done.46
  197.2 2.8 fusion.11
  201.4 3.2 collective-permute-done.50
  213.0 2.8 fusion.12
  217.2 3.2 collective-permute-done.54
  228.6 2.8 fusion.13
  232.8 3.2 collective-permute-done.58
  244.6 2.8 fusion.14
  248.8 3.2 collective-permute-done.62
  260.7 2.8 fusion.15
  264.9 3.2 collective-permute-done.66
  279.5 2.8 fusion.16
  284.4 3.2 collective-permute-done.72
  295.4 2.8 fusion.17
  299.6 3.2 collective-permute-done.76
  311.2 2.8 fusion.18
  315.4 3.2 collective-permute-done.80
  326.7 2.8 fusion.19
  330.9 3.2 collective-permute-done.84
  342.6 2.8 fusion.20
  346.8 3.2 collective-permute-done.88
  358.7 2.8 fusion.21
  363.0 3.2 collective-permute-done.92
  374.6 2.8 fusion.22
  378.8 3.2 collective-permute-done.96
  389.9 2.8 fusion.23
  394.1 3.2 collective-permute-done.100
  408.6 2.8 fusion.24
  413.6 3.2 collective-permute-done.106
  424.8 2.8 fusion.25
  429.0 3.2 collective-permute-done.110
  440.5 2.8 fusion.26
  444.7 3.2 collective-permute-done.114
  455.7 2.8 fusion.27
  459.9 3.2 collective-permute-done.118
  471.6 2.8 fusion.28
  475.7 3.2 collective-permute-done.122
  487.5 2.8 fusion.29
  491.8 3.2 collective-permute-done.126
  503.0 2.8 fusion.30
  507.3 3.2 collective-permute-done.130
  522.7 10.2 %all_to_all.5 = f32[8,1,128]{2,1,0:T(1,128)S(1)} all-to-all(f32[8,1,128]{2,1,0:T(1,128)S(1)} %reshape.1588), channel_id=1, replica_groups=mesh['area'=4,'sub'=8] {'sub'}, dimensions={0} | all-to-all | bytes 8192 | tf_op jit(solution)/shard_map/all_to_all | solution.py:89
  (611 shorter events, 334.7 us)
Async XLA Ops:
  0.6 11.2 %collective-permute-start = (f32[32,128]{1,0:T(8,128)}, f32[32,128]{1,0:T(8,128)S(1)}, u32[]{:S(2)}, u32[]{:S(2)}) collective-permute-start(f32[32,128]{1,0:T(8,128)} %bitcast.622), channel_id=1, source_target_pairs={{0,1},{1,0},{2,3},{3,2},{4,5},{5,4},{6,7},{7,6},{8,9},{9,8},{10,11... | collective-permute-start | bytes 49160 | tf_op jit(solution)/shard_map/ppermute | solution.py:19
  12.6 6.2 %collective-permute-start.1 = (f32[2,32,128]{2,1,0:T(8,128)S(1)}, f32[2,32,128]{2,1,0:T(8,128)S(1)}, u32[]{:S(2)}, u32[]{:S(2)}) collective-permute-start(f32[2,32,128]{2,1,0:T(8,128)S(1)} %get-tuple-element.150), channel_id=1, source_target_pairs={{0,2},{1,3},{2,4},{3,5},{4,6},{5,7},{6,0},{7,1},{8,10},{9,11},{10,... | collective-permute-start | bytes 98312 | tf_op jit(solution)/shard_map/ppermute | solution.py:24
  14.2 5.2 collective-permute-start.2
  29.1 5.8 %collective-permute-start.5 = (f32[2,32,128]{2,1,0:T(8,128)S(1)}, f32[2,32,128]{2,1,0:T(8,128)S(1)}, u32[]{:S(2)}, u32[]{:S(2)}) collective-permute-start(f32[2,32,128]{2,1,0:T(8,128)S(1)} %get-tuple-element.148), channel_id=1, source_target_pairs={{0,2},{1,3},{2,4},{3,5},{4,6},{5,7},{6,0},{7,1},{8,10},{9,11},{10,... | collective-permute-start | bytes 98312 | tf_op jit(solution)/shard_map/ppermute | solution.py:24
  29.4 6.1 %collective-permute-start.6 = (f32[2,32,128]{2,1,0:T(8,128)S(1)}, f32[2,32,128]{2,1,0:T(8,128)S(1)}, u32[]{:S(2)}, u32[]{:S(2)}) collective-permute-start(f32[2,32,128]{2,1,0:T(8,128)S(1)} %get-tuple-element.148), channel_id=1, source_target_pairs={{0,4},{1,5},{2,6},{3,7},{4,0},{5,1},{6,2},{7,3},{8,12},{9,13},{10,... | collective-permute-start | bytes 98312 | tf_op jit(solution)/shard_map/ppermute | solution.py:24
  45.2 5.8 %collective-permute-start.9 = (f32[2,32,128]{2,1,0:T(8,128)S(1)}, f32[2,32,128]{2,1,0:T(8,128)S(1)}, u32[]{:S(2)}, u32[]{:S(2)}) collective-permute-start(f32[2,32,128]{2,1,0:T(8,128)S(1)} %get-tuple-element.146), channel_id=1, source_target_pairs={{0,2},{1,3},{2,4},{3,5},{4,6},{5,7},{6,0},{7,1},{8,10},{9,11},{10,... | collective-permute-start | bytes 98312 | tf_op jit(solution)/shard_map/ppermute | solution.py:24
  45.9 5.5 %collective-permute-start.10 = (f32[2,32,128]{2,1,0:T(8,128)S(1)}, f32[2,32,128]{2,1,0:T(8,128)S(1)}, u32[]{:S(2)}, u32[]{:S(2)}) collective-permute-start(f32[2,32,128]{2,1,0:T(8,128)S(1)} %get-tuple-element.146), channel_id=1, source_target_pairs={{0,4},{1,5},{2,6},{3,7},{4,0},{5,1},{6,2},{7,3},{8,12},{9,13},{10,... | collective-permute-start | bytes 98312 | tf_op jit(solution)/shard_map/ppermute | solution.py:24
  60.4 5.7 %collective-permute-start.13 = (f32[2,32,128]{2,1,0:T(8,128)S(1)}, f32[2,32,128]{2,1,0:T(8,128)S(1)}, u32[]{:S(2)}, u32[]{:S(2)}) collective-permute-start(f32[2,32,128]{2,1,0:T(8,128)S(1)} %get-tuple-element.144), channel_id=1, source_target_pairs={{0,2},{1,3},{2,4},{3,5},{4,6},{5,7},{6,0},{7,1},{8,10},{9,11},{10,... | collective-permute-start | bytes 98312 | tf_op jit(solution)/shard_map/ppermute | solution.py:24
  76.3 5.7 %collective-permute-start.17 = (f32[2,32,128]{2,1,0:T(8,128)S(1)}, f32[2,32,128]{2,1,0:T(8,128)S(1)}, u32[]{:S(2)}, u32[]{:S(2)}) collective-permute-start(f32[2,32,128]{2,1,0:T(8,128)S(1)} %get-tuple-element.142), channel_id=1, source_target_pairs={{0,2},{1,3},{2,4},{3,5},{4,6},{5,7},{6,0},{7,1},{8,10},{9,11},{10,... | collective-permute-start | bytes 98312 | tf_op jit(solution)/shard_map/ppermute | solution.py:24
  77.2 6.6 %collective-permute-start.18 = (f32[2,32,128]{2,1,0:T(8,128)S(1)}, f32[2,32,128]{2,1,0:T(8,128)S(1)}, u32[]{:S(2)}, u32[]{:S(2)}) collective-permute-start(f32[2,32,128]{2,1,0:T(8,128)S(1)} %get-tuple-element.142), channel_id=1, source_target_pairs={{0,4},{1,5},{2,6},{3,7},{4,0},{5,1},{6,2},{7,3},{8,12},{9,13},{10,... | collective-permute-start | bytes 98312 | tf_op jit(solution)/shard_map/ppermute | solution.py:24
  92.6 5.7 %collective-permute-start.21 = (f32[2,32,128]{2,1,0:T(8,128)S(1)}, f32[2,32,128]{2,1,0:T(8,128)S(1)}, u32[]{:S(2)}, u32[]{:S(2)}) collective-permute-start(f32[2,32,128]{2,1,0:T(8,128)S(1)} %get-tuple-element.140), channel_id=1, source_target_pairs={{0,2},{1,3},{2,4},{3,5},{4,6},{5,7},{6,0},{7,1},{8,10},{9,11},{10,... | collective-permute-start | bytes 98312 | tf_op jit(solution)/shard_map/ppermute | solution.py:24
  93.5 5.4 %collective-permute-start.22 = (f32[2,32,128]{2,1,0:T(8,128)S(1)}, f32[2,32,128]{2,1,0:T(8,128)S(1)}, u32[]{:S(2)}, u32[]{:S(2)}) collective-permute-start(f32[2,32,128]{2,1,0:T(8,128)S(1)} %get-tuple-element.140), channel_id=1, source_target_pairs={{0,4},{1,5},{2,6},{3,7},{4,0},{5,1},{6,2},{7,3},{8,12},{9,13},{10,... | collective-permute-start | bytes 98312 | tf_op jit(solution)/shard_map/ppermute | solution.py:24
  108.1 5.7 %collective-permute-start.25 = (f32[2,32,128]{2,1,0:T(8,128)S(1)}, f32[2,32,128]{2,1,0:T(8,128)S(1)}, u32[]{:S(2)}, u32[]{:S(2)}) collective-permute-start(f32[2,32,128]{2,1,0:T(8,128)S(1)} %get-tuple-element.138), channel_id=1, source_target_pairs={{0,2},{1,3},{2,4},{3,5},{4,6},{5,7},{6,0},{7,1},{8,10},{9,11},{10,... | collective-permute-start | bytes 98312 | tf_op jit(solution)/shard_map/ppermute | solution.py:24
  109.4 5.0 collective-permute-start.26
  123.7 5.7 %collective-permute-start.29 = (f32[2,32,128]{2,1,0:T(8,128)S(1)}, f32[2,32,128]{2,1,0:T(8,128)S(1)}, u32[]{:S(2)}, u32[]{:S(2)}) collective-permute-start(f32[2,32,128]{2,1,0:T(8,128)S(1)} %get-tuple-element.136), channel_id=1, source_target_pairs={{0,2},{1,3},{2,4},{3,5},{4,6},{5,7},{6,0},{7,1},{8,10},{9,11},{10,... | collective-permute-start | bytes 98312 | tf_op jit(solution)/shard_map/ppermute | solution.py:24
  125.0 5.2 collective-permute-start.30
  139.8 5.7 %collective-permute-start.33 = (f32[2,32,128]{2,1,0:T(8,128)S(1)}, f32[2,32,128]{2,1,0:T(8,128)S(1)}, u32[]{:S(2)}, u32[]{:S(2)}) collective-permute-start(f32[2,32,128]{2,1,0:T(8,128)S(1)} %get-tuple-element.134), channel_id=1, source_target_pairs={{0,2},{1,3},{2,4},{3,5},{4,6},{5,7},{6,0},{7,1},{8,10},{9,11},{10,... | collective-permute-start | bytes 98312 | tf_op jit(solution)/shard_map/ppermute | solution.py:24
  141.1 5.2 collective-permute-start.34
  158.1 5.9 %collective-permute-start.39 = (f32[2,32,128]{2,1,0:T(8,128)S(1)}, f32[2,32,128]{2,1,0:T(8,128)S(1)}, u32[]{:S(2)}, u32[]{:S(2)}) collective-permute-start(f32[2,32,128]{2,1,0:T(8,128)S(1)} %get-tuple-element.132), channel_id=1, source_target_pairs={{0,2},{1,3},{2,4},{3,5},{4,6},{5,7},{6,0},{7,1},{8,10},{9,11},{10,... | collective-permute-start | bytes 98312 | tf_op jit(solution)/shard_map/ppermute | solution.py:24
  159.2 5.7 %collective-permute-start.40 = (f32[2,32,128]{2,1,0:T(8,128)S(1)}, f32[2,32,128]{2,1,0:T(8,128)S(1)}, u32[]{:S(2)}, u32[]{:S(2)}) collective-permute-start(f32[2,32,128]{2,1,0:T(8,128)S(1)} %get-tuple-element.132), channel_id=1, source_target_pairs={{0,4},{1,5},{2,6},{3,7},{4,0},{5,1},{6,2},{7,3},{8,12},{9,13},{10,... | collective-permute-start | bytes 98312 | tf_op jit(solution)/shard_map/ppermute | solution.py:24
  173.5 5.7 %collective-permute-start.43 = (f32[2,32,128]{2,1,0:T(8,128)S(1)}, f32[2,32,128]{2,1,0:T(8,128)S(1)}, u32[]{:S(2)}, u32[]{:S(2)}) collective-permute-start(f32[2,32,128]{2,1,0:T(8,128)S(1)} %get-tuple-element.130), channel_id=1, source_target_pairs={{0,2},{1,3},{2,4},{3,5},{4,6},{5,7},{6,0},{7,1},{8,10},{9,11},{10,... | collective-permute-start | bytes 98312 | tf_op jit(solution)/shard_map/ppermute | solution.py:24
  174.8 5.1 collective-permute-start.44
  189.1 5.7 %collective-permute-start.47 = (f32[2,32,128]{2,1,0:T(8,128)S(1)}, f32[2,32,128]{2,1,0:T(8,128)S(1)}, u32[]{:S(2)}, u32[]{:S(2)}) collective-permute-start(f32[2,32,128]{2,1,0:T(8,128)S(1)} %get-tuple-element.128), channel_id=1, source_target_pairs={{0,2},{1,3},{2,4},{3,5},{4,6},{5,7},{6,0},{7,1},{8,10},{9,11},{10,... | collective-permute-start | bytes 98312 | tf_op jit(solution)/shard_map/ppermute | solution.py:24
  190.4 5.1 collective-permute-start.48
  204.7 5.7 %collective-permute-start.51 = (f32[2,32,128]{2,1,0:T(8,128)S(1)}, f32[2,32,128]{2,1,0:T(8,128)S(1)}, u32[]{:S(2)}, u32[]{:S(2)}) collective-permute-start(f32[2,32,128]{2,1,0:T(8,128)S(1)} %get-tuple-element.126), channel_id=1, source_target_pairs={{0,2},{1,3},{2,4},{3,5},{4,6},{5,7},{6,0},{7,1},{8,10},{9,11},{10,... | collective-permute-start | bytes 98312 | tf_op jit(solution)/shard_map/ppermute | solution.py:24
  205.9 5.2 collective-permute-start.52
  220.4 5.7 %collective-permute-start.55 = (f32[2,32,128]{2,1,0:T(8,128)S(1)}, f32[2,32,128]{2,1,0:T(8,128)S(1)}, u32[]{:S(2)}, u32[]{:S(2)}) collective-permute-start(f32[2,32,128]{2,1,0:T(8,128)S(1)} %get-tuple-element.124), channel_id=1, source_target_pairs={{0,2},{1,3},{2,4},{3,5},{4,6},{5,7},{6,0},{7,1},{8,10},{9,11},{10,... | collective-permute-start | bytes 98312 | tf_op jit(solution)/shard_map/ppermute | solution.py:24
  221.5 5.3 collective-permute-start.56
  236.0 6.1 %collective-permute-start.59 = (f32[2,32,128]{2,1,0:T(8,128)S(1)}, f32[2,32,128]{2,1,0:T(8,128)S(1)}, u32[]{:S(2)}, u32[]{:S(2)}) collective-permute-start(f32[2,32,128]{2,1,0:T(8,128)S(1)} %get-tuple-element.122), channel_id=1, source_target_pairs={{0,2},{1,3},{2,4},{3,5},{4,6},{5,7},{6,0},{7,1},{8,10},{9,11},{10,... | collective-permute-start | bytes 98312 | tf_op jit(solution)/shard_map/ppermute | solution.py:24
  238.2 5.2 collective-permute-start.60
  252.0 5.7 %collective-permute-start.63 = (f32[2,32,128]{2,1,0:T(8,128)S(1)}, f32[2,32,128]{2,1,0:T(8,128)S(1)}, u32[]{:S(2)}, u32[]{:S(2)}) collective-permute-start(f32[2,32,128]{2,1,0:T(8,128)S(1)} %get-tuple-element.120), channel_id=1, source_target_pairs={{0,2},{1,3},{2,4},{3,5},{4,6},{5,7},{6,0},{7,1},{8,10},{9,11},{10,... | collective-permute-start | bytes 98312 | tf_op jit(solution)/shard_map/ppermute | solution.py:24
  253.0 5.1 collective-permute-start.64
  268.1 5.8 %collective-permute-start.67 = (f32[2,32,128]{2,1,0:T(8,128)S(1)}, f32[2,32,128]{2,1,0:T(8,128)S(1)}, u32[]{:S(2)}, u32[]{:S(2)}) collective-permute-start(f32[2,32,128]{2,1,0:T(8,128)S(1)} %get-tuple-element.118), channel_id=1, source_target_pairs={{0,2},{1,3},{2,4},{3,5},{4,6},{5,7},{6,0},{7,1},{8,10},{9,11},{10,... | collective-permute-start | bytes 98312 | tf_op jit(solution)/shard_map/ppermute | solution.py:24
  268.9 5.5 %collective-permute-start.68 = (f32[2,32,128]{2,1,0:T(8,128)S(1)}, f32[2,32,128]{2,1,0:T(8,128)S(1)}, u32[]{:S(2)}, u32[]{:S(2)}) collective-permute-start(f32[2,32,128]{2,1,0:T(8,128)S(1)} %get-tuple-element.118), channel_id=1, source_target_pairs={{0,4},{1,5},{2,6},{3,7},{4,0},{5,1},{6,2},{7,3},{8,12},{9,13},{10,... | collective-permute-start | bytes 98312 | tf_op jit(solution)/shard_map/ppermute | solution.py:24
  276.8 5.6 %collective-permute-start.71 = (f32[1,64]{1,0:T(1,128)S(1)}, f32[1,64]{1,0:T(1,128)S(1)}, u32[]{:S(2)}, u32[]{:S(2)}) collective-permute-start(f32[1,64]{1,0:T(1,128)S(1)} %fusion.51), channel_id=1, source_target_pairs={{0,8},{8,16},{16,24},{24,0},{1,9},{9,17},{17,25},{25,1},{2,10},{10... | collective-permute-start | bytes 776 | tf_op jit(solution)/shard_map/ppermute | solution.py:13
  276.9 5.5 %collective-permute-start.70 = (f32[1,2,64]{2,1,0:T(2,128)S(1)}, f32[1,2,64]{2,1,0:T(2,128)S(1)}, u32[]{:S(2)}, u32[]{:S(2)}) collective-permute-start(f32[1,2,64]{2,1,0:T(2,128)S(1)} %pad_maximum_fusion.97), channel_id=1, source_target_pairs={{0,24},{8,0},{16,8},{24,16},{1,25},{9,1},{17,9},{25,17},{2,26},{10... | collective-permute-start | bytes 1544 | tf_op jit(solution)/shard_map/ppermute | solution.py:13
  287.7 5.7 %collective-permute-start.73 = (f32[2,32,128]{2,1,0:T(8,128)S(1)}, f32[2,32,128]{2,1,0:T(8,128)S(1)}, u32[]{:S(2)}, u32[]{:S(2)}) collective-permute-start(f32[2,32,128]{2,1,0:T(8,128)S(1)} %get-tuple-element.116), channel_id=1, source_target_pairs={{0,2},{1,3},{2,4},{3,5},{4,6},{5,7},{6,0},{7,1},{8,10},{9,11},{10,... | collective-permute-start | bytes 98312 | tf_op jit(solution)/shard_map/ppermute | solution.py:24
  288.6 5.4 %collective-permute-start.74 = (f32[2,32,128]{2,1,0:T(8,128)S(1)}, f32[2,32,128]{2,1,0:T(8,128)S(1)}, u32[]{:S(2)}, u32[]{:S(2)}) collective-permute-start(f32[2,32,128]{2,1,0:T(8,128)S(1)} %get-tuple-element.116), channel_id=1, source_target_pairs={{0,4},{1,5},{2,6},{3,7},{4,0},{5,1},{6,2},{7,3},{8,12},{9,13},{10,... | collective-permute-start | bytes 98312 | tf_op jit(solution)/shard_map/ppermute | solution.py:24
  302.9 5.7 %collective-permute-start.77 = (f32[2,32,128]{2,1,0:T(8,128)S(1)}, f32[2,32,128]{2,1,0:T(8,128)S(1)}, u32[]{:S(2)}, u32[]{:S(2)}) collective-permute-start(f32[2,32,128]{2,1,0:T(8,128)S(1)} %get-tuple-element.114), channel_id=1, source_target_pairs={{0,2},{1,3},{2,4},{3,5},{4,6},{5,7},{6,0},{7,1},{8,10},{9,11},{10,... | collective-permute-start | bytes 98312 | tf_op jit(solution)/shard_map/ppermute | solution.py:24
  318.7 5.7 %collective-permute-start.81 = (f32[2,32,128]{2,1,0:T(8,128)S(1)}, f32[2,32,128]{2,1,0:T(8,128)S(1)}, u32[]{:S(2)}, u32[]{:S(2)}) collective-permute-start(f32[2,32,128]{2,1,0:T(8,128)S(1)} %get-tuple-element.112), channel_id=1, source_target_pairs={{0,2},{1,3},{2,4},{3,5},{4,6},{5,7},{6,0},{7,1},{8,10},{9,11},{10,... | collective-permute-start | bytes 98312 | tf_op jit(solution)/shard_map/ppermute | solution.py:24
  319.7 5.4 collective-permute-start.82
  334.1 5.7 %collective-permute-start.85 = (f32[2,32,128]{2,1,0:T(8,128)S(1)}, f32[2,32,128]{2,1,0:T(8,128)S(1)}, u32[]{:S(2)}, u32[]{:S(2)}) collective-permute-start(f32[2,32,128]{2,1,0:T(8,128)S(1)} %get-tuple-element.110), channel_id=1, source_target_pairs={{0,2},{1,3},{2,4},{3,5},{4,6},{5,7},{6,0},{7,1},{8,10},{9,11},{10,... | collective-permute-start | bytes 98312 | tf_op jit(solution)/shard_map/ppermute | solution.py:24
  350.0 5.9 %collective-permute-start.89 = (f32[2,32,128]{2,1,0:T(8,128)S(1)}, f32[2,32,128]{2,1,0:T(8,128)S(1)}, u32[]{:S(2)}, u32[]{:S(2)}) collective-permute-start(f32[2,32,128]{2,1,0:T(8,128)S(1)} %get-tuple-element.108), channel_id=1, source_target_pairs={{0,2},{1,3},{2,4},{3,5},{4,6},{5,7},{6,0},{7,1},{8,10},{9,11},{10,... | collective-permute-start | bytes 98312 | tf_op jit(solution)/shard_map/ppermute | solution.py:24
  351.0 6.6 %collective-permute-start.90 = (f32[2,32,128]{2,1,0:T(8,128)S(1)}, f32[2,32,128]{2,1,0:T(8,128)S(1)}, u32[]{:S(2)}, u32[]{:S(2)}) collective-permute-start(f32[2,32,128]{2,1,0:T(8,128)S(1)} %get-tuple-element.108), channel_id=1, source_target_pairs={{0,4},{1,5},{2,6},{3,7},{4,0},{5,1},{6,2},{7,3},{8,12},{9,13},{10,... | collective-permute-start | bytes 98312 | tf_op jit(solution)/shard_map/ppermute | solution.py:24
  366.2 5.7 %collective-permute-start.93 = (f32[2,32,128]{2,1,0:T(8,128)S(1)}, f32[2,32,128]{2,1,0:T(8,128)S(1)}, u32[]{:S(2)}, u32[]{:S(2)}) collective-permute-start(f32[2,32,128]{2,1,0:T(8,128)S(1)} %get-tuple-element.106), channel_id=1, source_target_pairs={{0,2},{1,3},{2,4},{3,5},{4,6},{5,7},{6,0},{7,1},{8,10},{9,11},{10,... | collective-permute-start | bytes 98312 | tf_op jit(solution)/shard_map/ppermute | solution.py:24
  367.2 5.3 collective-permute-start.94
  382.0 5.7 %collective-permute-start.97 = (f32[2,32,128]{2,1,0:T(8,128)S(1)}, f32[2,32,128]{2,1,0:T(8,128)S(1)}, u32[]{:S(2)}, u32[]{:S(2)}) collective-permute-start(f32[2,32,128]{2,1,0:T(8,128)S(1)} %get-tuple-element.104), channel_id=1, source_target_pairs={{0,2},{1,3},{2,4},{3,5},{4,6},{5,7},{6,0},{7,1},{8,10},{9,11},{10,... | collective-permute-start | bytes 98312 | tf_op jit(solution)/shard_map/ppermute | solution.py:24
  383.0 5.4 %collective-permute-start.98 = (f32[2,32,128]{2,1,0:T(8,128)S(1)}, f32[2,32,128]{2,1,0:T(8,128)S(1)}, u32[]{:S(2)}, u32[]{:S(2)}) collective-permute-start(f32[2,32,128]{2,1,0:T(8,128)S(1)} %get-tuple-element.104), channel_id=1, source_target_pairs={{0,4},{1,5},{2,6},{3,7},{4,0},{5,1},{6,2},{7,3},{8,12},{9,13},{10,... | collective-permute-start | bytes 98312 | tf_op jit(solution)/shard_map/ppermute | solution.py:24
  397.3 5.7 %collective-permute-start.101 = (f32[2,32,128]{2,1,0:T(8,128)S(1)}, f32[2,32,128]{2,1,0:T(8,128)S(1)}, u32[]{:S(2)}, u32[]{:S(2)}) collective-permute-start(f32[2,32,128]{2,1,0:T(8,128)S(1)} %get-tuple-element.102), channel_id=1, source_target_pairs={{0,2},{1,3},{2,4},{3,5},{4,6},{5,7},{6,0},{7,1},{8,10},{9,11},{10,... | collective-permute-start | bytes 98312 | tf_op jit(solution)/shard_map/ppermute | solution.py:24
  406.0 5.6 %collective-permute-start.105 = (f32[1,64]{1,0:T(1,128)S(1)}, f32[1,64]{1,0:T(1,128)S(1)}, u32[]{:S(2)}, u32[]{:S(2)}) collective-permute-start(f32[1,64]{1,0:T(1,128)S(1)} %fusion.50), channel_id=1, source_target_pairs={{0,8},{8,16},{16,24},{24,0},{1,9},{9,17},{17,25},{25,1},{2,10},{10... | collective-permute-start | bytes 776 | tf_op jit(solution)/shard_map/ppermute | solution.py:13
  406.1 5.5 %collective-permute-start.104 = (f32[1,2,64]{2,1,0:T(2,128)S(1)}, f32[1,2,64]{2,1,0:T(2,128)S(1)}, u32[]{:S(2)}, u32[]{:S(2)}) collective-permute-start(f32[1,2,64]{2,1,0:T(2,128)S(1)} %pad_maximum_fusion.98), channel_id=1, source_target_pairs={{0,24},{8,0},{16,8},{24,16},{1,25},{9,1},{17,9},{25,17},{2,26},{10... | collective-permute-start | bytes 1544 | tf_op jit(solution)/shard_map/ppermute | solution.py:13
  416.8 5.7 %collective-permute-start.107 = (f32[2,32,128]{2,1,0:T(8,128)S(1)}, f32[2,32,128]{2,1,0:T(8,128)S(1)}, u32[]{:S(2)}, u32[]{:S(2)}) collective-permute-start(f32[2,32,128]{2,1,0:T(8,128)S(1)} %get-tuple-element.100), channel_id=1, source_target_pairs={{0,2},{1,3},{2,4},{3,5},{4,6},{5,7},{6,0},{7,1},{8,10},{9,11},{10,... | collective-permute-start | bytes 98312 | tf_op jit(solution)/shard_map/ppermute | solution.py:24
  417.9 5.4 collective-permute-start.108
  432.2 5.7 %collective-permute-start.111 = (f32[2,32,128]{2,1,0:T(8,128)S(1)}, f32[2,32,128]{2,1,0:T(8,128)S(1)}, u32[]{:S(2)}, u32[]{:S(2)}) collective-permute-start(f32[2,32,128]{2,1,0:T(8,128)S(1)} %get-tuple-element.98), channel_id=1, source_target_pairs={{0,2},{1,3},{2,4},{3,5},{4,6},{5,7},{6,0},{7,1},{8,10},{9,11},{10,... | collective-permute-start | bytes 98312 | tf_op jit(solution)/shard_map/ppermute | solution.py:24
  433.5 5.1 collective-permute-start.112
  447.9 5.7 %collective-permute-start.115 = (f32[2,32,128]{2,1,0:T(8,128)S(1)}, f32[2,32,128]{2,1,0:T(8,128)S(1)}, u32[]{:S(2)}, u32[]{:S(2)}) collective-permute-start(f32[2,32,128]{2,1,0:T(8,128)S(1)} %get-tuple-element.96), channel_id=1, source_target_pairs={{0,2},{1,3},{2,4},{3,5},{4,6},{5,7},{6,0},{7,1},{8,10},{9,11},{10,... | collective-permute-start | bytes 98312 | tf_op jit(solution)/shard_map/ppermute | solution.py:24
  448.9 5.4 %collective-permute-start.116 = (f32[2,32,128]{2,1,0:T(8,128)S(1)}, f32[2,32,128]{2,1,0:T(8,128)S(1)}, u32[]{:S(2)}, u32[]{:S(2)}) collective-permute-start(f32[2,32,128]{2,1,0:T(8,128)S(1)} %get-tuple-element.96), channel_id=1, source_target_pairs={{0,4},{1,5},{2,6},{3,7},{4,0},{5,1},{6,2},{7,3},{8,12},{9,13},{10,... | collective-permute-start | bytes 98312 | tf_op jit(solution)/shard_map/ppermute | solution.py:24
  463.2 5.7 %collective-permute-start.119 = (f32[2,32,128]{2,1,0:T(8,128)S(1)}, f32[2,32,128]{2,1,0:T(8,128)S(1)}, u32[]{:S(2)}, u32[]{:S(2)}) collective-permute-start(f32[2,32,128]{2,1,0:T(8,128)S(1)} %get-tuple-element.94), channel_id=1, source_target_pairs={{0,2},{1,3},{2,4},{3,5},{4,6},{5,7},{6,0},{7,1},{8,10},{9,11},{10,... | collective-permute-start | bytes 98312 | tf_op jit(solution)/shard_map/ppermute | solution.py:24
  479.0 6.2 %collective-permute-start.123 = (f32[2,32,128]{2,1,0:T(8,128)S(1)}, f32[2,32,128]{2,1,0:T(8,128)S(1)}, u32[]{:S(2)}, u32[]{:S(2)}) collective-permute-start(f32[2,32,128]{2,1,0:T(8,128)S(1)} %get-tuple-element.92), channel_id=1, source_target_pairs={{0,2},{1,3},{2,4},{3,5},{4,6},{5,7},{6,0},{7,1},{8,10},{9,11},{10,... | collective-permute-start | bytes 98312 | tf_op jit(solution)/shard_map/ppermute | solution.py:24
  480.1 6.4 %collective-permute-start.124 = (f32[2,32,128]{2,1,0:T(8,128)S(1)}, f32[2,32,128]{2,1,0:T(8,128)S(1)}, u32[]{:S(2)}, u32[]{:S(2)}) collective-permute-start(f32[2,32,128]{2,1,0:T(8,128)S(1)} %get-tuple-element.92), channel_id=1, source_target_pairs={{0,4},{1,5},{2,6},{3,7},{4,0},{5,1},{6,2},{7,3},{8,12},{9,13},{10,... | collective-permute-start | bytes 98312 | tf_op jit(solution)/shard_map/ppermute | solution.py:24
  495.0 5.7 %collective-permute-start.127 = (f32[2,32,128]{2,1,0:T(8,128)S(1)}, f32[2,32,128]{2,1,0:T(8,128)S(1)}, u32[]{:S(2)}, u32[]{:S(2)}) collective-permute-start(f32[2,32,128]{2,1,0:T(8,128)S(1)} %get-tuple-element.90), channel_id=1, source_target_pairs={{0,2},{1,3},{2,4},{3,5},{4,6},{5,7},{6,0},{7,1},{8,10},{9,11},{10,... | collective-permute-start | bytes 98312 | tf_op jit(solution)/shard_map/ppermute | solution.py:24
  495.9 5.5 %collective-permute-start.128 = (f32[2,32,128]{2,1,0:T(8,128)S(1)}, f32[2,32,128]{2,1,0:T(8,128)S(1)}, u32[]{:S(2)}, u32[]{:S(2)}) collective-permute-start(f32[2,32,128]{2,1,0:T(8,128)S(1)} %get-tuple-element.90), channel_id=1, source_target_pairs={{0,4},{1,5},{2,6},{3,7},{4,0},{5,1},{6,2},{7,3},{8,12},{9,13},{10,... | collective-permute-start | bytes 98312 | tf_op jit(solution)/shard_map/ppermute | solution.py:24
  510.4 5.7 %collective-permute-start.131 = (f32[2,32,128]{2,1,0:T(8,128)S(1)}, f32[2,32,128]{2,1,0:T(8,128)S(1)}, u32[]{:S(2)}, u32[]{:S(2)}) collective-permute-start(f32[2,32,128]{2,1,0:T(8,128)S(1)} %get-tuple-element.88), channel_id=1, source_target_pairs={{0,2},{1,3},{2,4},{3,5},{4,6},{5,7},{6,0},{7,1},{8,10},{9,11},{10,... | collective-permute-start | bytes 98312 | tf_op jit(solution)/shard_map/ppermute | solution.py:24
  511.7 5.1 collective-permute-start.132
  (82 other events, 500.0 us)
